TPU v7x, 256 devices: a whole 4x4x8 slice. The times are simulated.
256 devices in a mesh: dp: 8 (over y, core), mp: 32 (over z, x).
Axes of the slice: x: 4, y: 4, z: 8, core: 2. Of those that a mesh axis runs over, the one named last changes fastest.
Arguments:
- table: bfloat16 [32, 2048, 128], P('mp'), may hold values from -6 to 6
- ids: int32 [65536, 32, 2], P('dp', 'mp'), may hold values from 0 to 2047
- counts: int32 [256, 8], P(('dp', 'mp')), may hold values from 1 to 96, 256 in all within a row
- labels: int32 [65536], P(('dp', 'mp')), may hold values from 0 to 4
- request_home: int32 [2048], replicated, may hold values from 0 to 2047, each once
- user_codes: bfloat16 [2048, 1024], P('dp'), may hold values from -6 to 6
- cross_down: bfloat16 [4096, 256], replicated, may hold values from -0.09375 to 0.09375
- cross_up: bfloat16 [256, 4096], replicated, may hold values from -0.375 to 0.375
- cross_bias: float32 [4096], replicated, may hold values from -4 to 4
- tower_weight: bfloat16 [4096, 1024], P('mp'), may hold values from -0.09375 to 0.09375
- tower_bias: float32 [1024], replicated, may hold values from -3 to 3
Outputs:
- scores: float32 [65536], P(('dp', 'mp'))
- pooled_grad: bfloat16 [65536, 32, 128], P('dp', 'mp')
Inputs may be any that keep to these rules, and one draw needn't show every extreme that they name: `counts`: each row sums to 256; its largest entry is exactly 96. `request_home`: a permutation of the request slots.
All inputs are finite; a program needn't handle non-finite values.
Results may differ from a plain program's by a relative error of at most 0.0097.
Values may be sent and summed in bfloat16 or wider, within the bound.
No kernel may reach another device: no remote copies, remote signals or barrier semaphores. Data moves between devices by JAX's collectives and lax.ppermute only.
A program may use at most 128 MiB of HBM per device.

v0:
```python
import math

import jax
import jax.numpy as jnp
from jax import lax
from jax.sharding import PartitionSpec as P


def pool_rows(table, ids):
    count_rows = ids.shape[0]
    hots = ids.shape[2]
    slab_rows = table.shape[1]
    block = math.gcd(count_rows, 512)
    lanes = jnp.arange(slab_rows, dtype=jnp.int32)
    slab = table[0]
    blocked = ids[:, 0, :].reshape(count_rows // block, block, hots)

    def one_block(idx_block):
        tally = jnp.zeros((block, slab_rows), jnp.float32)
        for which in range(hots):
            tally = tally + (idx_block[:, which][:, None] == lanes[None, :]).astype(jnp.float32)
        onehot = tally.astype(jnp.bfloat16)
        return jnp.dot(onehot, slab, preferred_element_type=jnp.float32).astype(jnp.bfloat16)

    summed = lax.map(one_block, blocked)
    results = [summed.reshape(count_rows, -1)]
    return jnp.stack(results, axis=1)


def members(counts_row, rows):
    ends = jnp.cumsum(counts_row)
    starts = ends - counts_row
    place = jnp.arange(rows, dtype=jnp.int32)[:, None]
    return (place >= starts[None, :]) & (place < ends[None, :])


def dot_last(left, right):
    return lax.dot_general(
        left, right, (((1,), (1,)), ((), ())), preferred_element_type=jnp.float32
    )


def pair_grad(scores, member, labels):
    gain = jnp.exp2(labels.astype(jnp.float32))
    member_f = member.astype(jnp.float32)
    same = jnp.dot(member_f, member_f.T) > 0.5
    diff = gain[:, None] - gain[None, :]
    gap = scores[None, :] - scores[:, None]
    turn = jnp.where(diff > 0, jax.nn.sigmoid(gap), jax.nn.sigmoid(-gap))
    total = jnp.sum(jnp.where(same, diff * turn, 0.0), axis=1)
    seg_gain = jnp.sum(jnp.where(member, (gain - 1.0)[:, None], 0.0), axis=0)
    norm = jnp.sum(jnp.where(member, seg_gain[None, :], 0.0), axis=1)
    return -total / jnp.maximum(norm, 1.0)


def local(
    table,
    ids,
    counts,
    labels,
    request_home,
    user_codes,
    cross_down,
    cross_up,
    cross_bias,
    tower_weight,
    tower_bias,
):
    parts = lax.axis_size("mp")
    rows = labels.shape[0]
    seg_count = counts.shape[1]
    width = user_codes.shape[1]
    scale = 1.0 / jnp.sqrt(jnp.float32(width))
    pooled = pool_rows(table, ids)
    moved = lax.all_to_all(pooled, "mp", split_axis=0, concat_axis=1, tiled=True)
    x0 = moved.reshape(rows, -1)
    member = members(counts[0], rows)
    every = lax.all_gather(user_codes, "dp", axis=0, tiled=True)
    slot_base = (lax.axis_index("dp") * parts + lax.axis_index("mp")) * seg_count
    wanted = slot_base + jnp.arange(seg_count, dtype=jnp.int32)
    pick = (request_home[None, :] == wanted[:, None]).astype(jnp.bfloat16)
    user_seg = jnp.dot(pick, every, preferred_element_type=jnp.float32).astype(jnp.bfloat16)
    z = jnp.dot(x0, cross_down, preferred_element_type=jnp.float32).astype(jnp.bfloat16)
    cross = jnp.dot(z, cross_up, preferred_element_type=jnp.float32) + cross_bias
    x1 = (x0 * cross + x0).astype(jnp.bfloat16)
    act = jnp.dot(
        x1,
        lax.all_gather(tower_weight, "mp", axis=0, tiled=True),
        preferred_element_type=jnp.float32,
    )
    act = act + tower_bias
    sig = jax.nn.sigmoid(act)
    hidden = (act * sig).astype(jnp.bfloat16)
    pair = dot_last(hidden, user_seg)
    score = jnp.sum(jnp.where(member, pair, 0.0), axis=1) * scale
    dscore = pair_grad(score, member, labels)
    code = jnp.dot(member.astype(jnp.bfloat16), user_seg, preferred_element_type=jnp.float32)
    slope = sig * (1.0 + act * (1.0 - sig))
    dact = (dscore[:, None] * code * scale * slope).astype(jnp.bfloat16)
    dx1 = dot_last(dact, lax.all_gather(tower_weight, "mp", axis=0, tiled=True))
    dcross = (dx1 * x0).astype(jnp.bfloat16)
    dz = dot_last(dcross, cross_up).astype(jnp.bfloat16)
    dx0 = dx1 * (1.0 + cross) + dot_last(dz, cross_down)
    grads = dx0.astype(jnp.bfloat16).reshape(moved.shape)
    returned = lax.all_to_all(grads, "mp", split_axis=1, concat_axis=0, tiled=True)
    return (score, returned)


def solution(mesh):
    in_specs = (
        P("mp", None, None),
        P("dp", "mp", None),
        P(("dp", "mp"), None),
        P(("dp", "mp")),
        P(),
        P("dp", None),
        P(),
        P(),
        P(),
        P("mp", None),
        P(),
    )
    out_specs = (P(("dp", "mp")), P("dp", "mp", None))
    return jax.shard_map(local, mesh=mesh, in_specs=in_specs, out_specs=out_specs, check_vma=False)
```

profile of v0, /device:TPU:2, one launch (start us, length us, event | category | flops | bytes accessed | tf_op | source)
XLA Modules:
  0.0 269.7 jit_solution(14666902381530985292)
XLA Ops:
  8.7 56.7 %while.12 = (s32[]{:T(128)}, bf16[16,512,128]{2,1,0:T(8,128)(2,1)}, s32[16,512,2]{1,2,0:T(2,128)}, bf16[2048,128]{1,0:T(8,128)(2,1)}, s32[]{:T(128)}) while((s32[]{:T(128)}, bf16[16,512,128]{2,1,0:T(8,128)(2,1)}, s32[16,512,2]{1,2,0:T(2,128)}, bf16[2048,128]{1,0:T(8,128)(2,1)}, s32[]{:T(128)}) %tuple.42), condition=%wide.region_2.3_spmd.clone.clone, body=%wide.region_1.2_spmd.clone.clone.sunk | while | flops 274792448 | bytes 675917 | solution.py:25
  9.4 2.8 %fusion.83 = bf16[16,512,128]{2,1,0:T(8,128)(2,1)} fusion(bf16[16,512,128]{2,1,0:T(8,128)(2,1)} %get-tuple-element.104, s32[]{:T(128)S(6)} %copy.52, bf16[2048,128]{1,0:T(8,128)(2,1)} %get-tuple-element.111, s32[512]{0:T(512)S(1)} %bitcast.84, s32[512]{0:T(512)S(1)} %bitcast.83), kind=kOutput, calls=%fused_computation.9.clone.1 | convolution fusion | flops 274792448 | bytes 659460 | tf_op jit(solution)/shard_map/while/body/eval_jaxpr/dot_general | solution.py:23
  12.9 2.8 %fusion.83 = bf16[16,512,128]{2,1,0:T(8,128)(2,1)} fusion(bf16[16,512,128]{2,1,0:T(8,128)(2,1)} %get-tuple-element.104, s32[]{:T(128)S(6)} %copy.52, bf16[2048,128]{1,0:T(8,128)(2,1)} %get-tuple-element.111, s32[512]{0:T(512)S(1)} %bitcast.84, s32[512]{0:T(512)S(1)} %bitcast.83), kind=kOutput, calls=%fused_computation.9.clone.1 | convolution fusion | flops 274792448 | bytes 659460 | tf_op jit(solution)/shard_map/while/body/eval_jaxpr/dot_general | solution.py:23
  16.5 2.8 %fusion.83 = bf16[16,512,128]{2,1,0:T(8,128)(2,1)} fusion(bf16[16,512,128]{2,1,0:T(8,128)(2,1)} %get-tuple-element.104, s32[]{:T(128)S(6)} %copy.52, bf16[2048,128]{1,0:T(8,128)(2,1)} %get-tuple-element.111, s32[512]{0:T(512)S(1)} %bitcast.84, s32[512]{0:T(512)S(1)} %bitcast.83), kind=kOutput, calls=%fused_computation.9.clone.1 | convolution fusion | flops 274792448 | bytes 659460 | tf_op jit(solution)/shard_map/while/body/eval_jaxpr/dot_general | solution.py:23
  20.0 2.8 %fusion.83 = bf16[16,512,128]{2,1,0:T(8,128)(2,1)} fusion(bf16[16,512,128]{2,1,0:T(8,128)(2,1)} %get-tuple-element.104, s32[]{:T(128)S(6)} %copy.52, bf16[2048,128]{1,0:T(8,128)(2,1)} %get-tuple-element.111, s32[512]{0:T(512)S(1)} %bitcast.84, s32[512]{0:T(512)S(1)} %bitcast.83), kind=kOutput, calls=%fused_computation.9.clone.1 | convolution fusion | flops 274792448 | bytes 659460 | tf_op jit(solution)/shard_map/while/body/eval_jaxpr/dot_general | solution.py:23
  23.5 2.9 %fusion.83 = bf16[16,512,128]{2,1,0:T(8,128)(2,1)} fusion(bf16[16,512,128]{2,1,0:T(8,128)(2,1)} %get-tuple-element.104, s32[]{:T(128)S(6)} %copy.52, bf16[2048,128]{1,0:T(8,128)(2,1)} %get-tuple-element.111, s32[512]{0:T(512)S(1)} %bitcast.84, s32[512]{0:T(512)S(1)} %bitcast.83), kind=kOutput, calls=%fused_computation.9.clone.1 | convolution fusion | flops 274792448 | bytes 659460 | tf_op jit(solution)/shard_map/while/body/eval_jaxpr/dot_general | solution.py:23
  27.1 2.8 %fusion.83 = bf16[16,512,128]{2,1,0:T(8,128)(2,1)} fusion(bf16[16,512,128]{2,1,0:T(8,128)(2,1)} %get-tuple-element.104, s32[]{:T(128)S(6)} %copy.52, bf16[2048,128]{1,0:T(8,128)(2,1)} %get-tuple-element.111, s32[512]{0:T(512)S(1)} %bitcast.84, s32[512]{0:T(512)S(1)} %bitcast.83), kind=kOutput, calls=%fused_computation.9.clone.1 | convolution fusion | flops 274792448 | bytes 659460 | tf_op jit(solution)/shard_map/while/body/eval_jaxpr/dot_general | solution.py:23
  30.6 2.8 %fusion.83 = bf16[16,512,128]{2,1,0:T(8,128)(2,1)} fusion(bf16[16,512,128]{2,1,0:T(8,128)(2,1)} %get-tuple-element.104, s32[]{:T(128)S(6)} %copy.52, bf16[2048,128]{1,0:T(8,128)(2,1)} %get-tuple-element.111, s32[512]{0:T(512)S(1)} %bitcast.84, s32[512]{0:T(512)S(1)} %bitcast.83), kind=kOutput, calls=%fused_computation.9.clone.1 | convolution fusion | flops 274792448 | bytes 659460 | tf_op jit(solution)/shard_map/while/body/eval_jaxpr/dot_general | solution.py:23
  34.2 2.9 %fusion.83 = bf16[16,512,128]{2,1,0:T(8,128)(2,1)} fusion(bf16[16,512,128]{2,1,0:T(8,128)(2,1)} %get-tuple-element.104, s32[]{:T(128)S(6)} %copy.52, bf16[2048,128]{1,0:T(8,128)(2,1)} %get-tuple-element.111, s32[512]{0:T(512)S(1)} %bitcast.84, s32[512]{0:T(512)S(1)} %bitcast.83), kind=kOutput, calls=%fused_computation.9.clone.1 | convolution fusion | flops 274792448 | bytes 659460 | tf_op jit(solution)/shard_map/while/body/eval_jaxpr/dot_general | solution.py:23
  37.7 2.8 %fusion.83 = bf16[16,512,128]{2,1,0:T(8,128)(2,1)} fusion(bf16[16,512,128]{2,1,0:T(8,128)(2,1)} %get-tuple-element.104, s32[]{:T(128)S(6)} %copy.52, bf16[2048,128]{1,0:T(8,128)(2,1)} %get-tuple-element.111, s32[512]{0:T(512)S(1)} %bitcast.84, s32[512]{0:T(512)S(1)} %bitcast.83), kind=kOutput, calls=%fused_computation.9.clone.1 | convolution fusion | flops 274792448 | bytes 659460 | tf_op jit(solution)/shard_map/while/body/eval_jaxpr/dot_general | solution.py:23
  41.3 2.9 %fusion.83 = bf16[16,512,128]{2,1,0:T(8,128)(2,1)} fusion(bf16[16,512,128]{2,1,0:T(8,128)(2,1)} %get-tuple-element.104, s32[]{:T(128)S(6)} %copy.52, bf16[2048,128]{1,0:T(8,128)(2,1)} %get-tuple-element.111, s32[512]{0:T(512)S(1)} %bitcast.84, s32[512]{0:T(512)S(1)} %bitcast.83), kind=kOutput, calls=%fused_computation.9.clone.1 | convolution fusion | flops 274792448 | bytes 659460 | tf_op jit(solution)/shard_map/while/body/eval_jaxpr/dot_general | solution.py:23
  44.8 2.8 %fusion.83 = bf16[16,512,128]{2,1,0:T(8,128)(2,1)} fusion(bf16[16,512,128]{2,1,0:T(8,128)(2,1)} %get-tuple-element.104, s32[]{:T(128)S(6)} %copy.52, bf16[2048,128]{1,0:T(8,128)(2,1)} %get-tuple-element.111, s32[512]{0:T(512)S(1)} %bitcast.84, s32[512]{0:T(512)S(1)} %bitcast.83), kind=kOutput, calls=%fused_computation.9.clone.1 | convolution fusion | flops 274792448 | bytes 659460 | tf_op jit(solution)/shard_map/while/body/eval_jaxpr/dot_general | solution.py:23
  62.5 2.8 %fusion.83 = bf16[16,512,128]{2,1,0:T(8,128)(2,1)} fusion(bf16[16,512,128]{2,1,0:T(8,128)(2,1)} %get-tuple-element.104, s32[]{:T(128)S(6)} %copy.52, bf16[2048,128]{1,0:T(8,128)(2,1)} %get-tuple-element.111, s32[512]{0:T(512)S(1)} %bitcast.84, s32[512]{0:T(512)S(1)} %bitcast.83), kind=kOutput, calls=%fused_computation.9.clone.1 | convolution fusion | flops 274792448 | bytes 659460 | tf_op jit(solution)/shard_map/while/body/eval_jaxpr/dot_general | solution.py:23
  65.9 4.5 %reduce = bf16[8192,128]{1,0:T(8,128)(2,1)} reduce(bf16[8192,1,128]{2,0,1:T(8,128)(2,1)} %bitcast.82, bf16[]{:T(256)} %broadcast.49), dimensions={1}, to_apply=%copy.18.reduce_sub_computation | reduce | bytes 4194306 | tf_op jit(solution)/shard_map/stack;reshape | solution.py:27
  70.4 4.0 %reshape.50 = bf16[32,2,16384]{2,1,0:T(2,128)(2,1)} reshape(bf16[8192,128]{1,0:T(8,128)(2,1)} %reduce) | data formatting | bytes 4194304
  74.4 11.8 %all-to-all-start = ((bf16[32,2,16384]{2,1,0:T(2,128)(2,1)}), bf16[32,2,16384]{2,1,0:T(2,128)(2,1)}, u32[]{:S(2)}, u32[]{:S(2)}) async-start(bf16[32,2,16384]{2,1,0:T(2,128)(2,1)} %reshape.50), calls=%async_computation | async-start | bytes 4194304 | tf_op jit(solution)/shard_map/all_to_all | solution.py:75
  86.7 64.3 %all-to-all-done = bf16[32,2,16384]{2,1,0:T(2,128)(2,1)} async-done(((bf16[32,2,16384]{2,1,0:T(2,128)(2,1)}), bf16[32,2,16384]{2,1,0:T(2,128)(2,1)}, u32[]{:S(2)}, u32[]{:S(2)}) %all-to-all-start) | async-done | bytes 2097184 | tf_op jit(solution)/shard_map/all_to_all | solution.py:75
  150.9 10.5 %reshape.51 = bf16[8192,1,128]{2,1,0:T(2,128)(2,1)} reshape(bf16[32,2,16384]{2,1,0:T(2,128)(2,1)} %all-to-all-done) | data formatting | bytes 4194304
  166.7 6.6 %convolution_add_fusion.1 = f32[256,4096]{1,0:T(8,128)} fusion(bf16[256,4096]{1,0:T(8,128)(2,1)S(1)} %copy-done, f32[4096]{0:T(1024)S(1)} %copy-done.1, bf16[4096,256]{1,0:T(8,128)(2,1)} %param.19, bf16[32,8,32,128]{3,2,1,0:T(8,128)(2,1)} %bitcast.76), kind=kOutput, calls=%fused_computation.13 | convolution fusion | flops 1074855936 | bytes 10502144 | tf_op jit(solution)/shard_map/dot_general | solution.py:84
  173.3 2.9 %convolution_convert_fusion = bf16[8,1024]{1,0:T(8,128)(2,1)S(1)} fusion(bf16[2048,1024]{1,0:T(8,128)(2,1)} %all-gather.5.cloned.1.call-done, s32[2048]{0:T(1024)S(1)} %copy-done.2, s32[8]{0:T(128)S(1)} %iota_add_fusion), kind=kOutput, calls=%fused_computation.40 | convolution fusion | flops 33579008 | bytes 4218912 | tf_op jit(solution)/shard_map/dot_general | solution.py:82
  176.2 8.0 %fusion.25 = f32[256,1024]{1,0:T(8,128)S(1)} fusion(bf16[4096,1024]{1,0:T(8,128)(2,1)} %all-gather.3.cloned.1.call-done, f32[256,4096]{1,0:T(8,128)} %convolution_add_fusion.1, bf16[32,8,32,128]{3,2,1,0:T(8,128)(2,1)} %bitcast.77, f32[1024]{0:T(1024)S(1)} %copy-done.5), kind=kOutput, calls=%fused_computation.32 | convolution fusion | flops 2151940096 | bytes 15732736 | tf_op jit(solution)/shard_map/dot_general | solution.py:86
  185.0 8.2 %fusion.29 = f32[256,4096]{1,0:T(8,128)} fusion(bf16[4096,1024]{1,0:T(8,128)(2,1)} %all-gather.3.cloned.1.call-done, bf16[8,1024]{1,0:T(8,128)(2,1)S(1)} %convolution_convert_fusion, f32[256,1024]{1,0:T(8,128)S(1)} %fusion.25, f32[256]{0:T(256)S(1)} %maximum_divide_fusion, s32[8]{0:T(128)S(1)} %bitcast.90, s32[8]{0:T(128)S(1)} %fusion.60), kind=kOutput, calls=%fused_computation.34 | convolution fusion | flops 2154567680 | bytes 13648960 | tf_op jit(solution)/shard_map/dot_general | solution.py:38
  193.2 9.8 %fusion.19 = bf16[32,32,8,128]{3,2,1,0:T(8,128)(2,1)} fusion(bf16[4096,256]{1,0:T(8,128)(2,1)} %param.19, f32[256,4096]{1,0:T(8,128)} %fusion.29, f32[256,4096]{1,0:T(8,128)} %convolution_add_fusion.1, bf16[256,4096]{1,0:T(8,128)(2,1)S(1)} %copy-done, bf16[32,8,32,128]{3,2,1,0:T(8,128)(2,1)} %bitcast.78), kind=kOutput, calls=%fused_computation.25 | convolution fusion | flops 1081147392 | bytes 16777216 | tf_op jit(solution)/shard_map/dot_general | solution.py:38
  205.2 56.3 %all_to_all.33 = bf16[256,32,128]{2,0,1:T(8,128)(2,1)S(1)} all-to-all(bf16[256,32,128]{2,0,1:T(8,128)(2,1)S(1)} %bitcast.80), channel_id=1, replica_groups=mesh['dp'=8,'mp'=32] {'mp'}, dimensions={1} | all-to-all | bytes 4194304 | tf_op jit(solution)/shard_map/all_to_all | solution.py:105
  (72 shorter events, 34.4 us)
Async XLA Ops:
  7.2 159.5 %copy-start = (bf16[256,4096]{1,0:T(8,128)(2,1)S(1)}, bf16[256,4096]{1,0:T(8,128)(2,1)}, u32[]{:S(2)}) copy-start(bf16[256,4096]{1,0:T(8,128)(2,1)} %param.20) | copy-start | bytes 6291460
  7.2 166.1 %all-gather.5.cloned.1.call-start = ((), (), s32[]{:S(2)}) async-start(), calls=%async_computation.3 | async-start | bytes 4718592 | tf_op jit(solution)/shard_map/all_gather | solution.py:78
  7.9 168.3 %all-gather.3.cloned.1.call-start = ((), (), s32[]{:S(2)}) async-start(), calls=%async_computation.2 | async-start | bytes 8650752 | tf_op jit(solution)/shard_map/all_gather | solution.py:88
  74.4 11.8 %copy-start.6 = (s32[1,8]{1,0:T(1,128)S(1)}, s32[1,8]{1,0:T(1,128)}, u32[]{:S(2)}) copy-start(s32[1,8]{1,0:T(1,128)} %param.15) | copy-start | bytes 100
  74.4 12.0 %copy-start.3 = (s32[256]{0:T(256)S(1)}, s32[256]{0:T(256)}, u32[]{:S(2)}) copy-start(s32[256]{0:T(256)} %param.16) | copy-start | bytes 3076
  74.4 76.6 %all-to-all-start = ((bf16[32,2,16384]{2,1,0:T(2,128)(2,1)}), bf16[32,2,16384]{2,1,0:T(2,128)(2,1)}, u32[]{:S(2)}, u32[]{:S(2)}) async-start(bf16[32,2,16384]{2,1,0:T(2,128)(2,1)} %reshape.50), calls=%async_computation | async-start | bytes 4194304 | tf_op jit(solution)/shard_map/all_to_all | solution.py:75
  164.0 2.7 copy-start.1
  166.7 6.6 %copy-start.2 = (s32[2048]{0:T(1024)S(1)}, s32[2048]{0:T(1024)}, u32[]{:S(2)}) copy-start(s32[2048]{0:T(1024)} %param.17) | copy-start | bytes 24580
  173.3 2.9 %copy-start.5 = (f32[1024]{0:T(1024)S(1)}, f32[1024]{0:T(1024)}, u32[]{:S(2)}) copy-start(f32[1024]{0:T(1024)} %param.23) | copy-start | bytes 12292
  184.6 8.6 %copy-start.4 = (f32[256]{0:T(256)}, f32[256]{0:T(256)S(1)}, u32[]{:S(2)}) copy-start(f32[256]{0:T(256)S(1)} %broadcast_multiply_fusion) | copy-start | bytes 3076
Sparse Core Ops, SparseCore 0:
  9.8 37.5 all-gather.4
  50.0 124.5 all-gather.2
where the time goes:
time: 273 us; the launch traced here: 270 us
  matrix products  81.8 us (30%)
  waiting for transfers between devices  65.6 us (24%)
  blocking collectives  56.3 us (21%)
  local copies, waits for them, and re-layouts  34.8 us (13%)
  between operations  14.1 us (5%)
  starting transfers between devices  11.9 us (4%)
  other arithmetic  5.02 us (2%)
    all_to_all x1, waiting for transfers between devices, local(): lax.all_to_all(pooled, 'mp', split_axis=0, concat_axis=1, tiled=True)  64.3 us
    all_to_all x1, blocking collectives, local(): lax.all_to_all(grads, 'mp', split_axis=1, concat_axis=0, tiled=True)  56.3 us
    dot_general x16, matrix products, one_block(): jnp.dot(onehot, slab, preferred_element_type=jnp.float32)  45.5 us
    dot_general x3, matrix products, dot_last(): lax.dot_general(left, right, (((1,), (1,)), ((), ())), preferred_element_...  18.5 us
    unnamed x18, local copies, waits for them, and re-layouts  18.4 us
    all_to_all x1, starting transfers between devices, local(): lax.all_to_all(pooled, 'mp', split_axis=0, concat_axis=1, tiled=True)  11.8 us
    squeeze x16, local copies, waits for them, and re-layouts, pool_rows(): summed = lax.map(one_block, blocked)  11 us
    dot_general x1, matrix products, local(): jnp.dot(x1, lax.all_gather(tower_weight, 'mp', axis=0, tiled=True), prefe...  7.98 us
  transfers between devices with their start and end apart: 3, of which 1 were waited for; matrix products, arithmetic and copies ran while one was open for 34% of the time, Pallas kernels for 0%

commit v1 on v0

v1 whole, which is shorter than its diff:
```python
import jax
import jax.numpy as jnp
from jax import lax
from jax.sharding import PartitionSpec as P


def members(counts_row, rows):
    ends = jnp.cumsum(counts_row)
    starts = ends - counts_row
    place = jnp.arange(rows, dtype=jnp.int32)[:, None]
    return (place >= starts[None, :]) & (place < ends[None, :])


def dot_last(left, right):
    return lax.dot_general(
        left, right, (((1,), (1,)), ((), ())), preferred_element_type=jnp.float32
    )


def pair_grad(scores, member, labels):
    gain = jnp.exp2(labels.astype(jnp.float32))
    member_f = member.astype(jnp.float32)
    same = jnp.dot(member_f, member_f.T) > 0.5
    diff = gain[:, None] - gain[None, :]
    gap = scores[None, :] - scores[:, None]
    turn = jnp.where(diff > 0, jax.nn.sigmoid(gap), jax.nn.sigmoid(-gap))
    total = jnp.sum(jnp.where(same, diff * turn, 0.0), axis=1)
    seg_gain = jnp.sum(jnp.where(member, (gain - 1.0)[:, None], 0.0), axis=0)
    norm = jnp.sum(jnp.where(member, seg_gain[None, :], 0.0), axis=1)
    return -total / jnp.maximum(norm, 1.0)


def local(
    table,
    ids,
    counts,
    labels,
    request_home,
    user_codes,
    cross_down,
    cross_up,
    cross_bias,
    tower_weight,
    tower_bias,
):
    f32, bf16 = jnp.float32, jnp.bfloat16
    n_mp = lax.axis_size("mp")
    n_dp = lax.axis_size("dp")
    d_idx = lax.axis_index("dp")
    m_idx = lax.axis_index("mp")
    rows = labels.shape[0]
    seg_count = counts.shape[1]
    width = user_codes.shape[1]
    emb = table.shape[2]
    rank = cross_down.shape[1]
    scale = 1.0 / jnp.sqrt(jnp.float32(width))

    piece = tower_weight.shape[1] // n_dp
    w_piece = lax.dynamic_slice_in_dim(tower_weight, d_idx * piece, piece, axis=1)
    w_cols = lax.all_gather(w_piece, "mp", axis=0, tiled=True)
    w_all = lax.all_gather(w_cols, "dp", axis=1, tiled=True)
    w3 = w_all.reshape(n_mp, emb, width)

    held = user_codes.shape[0]
    home_local = lax.dynamic_slice_in_dim(request_home, d_idx * held, held)
    wanted = (
        (jnp.arange(n_dp, dtype=jnp.int32)[:, None] * n_mp + m_idx) * seg_count
        + jnp.arange(seg_count, dtype=jnp.int32)[None, :]
    ).reshape(-1)
    pick = (home_local[None, :] == wanted[:, None]).astype(bf16)
    mine = jnp.dot(pick, user_codes, preferred_element_type=f32).astype(bf16)
    user_seg = lax.psum_scatter(
        mine.reshape(n_dp, seg_count, width), "dp", scatter_dimension=0, tiled=False
    )

    slab = table[0]
    picked = jnp.take(slab, ids[:, 0, :], axis=0, mode="clip")
    pooled = jnp.sum(picked.astype(f32), axis=1).astype(bf16)
    x0f = lax.all_to_all(
        pooled.reshape(n_mp, rows, emb), "mp", split_axis=0, concat_axis=0, tiled=True
    )

    member = members(counts[0], rows)
    cd3 = cross_down.reshape(n_mp, emb, rank)
    cu3 = cross_up.reshape(rank, n_mp, emb)
    bias3 = cross_bias.reshape(n_mp, 1, emb)
    z = jnp.einsum("fcd,fdr->cr", x0f, cd3, preferred_element_type=f32).astype(bf16)
    cross = jnp.einsum("cr,rfd->fcd", z, cu3, preferred_element_type=f32) + bias3
    x1 = (x0f * cross + x0f).astype(bf16)
    act = jnp.einsum("fcd,fdh->ch", x1, w3, preferred_element_type=f32) + tower_bias
    sig = jax.nn.sigmoid(act)
    hidden = (act * sig).astype(bf16)
    pair = dot_last(hidden, user_seg)
    score = jnp.sum(jnp.where(member, pair, 0.0), axis=1) * scale
    dscore = pair_grad(score, member, labels)
    code = jnp.dot(member.astype(bf16), user_seg, preferred_element_type=f32)
    slope = sig * (1.0 + act * (1.0 - sig))
    dact = (dscore[:, None] * code * scale * slope).astype(bf16)
    dx1 = jnp.einsum("ch,fdh->fcd", dact, w3, preferred_element_type=f32)
    dcross = (dx1 * x0f).astype(bf16)
    dz = jnp.einsum("fcd,rfd->cr", dcross, cu3, preferred_element_type=f32).astype(bf16)
    dx0 = dx1 * (1.0 + cross) + jnp.einsum(
        "cr,fdr->fcd", dz, cd3, preferred_element_type=f32
    )
    grads = dx0.astype(bf16)
    returned = lax.all_to_all(grads, "mp", split_axis=0, concat_axis=0, tiled=True)
    return (score, returned.reshape(n_mp * rows, 1, emb))


def solution(mesh):
    in_specs = (
        P("mp", None, None),
        P("dp", "mp", None),
        P(("dp", "mp"), None),
        P(("dp", "mp")),
        P(),
        P("dp", None),
        P(),
        P(),
        P(),
        P("mp", None),
        P(),
    )
    out_specs = (P(("dp", "mp")), P("dp", "mp", None))
    return jax.shard_map(local, mesh=mesh, in_specs=in_specs, out_specs=out_specs, check_vma=False)
```

time: 273 us -> 347 us (1.27)
  waiting for transfers between devices: 65.6 us -> 123 us
  matrix products: 81.8 us -> 32.4 us
  other arithmetic: 5.02 us -> 46.4 us
  local copies, waits for them, and re-layouts: 34.8 us -> 69.3 us
  starting transfers between devices: 11.9 us -> 7.96 us
    all_gather x2, waiting for transfers between devices: 0.01 us -> 80.6 us  [the longest x1 80.5 us: local(): w_cols = lax.all_gather(w_piece, 'mp', axis=0, tiled=True)]
    gather x0 -> x1, local copies, waits for them, and re-layouts: none -> 57.8 us  [local(): picked = jnp.take(slab, ids[:, 0, :], axis=0, mode='clip')]
    reduce_sum x0 -> x1, other arithmetic: none -> 45.8 us  [local(): pooled = jnp.sum(picked.astype(f32), axis=1).astype(bf16)]
    dot_general x19 -> x5, matrix products: 63 us -> 30.9 us  [the longest x1 9.56 us: local(): jnp.einsum('cr,fdr->fcd', dz, cd3, preferred_element_type=f32)]
    all_to_all x1, waiting for transfers between devices: 64.3 us -> 42.3 us  [local(): lax.all_to_all(pooled.reshape(n_mp, rows, emb), 'mp', split_axis=0, conca...]
    dot_general x3 -> x1, matrix products: 18.5 us -> 1.13 us  [dot_last(): lax.dot_general(left, right, (((1,), (1,)), ((), ())), preferred_element_...]
    unnamed x18 -> x20, local copies, waits for them, and re-layouts: 18.4 us -> 5.04 us
    squeeze x16 -> x0, local copies, waits for them, and re-layouts: 11 us -> none  [pool_rows(): summed = lax.map(one_block, blocked)]
  transfers between devices with their start and end apart: 3 -> 4, of which waited for: 1 -> 2; matrix products, arithmetic and copies ran while one was open for 34% -> 37% of each run, Pallas kernels for 0% -> 0%
where the time goes in v1:
time: 347 us; the launch traced here: 346 us
  waiting for transfers between devices  123 us (35%)
  local copies, waits for them, and re-layouts  69.3 us (20%)
  blocking collectives  53.3 us (15%)
  other arithmetic  46.4 us (13%)
  matrix products  32.4 us (9%)
  between operations  13.9 us (4%)
  starting transfers between devices  7.96 us (2%)
    all_gather x1, waiting for transfers between devices, local(): w_cols = lax.all_gather(w_piece, 'mp', axis=0, tiled=True)  80.5 us
    gather x1, local copies, waits for them, and re-layouts, local(): picked = jnp.take(slab, ids[:, 0, :], axis=0, mode='clip')  57.8 us
    all_to_all x1, blocking collectives, local(): lax.all_to_all(grads, 'mp', split_axis=0, concat_axis=0, tiled=True)  53.3 us
    reduce_sum x1, other arithmetic, local(): pooled = jnp.sum(picked.astype(f32), axis=1).astype(bf16)  45.8 us
    all_to_all x1, waiting for transfers between devices, local(): lax.all_to_all(pooled.reshape(n_mp, rows, emb), 'mp', split_axis=0, conca...  42.3 us
    dot_general x1, matrix products, local(): jnp.einsum('cr,fdr->fcd', dz, cd3, preferred_element_type=f32)  9.56 us
    all_to_all x1, starting transfers between devices, local(): lax.all_to_all(pooled.reshape(n_mp, rows, emb), 'mp', split_axis=0, conca...  7.66 us
    dot_general x1, matrix products, local(): dx1 = jnp.einsum('ch,fdh->fcd', dact, w3, preferred_element_type=f32)  7.14 us
  transfers between devices with their start and end apart: 4, of which 2 were waited for; matrix products, arithmetic and copies ran while one was open for 37% of the time, Pallas kernels for 0%

profile of v1, /device:TPU:2, one launch (start us, length us, event | category | flops | bytes accessed | tf_op | source)
XLA Modules:
  0.0 346.1 jit_solution(14947742715400940034)
XLA Ops:
  7.2 1.5 constant_dynamic-slice_fusion
  8.8 80.5 %all-gather.3.cloned.1.call-done = bf16[4096,128]{1,0:T(8,128)(2,1)} async-done(((bf16[128,128]{1,0:T(8,128)(2,1)}), bf16[4096,128]{1,0:T(8,128)(2,1)}) %all-gather.3.cloned.1.call-update) | async-done | bytes 1048592 | tf_op jit(solution)/shard_map/all_gather | solution.py:60
  89.4 3.4 copy.18
  92.8 4.1 %reshape.87 = s32[16384]{0:T(1024)S(1)} reshape(s32[8192,1,2]{2,0,1:T(8,128)} %copy.18) | data formatting | bytes 131072 | tf_op jit(solution)/shard_map/jit(_take)/broadcast_in_dim | solution.py:77
  96.9 57.8 %gather_fusion = bf16[16384,128]{1,0:T(8,128)(2,1)} fusion(bf16[2048,128]{1,0:T(8,128)(2,1)S(1)} %bitcast.114, s32[16384]{0:T(1024)S(1)} %broadcast_clamp_fusion), kind=kCustom, calls=%fused_computation | custom fusion | bytes 8454144 | tf_op jit(solution)/shard_map/jit(_take)/gather | solution.py:77
  154.7 45.8 %reduce_sum.48 = bf16[8192,128]{1,0:T(8,128)(2,1)} reduce(bf16[8192,2,128]{2,1,0:T(2,128)(2,1)} %bitcast.115, bf16[]{:T(256)} %constant.18.clone.1), dimensions={1}, to_apply=%region_1.2 | reduce | flops 1048576 | bytes 6291458 | tf_op jit(solution)/shard_map/reduce_sum | solution.py:78
  200.5 7.7 %all-to-all-start = ((bf16[32,256,128]{2,1,0:T(8,128)(2,1)}), bf16[32,256,128]{2,1,0:T(8,128)(2,1)}, u32[]{:S(2)}, u32[]{:S(2)}) async-start(bf16[32,256,128]{2,1,0:T(8,128)(2,1)} %bitcast.116), calls=%async_computation | async-start | bytes 4194304 | tf_op jit(solution)/shard_map/all_to_all | solution.py:79
  208.2 0.2 reduce-scatter.2.cloned.1.call-start
  208.5 0.1 add.100
  208.6 0.8 dynamic_slice.7
  209.4 0.9 fusion.36
  210.3 0.2 reduce-window.4
  210.5 0.2 select_reduce_fusion.1
  210.7 0.1 select_reduce_fusion
  210.8 42.3 %all-to-all-done = bf16[32,256,128]{2,1,0:T(8,128)(2,1)} async-done(((bf16[32,256,128]{2,1,0:T(8,128)(2,1)}), bf16[32,256,128]{2,1,0:T(8,128)(2,1)}, u32[]{:S(2)}, u32[]{:S(2)}) %all-to-all-start) | async-done | bytes 2097184 | tf_op jit(solution)/shard_map/all_to_all | solution.py:79
  253.1 6.6 %fusion.8 = f32[256,32,128]{2,0,1:T(8,128)} fusion(bf16[32,256,128]{2,1,0:T(8,128)(2,1)} %all-to-all-done, bf16[32,128,256]{2,1,0:T(8,128)(2,1)S(1)} %bitcast.112, bf16[256,4096]{1,0:T(8,128)(2,1)} %param.18), kind=kOutput, calls=%fused_computation.12 | convolution fusion | flops 1073807360 | bytes 10485760 | tf_op jit(solution)/shard_map/cr,rfd->fcd/dot_general | solution.py:88
  259.7 6.7 %fusion.18 = f32[256,1024]{1,0:T(8,128)S(1)} fusion(bf16[32,128,1024]{2,1,0:T(8,128)(2,1)} %bitcast.125, bf16[32,256,128]{2,1,0:T(8,128)(2,1)} %all-to-all-done, f32[256,32,128]{2,0,1:T(8,128)} %fusion.8, f32[32,128]{1,0:T(8,128)S(1)} %bitcast.118, f32[1024]{0:T(1024)S(1)} %copy-done.7), kind=kOutput, calls=%fused_computation.21 | convolution fusion | flops 2152988672 | bytes 15749120 | tf_op jit(solution)/shard_map/fcd,fdh->ch/dot_general | solution.py:90
  266.4 1.1 fusion.47
  267.6 0.4 fusion.35
  268.0 0.3 copy-done.6
  268.3 7.1 %fusion.48 = f32[32,128,256]{1,2,0:T(8,128)} fusion(bf16[32,128,1024]{2,1,0:T(8,128)(2,1)} %bitcast.126, f32[256,1024]{1,0:T(8,128)S(1)} %fusion.18, f32[256]{0:T(256)S(1)} %maximum_divide_fusion, bf16[1,8,1024]{2,1,0:T(8,128)(2,1)S(1)} %copy-done.6, s32[8]{0:T(128)S(1)} %bitcast.124, s32[8]{0:T(128)S(1)} %fusion.65), kind=kOutput, calls=%fused_computation.39 | convolution fusion | flops 2154567680 | bytes 13648960 | tf_op jit(solution)/shard_map/ch,fdh->fcd/dot_general | solution.py:99
  275.4 9.6 %fusion.2 = bf16[32,256,128]{2,1,0:T(8,128)(2,1)} fusion(f32[32,128,256]{1,2,0:T(8,128)} %fusion.48, f32[256,32,128]{2,0,1:T(8,128)} %fusion.8, bf16[32,128,256]{2,1,0:T(8,128)(2,1)S(1)} %bitcast.113, f32[32,128]{1,0:T(8,128)S(1)} %bitcast.119, bf16[32,256,128]{2,1,0:T(8,128)(2,1)} %all-to-all-done, bf16[256,4096]{1,0:T(8,128)(2,1)} %param.18), kind=kOutput, calls=%fused_computation.6 | convolution fusion | flops 1082195968 | bytes 16793600 | tf_op jit(solution)/shard_map/cr,fdr->fcd/dot_general | solution.py:102
  285.0 53.3 %all_to_all.10 = bf16[32,256,128]{2,1,0:T(8,128)(2,1)S(1)} all-to-all(bf16[32,256,128]{2,1,0:T(8,128)(2,1)} %fusion.2), channel_id=1, replica_groups=mesh['dp'=8,'mp'=32] {'mp'}, dimensions={0} | all-to-all | bytes 4194304 | tf_op jit(solution)/shard_map/all_to_all | solution.py:106
  338.3 1.3 copy.43
  (31 shorter events, 0.3 us)
Async XLA Ops:
  7.2 246.0 %copy-start = (bf16[4096,256]{1,0:T(8,128)(2,1)S(1)}, bf16[4096,256]{1,0:T(8,128)(2,1)}, u32[]{:S(2)}) copy-start(bf16[4096,256]{1,0:T(8,128)(2,1)} %param.17) | copy-start | bytes 6291460
  7.2 82.2 %all-gather.3.cloned.1.call-start = ((), (), s32[]{:S(2)}) async-start(), calls=%async_computation.3 | async-start | bytes 1081344 | tf_op jit(solution)/shard_map/all_gather | solution.py:60
  8.8 251.0 %all-gather.5.cloned.1.call-start = ((), (), s32[]{:S(2)}) async-start(), calls=%async_computation.4 | async-start | bytes 9437184 | tf_op jit(solution)/shard_map/all_gather | solution.py:61
  92.8 4.1 %copy-start.1 = (bf16[1,2048,128]{2,1,0:T(8,128)(2,1)S(1)}, bf16[1,2048,128]{2,1,0:T(8,128)(2,1)}, u32[]{:S(2)}) copy-start(bf16[1,2048,128]{2,1,0:T(8,128)(2,1)} %param.11) | copy-start | bytes 1572868
  200.5 8.8 %copy-start.2 = (bf16[256,1024]{1,0:T(8,128)(2,1)S(1)}, bf16[256,1024]{1,0:T(8,128)(2,1)}, u32[]{:S(2)}) copy-start(bf16[256,1024]{1,0:T(8,128)(2,1)} %param.16) | copy-start | bytes 1572868
  200.5 9.8 %copy-start.8 = (s32[1,8]{1,0:T(1,128)S(1)}, s32[1,8]{1,0:T(1,128)}, u32[]{:S(2)}) copy-start(s32[1,8]{1,0:T(1,128)} %param.13) | copy-start | bytes 100
  200.5 10.0 %copy-start.4 = (s32[256]{0:T(256)S(1)}, s32[256]{0:T(256)}, u32[]{:S(2)}) copy-start(s32[256]{0:T(256)} %param.14) | copy-start | bytes 3076
  200.5 52.6 %all-to-all-start = ((bf16[32,256,128]{2,1,0:T(8,128)(2,1)}), bf16[32,256,128]{2,1,0:T(8,128)(2,1)}, u32[]{:S(2)}, u32[]{:S(2)}) async-start(bf16[32,256,128]{2,1,0:T(8,128)(2,1)} %bitcast.116), calls=%async_computation | async-start | bytes 4194304 | tf_op jit(solution)/shard_map/all_to_all | solution.py:79
  208.2 58.2 %reduce-scatter.2.cloned.1.call-start = ((), (), s32[]{:S(2)}) async-start(), calls=%async_computation.5 | async-start | bytes 147456 | tf_op jit(solution)/shard_map/reduce_scatter | solution.py:72
  253.1 6.6 %copy-start.3 = (f32[4096]{0:T(1024)S(1)}, f32[4096]{0:T(1024)}, u32[]{:S(2)}) copy-start(f32[4096]{0:T(1024)} %param.19) | copy-start | bytes 49156
  253.1 6.6 %copy-start.7 = (f32[1024]{0:T(1024)S(1)}, f32[1024]{0:T(1024)}, u32[]{:S(2)}) copy-start(f32[1024]{0:T(1024)} %param.21) | copy-start | bytes 12292
  267.6 0.7 copy-start.6
  267.6 7.8 %copy-start.5 = (f32[256]{0:T(256)}, f32[256]{0:T(256)S(1)}, u32[]{:S(2)}) copy-start(f32[256]{0:T(256)S(1)} %broadcast_multiply_fusion) | copy-start | bytes 3076
Sparse Core Ops, SparseCore 0:
  11.1 78.1 all-gather.2
  91.2 54.5 all-gather.4
  211.5 35.0 reduce-scatter.1

commit v2 on v1

--- a/solution.py
+++ b/solution.py
@@ -1,7 +1,51 @@
 import jax
 import jax.numpy as jnp
 from jax import lax
+from jax.experimental import pallas as pl
+from jax.experimental.pallas import tpu as pltpu
 from jax.sharding import PartitionSpec as P
+
+
+def pool_kernel(ids_ref, tab_ref, out_ref, tabf, acc):
+    step = pl.program_id(0)
+    blk = out_ref.shape[0]
+    total = ids_ref.shape[0] // 2
+
+    @pl.when(step == 0)
+    def _():
+        tabf[...] = tab_ref[...].astype(jnp.float32)
+
+    base = step * blk
+
+    def body(j, carry):
+        for u in range(8):
+            c = j * 8 + u
+            a = ids_ref[base + c]
+            b = ids_ref[total + base + c]
+            acc[pl.ds(c, 1), :] = tabf[pl.ds(a, 1), :] + tabf[pl.ds(b, 1), :]
+        return carry
+
+    lax.fori_loop(0, blk // 8, body, 0)
+    out_ref[...] = acc[...].astype(out_ref.dtype)
+
+
+def pool_rows(slab, flat_ids, count, blk=1024):
+    slab_rows, emb = slab.shape
+    spec = pltpu.PrefetchScalarGridSpec(
+        num_scalar_prefetch=1,
+        grid=(count // blk,),
+        in_specs=[pl.BlockSpec((slab_rows, emb), lambda i, ids: (0, 0))],
+        out_specs=pl.BlockSpec((blk, emb), lambda i, ids: (i, 0)),
+        scratch_shapes=[
+            pltpu.VMEM((slab_rows, emb), jnp.float32),
+            pltpu.VMEM((blk, emb), jnp.float32),
+        ],
+    )
+    return pl.pallas_call(
+        pool_kernel,
+        grid_spec=spec,
+        out_shape=jax.ShapeDtypeStruct((count, emb), slab.dtype),
+    )(flat_ids, slab)
 
 
 def members(counts_row, rows):
@@ -57,7 +101,10 @@
 
     piece = tower_weight.shape[1] // n_dp
     w_piece = lax.dynamic_slice_in_dim(tower_weight, d_idx * piece, piece, axis=1)
-    w_cols = lax.all_gather(w_piece, "mp", axis=0, tiled=True)
+    w_cols = lax.all_to_all(
+        jnp.broadcast_to(w_piece[None], (n_mp,) + w_piece.shape),
+        "mp", split_axis=0, concat_axis=0, tiled=True,
+    ).reshape(n_mp * w_piece.shape[0], piece)
     w_all = lax.all_gather(w_cols, "dp", axis=1, tiled=True)
     w3 = w_all.reshape(n_mp, emb, width)
 
@@ -73,9 +120,9 @@
         mine.reshape(n_dp, seg_count, width), "dp", scatter_dimension=0, tiled=False
     )
 
-    slab = table[0]
-    picked = jnp.take(slab, ids[:, 0, :], axis=0, mode="clip")
-    pooled = jnp.sum(picked.astype(f32), axis=1).astype(bf16)
+    count = ids.shape[0]
+    flat_ids = jnp.transpose(ids[:, 0, :]).reshape(-1)
+    pooled = pool_rows(table[0], flat_ids, count)
     x0f = lax.all_to_all(
         pooled.reshape(n_mp, rows, emb), "mp", split_axis=0, concat_axis=0, tiled=True
     )

time: 347 us -> 224 us (0.65)
  waiting for transfers between devices: 123 us -> 42.1 us
  local copies, waits for them, and re-layouts: 69.3 us -> 8.29 us
  other arithmetic: 46.4 us -> 0.56 us
  blocking collectives: 53.3 us -> 95 us
  Pallas kernels: 0 us -> 25 us
    all_gather x1 -> x0, waiting for transfers between devices: 80.5 us -> none  [local(): w_cols = lax.all_gather(w_piece, 'mp', axis=0, tiled=True)]
    gather x1 -> x0, local copies, waits for them, and re-layouts: 57.8 us -> none  [local(): picked = jnp.take(slab, ids[:, 0, :], axis=0, mode='clip')]
    reduce_sum x1 -> x0, other arithmetic: 45.8 us -> none  [local(): pooled = jnp.sum(picked.astype(f32), axis=1).astype(bf16)]
    all_to_all x0 -> x1, blocking collectives: none -> 39.6 us  [local(): lax.all_to_all(jnp.broadcast_to(w_piece[None], (n_mp,) + w_piece.shape),...]
    pallas_call x0 -> x1, Pallas kernels: none -> 25 us  [pool_rows(): pl.pallas_call(pool_kernel, grid_spec=spec, out_shape=jax.ShapeDtypeStruc...]
    reshape x0 -> x1, local copies, waits for them, and re-layouts: none -> 4.09 us  [local(): cu3 = cross_up.reshape(rank, n_mp, emb)]
    broadcast_in_dim x1, local copies, waits for them, and re-layouts: 4.06 us -> 0.23 us  [local(): jnp.broadcast_to(w_piece[None], (n_mp,) + w_piece.shape)]
  transfers between devices with their start and end apart: 4 -> 3, of which waited for: 2 -> 1; matrix products, arithmetic and copies ran while one was open for 37% -> 9% of each run, Pallas kernels for 0% -> 11%
where the time goes in v2:
time: 224 us; the launch traced here: 223 us
  blocking collectives  95 us (42%)
  waiting for transfers between devices  42.1 us (19%)
  matrix products  32.4 us (14%)
  Pallas kernels  25 us (11%)
  between operations  14.2 us (6%)
  local copies, waits for them, and re-layouts  8.29 us (4%)
  starting transfers between devices  5.83 us (3%)
    all_to_all x1, blocking collectives, local(): lax.all_to_all(grads, 'mp', split_axis=0, concat_axis=0, tiled=True)  55.4 us
    all_to_all x1, waiting for transfers between devices, local(): lax.all_to_all(pooled.reshape(n_mp, rows, emb), 'mp', split_axis=0, conca...  42.1 us
    all_to_all x1, blocking collectives, local(): lax.all_to_all(jnp.broadcast_to(w_piece[None], (n_mp,) + w_piece.shape),...  39.6 us
    pallas_call x1, Pallas kernels, pool_rows(): pl.pallas_call(pool_kernel, grid_spec=spec, out_shape=jax.ShapeDtypeStruc...  25 us
    dot_general x1, matrix products, local(): jnp.einsum('cr,fdr->fcd', dz, cd3, preferred_element_type=f32)  9.52 us
    dot_general x1, matrix products, local(): dx1 = jnp.einsum('ch,fdh->fcd', dact, w3, preferred_element_type=f32)  7.14 us
    dot_general x1, matrix products, local(): jnp.einsum('fcd,fdh->ch', x1, w3, preferred_element_type=f32) + tower_bias  6.69 us
    dot_general x1, matrix products, local(): jnp.einsum('cr,rfd->fcd', z, cu3, preferred_element_type=f32) + bias3  6.6 us
  transfers between devices with their start and end apart: 3, of which 1 were waited for; matrix products, arithmetic and copies ran while one was open for 9% of the time, Pallas kernels for 11%

profile of v2, /device:TPU:2, one launch (start us, length us, event | category | flops | bytes accessed | tf_op | source)
XLA Modules:
  0.0 223.3 jit_solution(6106555202517490794)
XLA Ops:
  7.2 0.9 constant_dynamic-slice_fusion
  8.1 0.2 broadcast_in_dim.20
  8.4 39.6 %all_to_all.15 = bf16[32,128,128]{2,1,0:T(8,128)(2,1)} all-to-all(bf16[32,128,128]{2,1,0:T(8,128)(2,1)S(1)} %broadcast_in_dim.20), channel_id=1, replica_groups=mesh['dp'=8,'mp'=32] {'mp'}, dimensions={0} | all-to-all | bytes 2097152 | tf_op jit(solution)/shard_map/all_to_all | solution.py:104
  48.0 0.6 copy.20
  48.6 25.0 %shard_map.122 = bf16[8192,128]{1,0:T(8,128)(2,1)} custom-call(s32[16384]{0:T(1024)} %bitcast.105, bf16[2048,128]{1,0:T(8,128)(2,1)} %bitcast.104), custom_call_target="tpu_custom_call" | custom-call | tf_op jit(solution)/shard_map/pallas_call | solution.py:44
  73.6 5.8 %all-to-all-start = ((bf16[32,256,128]{2,1,0:T(8,128)(2,1)}), bf16[32,256,128]{2,1,0:T(8,128)(2,1)}, u32[]{:S(2)}, u32[]{:S(2)}) async-start(bf16[32,256,128]{2,1,0:T(8,128)(2,1)} %bitcast.101), calls=%async_computation | async-start | bytes 4194304 | tf_op jit(solution)/shard_map/all_to_all | solution.py:126
  79.4 0.1 iota_add_fusion
  79.5 0.1 add.100
  79.6 0.8 dynamic_slice.7
  80.3 0.9 fusion.30
  81.3 0.2 reduce-window.4
  81.5 4.1 %copy.19 = bf16[256,4096]{0,1:T(8,128)(2,1)} copy(bf16[256,4096]{1,0:T(8,128)(2,1)} %param.18) | data formatting | bytes 4194304 | tf_op jit(solution)/shard_map/reshape | solution.py:132
  85.6 0.2 select_reduce_fusion.1
  85.8 0.1 select_reduce_fusion
  85.8 42.1 %all-to-all-done = bf16[32,256,128]{2,1,0:T(8,128)(2,1)} async-done(((bf16[32,256,128]{2,1,0:T(8,128)(2,1)}), bf16[32,256,128]{2,1,0:T(8,128)(2,1)}, u32[]{:S(2)}, u32[]{:S(2)}) %all-to-all-start) | async-done | bytes 2097184 | tf_op jit(solution)/shard_map/all_to_all | solution.py:126
  127.9 6.6 %fusion.35 = f32[256,32,128]{2,0,1:T(8,128)} fusion(bf16[256,32,128]{0,2,1:T(8,128)(2,1)} %bitcast.99, bf16[32,256,128]{2,1,0:T(8,128)(2,1)} %all-to-all-done, bf16[32,128,256]{2,1,0:T(8,128)(2,1)S(1)} %bitcast.97), kind=kOutput, calls=%fused_computation.31 | convolution fusion | flops 1073807360 | bytes 10485760 | tf_op jit(solution)/shard_map/cr,rfd->fcd/dot_general | solution.py:135
  134.5 6.7 %fusion.13 = f32[256,1024]{1,0:T(8,128)S(1)} fusion(bf16[32,128,1024]{2,1,0:T(8,128)(2,1)} %bitcast.114, bf16[32,256,128]{2,1,0:T(8,128)(2,1)} %all-to-all-done, f32[256,32,128]{2,0,1:T(8,128)} %fusion.35, f32[32,128]{1,0:T(8,128)S(1)} %bitcast.107, f32[1024]{0:T(1024)S(1)} %copy-done.7), kind=kOutput, calls=%fused_computation.15 | convolution fusion | flops 2152988672 | bytes 15749120 | tf_op jit(solution)/shard_map/fcd,fdh->ch/dot_general | solution.py:137
  141.3 1.1 fusion.34
  142.4 0.4 fusion.26
  142.9 0.2 copy-done.6
  143.1 7.1 %fusion.36 = f32[32,128,256]{1,2,0:T(8,128)} fusion(bf16[32,128,1024]{2,1,0:T(8,128)(2,1)} %bitcast.115, f32[256,1024]{1,0:T(8,128)S(1)} %fusion.13, f32[256]{0:T(256)S(1)} %maximum_divide_fusion, bf16[1,8,1024]{2,1,0:T(8,128)(2,1)S(1)} %copy-done.6, s32[8]{0:T(128)S(1)} %bitcast.113, s32[8]{0:T(128)S(1)} %fusion.53), kind=kOutput, calls=%fused_computation.34 | convolution fusion | flops 2154567680 | bytes 13648960 | tf_op jit(solution)/shard_map/ch,fdh->fcd/dot_general | solution.py:146
  150.3 9.5 %fusion.2 = bf16[32,256,128]{2,1,0:T(8,128)(2,1)} fusion(f32[32,128,256]{1,2,0:T(8,128)} %fusion.36, f32[256,32,128]{2,0,1:T(8,128)} %fusion.35, bf16[32,128,256]{2,1,0:T(8,128)(2,1)S(1)} %bitcast.98, f32[32,128]{1,0:T(8,128)S(1)} %bitcast.108, bf16[256,32,128]{0,2,1:T(8,128)(2,1)} %bitcast.100, bf16[32,256,128]{2,1,0:T(8,128)(2,1)} %all-to-all-done), kind=kOutput, calls=%fused_computation.5 | convolution fusion | flops 1082195968 | bytes 16793600 | tf_op jit(solution)/shard_map/cr,fdr->fcd/dot_general | solution.py:149
  159.8 55.4 %all_to_all.16 = bf16[32,256,128]{2,1,0:T(8,128)(2,1)S(1)} all-to-all(bf16[32,256,128]{2,1,0:T(8,128)(2,1)} %fusion.2), channel_id=1, replica_groups=mesh['dp'=8,'mp'=32] {'mp'}, dimensions={0} | all-to-all | bytes 4194304 | tf_op jit(solution)/shard_map/all_to_all | solution.py:153
  215.2 1.3 copy.22
  (28 shorter events, 0.2 us)
Async XLA Ops:
  7.2 120.8 %copy-start = (bf16[4096,256]{1,0:T(8,128)(2,1)S(1)}, bf16[4096,256]{1,0:T(8,128)(2,1)}, u32[]{:S(2)}) copy-start(bf16[4096,256]{1,0:T(8,128)(2,1)} %param.17) | copy-start | bytes 6291460
  7.2 127.4 %all-gather.2.cloned.1.call-start = ((), (), s32[]{:S(2)}) async-start(), calls=%async_computation.4 | async-start | bytes 9437184 | tf_op jit(solution)/shard_map/all_gather | solution.py:108
  8.1 39.8 %copy-start.2 = (s32[8192,1,2]{0,2,1:T(2,128)S(1)}, s32[8192,1,2]{0,2,1:T(2,128)}, u32[]{:S(2)}) copy-start(s32[8192,1,2]{0,2,1:T(2,128)} %param.12) | copy-start | bytes 196612
  73.6 6.7 %copy-start.1 = (bf16[256,1024]{1,0:T(8,128)(2,1)S(1)}, bf16[256,1024]{1,0:T(8,128)(2,1)}, u32[]{:S(2)}) copy-start(bf16[256,1024]{1,0:T(8,128)(2,1)} %param.16) | copy-start | bytes 1572868
  73.6 7.7 %copy-start.8 = (s32[1,8]{1,0:T(1,128)S(1)}, s32[1,8]{1,0:T(1,128)}, u32[]{:S(2)}) copy-start(s32[1,8]{1,0:T(1,128)} %param.13) | copy-start | bytes 100
  73.6 54.3 %all-to-all-start = ((bf16[32,256,128]{2,1,0:T(8,128)(2,1)}), bf16[32,256,128]{2,1,0:T(8,128)(2,1)}, u32[]{:S(2)}, u32[]{:S(2)}) async-start(bf16[32,256,128]{2,1,0:T(8,128)(2,1)} %bitcast.101), calls=%async_computation | async-start | bytes 4194304 | tf_op jit(solution)/shard_map/all_to_all | solution.py:126
  79.4 61.9 %reduce-scatter.2.cloned.1.call-start = ((), (), s32[]{:S(2)}) async-start(), calls=%async_computation.5 | async-start | bytes 147456 | tf_op jit(solution)/shard_map/reduce_scatter | solution.py:119
  81.5 4.1 %copy-start.4 = (s32[256]{0:T(256)S(1)}, s32[256]{0:T(256)}, u32[]{:S(2)}) copy-start(s32[256]{0:T(256)} %param.14) | copy-start | bytes 3076
  127.9 6.6 %copy-start.3 = (f32[4096]{0:T(1024)S(1)}, f32[4096]{0:T(1024)}, u32[]{:S(2)}) copy-start(f32[4096]{0:T(1024)} %param.19) | copy-start | bytes 49156
  127.9 6.6 %copy-start.7 = (f32[1024]{0:T(1024)S(1)}, f32[1024]{0:T(1024)}, u32[]{:S(2)}) copy-start(f32[1024]{0:T(1024)} %param.21) | copy-start | bytes 12292
  142.4 0.7 copy-start.6
  142.4 7.8 %copy-start.5 = (f32[256]{0:T(256)}, f32[256]{0:T(256)S(1)}, u32[]{:S(2)}) copy-start(f32[256]{0:T(256)S(1)} %broadcast_multiply_fusion) | copy-start | bytes 3076
Sparse Core Ops, SparseCore 0:
  48.1 52.8 all-gather.1
  103.5 34.9 reduce-scatter.1

commit v3 on v2

--- a/solution.py
+++ b/solution.py
@@ -3,7 +3,7 @@
 from jax import lax
 from jax.experimental import pallas as pl
 from jax.experimental.pallas import tpu as pltpu
-from jax.sharding import PartitionSpec as P
+from jax.sharding import Mesh, PartitionSpec as P
 
 
 def pool_kernel(ids_ref, tab_ref, out_ref, tabf, acc):
@@ -72,6 +72,26 @@
     seg_gain = jnp.sum(jnp.where(member, (gain - 1.0)[:, None], 0.0), axis=0)
     norm = jnp.sum(jnp.where(member, seg_gain[None, :], 0.0), axis=1)
     return -total / jnp.maximum(norm, 1.0)
+
+
+DP = ("y", "c")
+MP = ("z", "x")
+
+
+def a2a_mp(v, nz, nx):
+    shape = v.shape
+    v = v.reshape((nz, nx) + shape[1:])
+    v = lax.all_to_all(v, "x", split_axis=1, concat_axis=1, tiled=True)
+    v = lax.all_to_all(v, "z", split_axis=0, concat_axis=0, tiled=True)
+    return v.reshape(shape)
+
+
+def gather_mp(v, nz, nx):
+    v = jnp.broadcast_to(v[None], (nx,) + v.shape)
+    v = lax.all_to_all(v, "x", split_axis=0, concat_axis=0, tiled=True)
+    v = jnp.broadcast_to(v[None], (nz,) + v.shape)
+    v = lax.all_to_all(v, "z", split_axis=0, concat_axis=0, tiled=True)
+    return v.reshape((nz * nx,) + v.shape[2:])
 
 
 def local(
@@ -88,10 +108,11 @@
     tower_bias,
 ):
     f32, bf16 = jnp.float32, jnp.bfloat16
-    n_mp = lax.axis_size("mp")
-    n_dp = lax.axis_size("dp")
-    d_idx = lax.axis_index("dp")
-    m_idx = lax.axis_index("mp")
+    nz, nx = lax.axis_size("z"), lax.axis_size("x")
+    n_mp = nz * nx
+    n_dp = lax.axis_size("y") * lax.axis_size("c")
+    d_idx = lax.axis_index("y") * lax.axis_size("c") + lax.axis_index("c")
+    m_idx = lax.axis_index("z") * nx + lax.axis_index("x")
     rows = labels.shape[0]
     seg_count = counts.shape[1]
     width = user_codes.shape[1]
@@ -101,11 +122,8 @@
 
     piece = tower_weight.shape[1] // n_dp
     w_piece = lax.dynamic_slice_in_dim(tower_weight, d_idx * piece, piece, axis=1)
-    w_cols = lax.all_to_all(
-        jnp.broadcast_to(w_piece[None], (n_mp,) + w_piece.shape),
-        "mp", split_axis=0, concat_axis=0, tiled=True,
-    ).reshape(n_mp * w_piece.shape[0], piece)
-    w_all = lax.all_gather(w_cols, "dp", axis=1, tiled=True)
+    w_cols = gather_mp(w_piece, nz, nx).reshape(n_mp * w_piece.shape[0], piece)
+    w_all = lax.all_gather(w_cols, DP, axis=1, tiled=True)
     w3 = w_all.reshape(n_mp, emb, width)
 
     held = user_codes.shape[0]
@@ -117,15 +135,13 @@
     pick = (home_local[None, :] == wanted[:, None]).astype(bf16)
     mine = jnp.dot(pick, user_codes, preferred_element_type=f32).astype(bf16)
     user_seg = lax.psum_scatter(
-        mine.reshape(n_dp, seg_count, width), "dp", scatter_dimension=0, tiled=False
+        mine.reshape(n_dp, seg_count, width), DP, scatter_dimension=0, tiled=False
     )
 
     count = ids.shape[0]
     flat_ids = jnp.transpose(ids[:, 0, :]).reshape(-1)
     pooled = pool_rows(table[0], flat_ids, count)
-    x0f = lax.all_to_all(
-        pooled.reshape(n_mp, rows, emb), "mp", split_axis=0, concat_axis=0, tiled=True
-    )
+    x0f = a2a_mp(pooled.reshape(n_mp, rows, emb), nz, nx)
 
     member = members(counts[0], rows)
     cd3 = cross_down.reshape(n_mp, emb, rank)
@@ -150,23 +166,37 @@
         "cr,fdr->fcd", dz, cd3, preferred_element_type=f32
     )
     grads = dx0.astype(bf16)
-    returned = lax.all_to_all(grads, "mp", split_axis=0, concat_axis=0, tiled=True)
+    returned = a2a_mp(grads, nz, nx)
     return (score, returned.reshape(n_mp * rows, 1, emb))
 
 
+def split_mesh(mesh):
+    grid = mesh.devices
+    n_dp, n_mp = grid.shape
+    try:
+        nx = len({d.coords[0] for d in grid[0, :]})
+        nc = len({d.core_on_chip for d in grid[:, 0]})
+    except AttributeError:
+        nx, nc = 1, 1
+    if n_mp % nx or n_dp % nc:
+        nx, nc = 1, 1
+    return Mesh(grid.reshape(n_dp // nc, nc, n_mp // nx, nx), ("y", "c", "z", "x"))
+
+
 def solution(mesh):
+    mesh4 = split_mesh(mesh)
     in_specs = (
-        P("mp", None, None),
-        P("dp", "mp", None),
-        P(("dp", "mp"), None),
-        P(("dp", "mp")),
-        P(),
-        P("dp", None),
-        P(),
-        P(),
-        P(),
-        P("mp", None),
-        P(),
-    )
-    out_specs = (P(("dp", "mp")), P("dp", "mp", None))
-    return jax.shard_map(local, mesh=mesh, in_specs=in_specs, out_specs=out_specs, check_vma=False)
+        P(MP, None, None),
+        P(DP, MP, None),
+        P(DP + MP, None),
+        P(DP + MP),
+        P(),
+        P(DP, None),
+        P(),
+        P(),
+        P(),
+        P(MP, None),
+        P(),
+    )
+    out_specs = (P(DP + MP), P(DP, MP, None))
+    return jax.shard_map(local, mesh=mesh4, in_specs=in_specs, out_specs=out_specs, check_vma=False)

time: 224 us -> 284 us (1.27)
  blocking collectives: 95 us -> 149 us
  waiting for transfers between devices: 42.1 us -> 45.8 us
    all_to_all x2 -> x5, blocking collectives: 95 us -> 149 us  [the longest x1 53.5 us: a2a_mp(): v = lax.all_to_all(v, 'z', split_axis=0, concat_axis=0, tiled=True)]
    all_to_all x1, waiting for transfers between devices: 42.1 us -> 45.7 us  [a2a_mp(): v = lax.all_to_all(v, 'z', split_axis=0, concat_axis=0, tiled=True)]
  transfers between devices with their start and end apart: 3 -> 3, of which waited for: 1 -> 1; matrix products, arithmetic and copies ran while one was open for 9% -> 7% of each run, Pallas kernels for 11% -> 9%
where the time goes in v3:
time: 284 us; the launch traced here: 281 us
  blocking collectives  149 us (52%)
  waiting for transfers between devices  45.8 us (16%)
  matrix products  32.4 us (11%)
  Pallas kernels  25 us (9%)
  between operations  14.2 us (5%)
  local copies, waits for them, and re-layouts  9.47 us (3%)
  starting transfers between devices  4.56 us (2%)
    all_to_all x1, blocking collectives, a2a_mp(): v = lax.all_to_all(v, 'z', split_axis=0, concat_axis=0, tiled=True)  53.5 us
    all_to_all x2, blocking collectives, a2a_mp(): v = lax.all_to_all(v, 'x', split_axis=1, concat_axis=1, tiled=True)  51.1 us
    all_to_all x1, waiting for transfers between devices, a2a_mp(): v = lax.all_to_all(v, 'z', split_axis=0, concat_axis=0, tiled=True)  45.7 us
    all_to_all x1, blocking collectives, gather_mp(): v = lax.all_to_all(v, 'z', split_axis=0, concat_axis=0, tiled=True)  35.7 us
    pallas_call x1, Pallas kernels, pool_rows(): pl.pallas_call(pool_kernel, grid_spec=spec, out_shape=jax.ShapeDtypeStruc...  25 us
    dot_general x1, matrix products, local(): jnp.einsum('cr,fdr->fcd', dz, cd3, preferred_element_type=f32)  9.56 us
    all_to_all x1, blocking collectives, gather_mp(): v = lax.all_to_all(v, 'x', split_axis=0, concat_axis=0, tiled=True)  9.15 us
    dot_general x1, matrix products, local(): dx1 = jnp.einsum('ch,fdh->fcd', dact, w3, preferred_element_type=f32)  7.14 us
  transfers between devices with their start and end apart: 3, of which 1 were waited for; matrix products, arithmetic and copies ran while one was open for 7% of the time, Pallas kernels for 9%

profile of v3, /device:TPU:2, one launch (start us, length us, event | category | flops | bytes accessed | tf_op | source)
XLA Modules:
  0.0 281.3 jit_solution(7859036296354775748)
XLA Ops:
  7.2 0.9 constant_dynamic-slice_fusion
  8.2 9.1 %all_to_all.30 = bf16[4,128,128]{2,1,0:T(8,128)(2,1)S(1)} all-to-all(bf16[4,128,128]{2,1,0:T(8,128)(2,1)S(1)} %broadcast_in_dim.21), channel_id=1, replica_groups=mesh['y'=4,'c'=2,'z'=8,'x'=4] {'x'}, dimensions={0} | all-to-all | bytes 262144 | tf_op jit(solution)/shard_map/all_to_all | solution.py:91
  17.3 0.2 broadcast_in_dim.23
  17.5 35.7 %all_to_all.31 = bf16[8,4,128,128]{3,2,1,0:T(8,128)(2,1)} all-to-all(bf16[8,4,128,128]{3,2,1,0:T(8,128)(2,1)S(1)} %broadcast_in_dim.23), channel_id=1, replica_groups=mesh['y'=4,'c'=2,'z'=8,'x'=4] {'z'}, dimensions={0} | all-to-all | bytes 2097152 | tf_op jit(solution)/shard_map/all_to_all | solution.py:93
  53.2 0.6 copy.36
  53.9 25.0 %shard_map.122 = bf16[8192,128]{1,0:T(8,128)(2,1)} custom-call(s32[16384]{0:T(1024)} %bitcast.124, bf16[2048,128]{1,0:T(8,128)(2,1)} %bitcast.123), custom_call_target="tpu_custom_call" | custom-call | tf_op jit(solution)/shard_map/pallas_call | solution.py:44
  78.8 1.8 copy.27
  80.6 25.9 %all_to_all.32 = bf16[8,4,256,128]{3,2,0,1:T(8,128)(2,1)S(1)} all-to-all(bf16[8,4,256,128]{3,2,0,1:T(8,128)(2,1)S(1)} %copy.27), channel_id=1, replica_groups=mesh['y'=4,'c'=2,'z'=8,'x'=4] {'x'}, dimensions={1} | all-to-all | bytes 4194304 | tf_op jit(solution)/shard_map/all_to_all | solution.py:84
  106.5 1.5 copy.28
  108.0 4.5 %all-to-all-start.1 = ((bf16[8,4,256,128]{3,2,1,0:T(8,128)(2,1)}), bf16[8,4,256,128]{3,2,1,0:T(8,128)(2,1)}, u32[]{:S(2)}, u32[]{:S(2)}) async-start(bf16[8,4,256,128]{3,2,1,0:T(8,128)(2,1)} %copy.28), calls=%async_computation.1 | async-start | bytes 4194304 | tf_op jit(solution)/shard_map/all_to_all | solution.py:85
  112.7 0.8 dynamic_slice.7
  113.5 0.9 fusion.36
  114.9 45.7 %all-to-all-done.1 = bf16[8,4,256,128]{3,2,1,0:T(8,128)(2,1)} async-done(((bf16[8,4,256,128]{3,2,1,0:T(8,128)(2,1)}), bf16[8,4,256,128]{3,2,1,0:T(8,128)(2,1)}, u32[]{:S(2)}, u32[]{:S(2)}) %all-to-all-start.1) | async-done | bytes 2097184 | tf_op jit(solution)/shard_map/all_to_all | solution.py:85
  160.6 6.6 %fusion.8 = f32[256,32,128]{2,0,1:T(8,128)} fusion(bf16[32,256,128]{2,1,0:T(8,128)(2,1)} %bitcast.8, bf16[32,128,256]{2,1,0:T(8,128)(2,1)S(1)} %bitcast.117, bf16[256,4096]{1,0:T(8,128)(2,1)} %param.18), kind=kOutput, calls=%fused_computation.11 | convolution fusion | flops 1073807360 | bytes 10485760 | tf_op jit(solution)/shard_map/cr,rfd->fcd/dot_general | solution.py:151
  167.2 6.7 %fusion.18 = f32[256,1024]{1,0:T(8,128)S(1)} fusion(bf16[32,128,1024]{2,1,0:T(8,128)(2,1)} %bitcast.133, bf16[32,256,128]{2,1,0:T(8,128)(2,1)} %bitcast.8, f32[256,32,128]{2,0,1:T(8,128)} %fusion.8, f32[32,128]{1,0:T(8,128)S(1)} %bitcast.126, f32[1024]{0:T(1024)S(1)} %copy-done.7), kind=kOutput, calls=%fused_computation.20 | convolution fusion | flops 2152988672 | bytes 15749120 | tf_op jit(solution)/shard_map/fcd,fdh->ch/dot_general | solution.py:153
  173.9 1.1 fusion.47
  175.1 0.4 fusion.35
  175.5 0.3 copy-done.6
  175.8 7.1 %fusion.48 = f32[32,128,256]{1,2,0:T(8,128)} fusion(bf16[32,128,1024]{2,1,0:T(8,128)(2,1)} %bitcast.134, f32[256,1024]{1,0:T(8,128)S(1)} %fusion.18, f32[256]{0:T(256)S(1)} %maximum_divide_fusion, bf16[1,8,1024]{2,1,0:T(8,128)(2,1)S(1)} %copy-done.6, s32[8]{0:T(128)S(1)} %bitcast.132, s32[8]{0:T(128)S(1)} %fusion.65), kind=kOutput, calls=%fused_computation.38 | convolution fusion | flops 2154567680 | bytes 13648960 | tf_op jit(solution)/shard_map/ch,fdh->fcd/dot_general | solution.py:162
  182.9 9.6 %fusion.2 = bf16[32,256,128]{2,1,0:T(8,128)(2,1)} fusion(f32[32,128,256]{1,2,0:T(8,128)} %fusion.48, f32[256,32,128]{2,0,1:T(8,128)} %fusion.8, bf16[32,128,256]{2,1,0:T(8,128)(2,1)S(1)} %bitcast.118, f32[32,128]{1,0:T(8,128)S(1)} %bitcast.127, bf16[32,256,128]{2,1,0:T(8,128)(2,1)} %bitcast.8, bf16[256,4096]{1,0:T(8,128)(2,1)} %param.18), kind=kOutput, calls=%fused_computation.5 | convolution fusion | flops 1082195968 | bytes 16793600 | tf_op jit(solution)/shard_map/cr,fdr->fcd/dot_general | solution.py:165
  192.5 1.7 copy.32
  194.2 25.2 %all_to_all.33 = bf16[8,4,256,128]{3,2,0,1:T(8,128)(2,1)S(1)} all-to-all(bf16[8,4,256,128]{3,2,0,1:T(8,128)(2,1)S(1)} %copy.32), channel_id=1, replica_groups=mesh['y'=4,'c'=2,'z'=8,'x'=4] {'x'}, dimensions={1} | all-to-all | bytes 4194304 | tf_op jit(solution)/shard_map/all_to_all | solution.py:84
  219.6 53.5 %all_to_all.34 = bf16[8,4,256,128]{3,2,1,0:T(8,128)(2,1)S(1)} all-to-all(bf16[8,4,256,128]{3,2,1,0:T(8,128)(2,1)S(1)} %copy.33), channel_id=1, replica_groups=mesh['y'=4,'c'=2,'z'=8,'x'=4] {'z'}, dimensions={0} | all-to-all | bytes 4194304 | tf_op jit(solution)/shard_map/all_to_all | solution.py:85
  273.1 1.3 copy.54
  (35 shorter events, 1.0 us)
Async XLA Ops:
  7.2 153.5 %copy-start = (bf16[4096,256]{1,0:T(8,128)(2,1)S(1)}, bf16[4096,256]{1,0:T(8,128)(2,1)}, u32[]{:S(2)}) copy-start(bf16[4096,256]{1,0:T(8,128)(2,1)} %param.17) | copy-start | bytes 6291460
  7.2 160.0 %all-gather.2.cloned.1.call-start = ((), (), s32[]{:S(2)}) async-start(), calls=%async_computation.7 | async-start | bytes 9437184 | tf_op jit(solution)/shard_map/all_gather | solution.py:126
  17.3 35.9 %copy-start.2 = (s32[8192,1,2]{0,2,1:T(2,128)S(1)}, s32[8192,1,2]{0,2,1:T(2,128)}, u32[]{:S(2)}) copy-start(s32[8192,1,2]{0,2,1:T(2,128)} %param.12) | copy-start | bytes 196612
  108.0 5.5 %copy-start.1 = (bf16[256,1024]{1,0:T(8,128)(2,1)S(1)}, bf16[256,1024]{1,0:T(8,128)(2,1)}, u32[]{:S(2)}) copy-start(bf16[256,1024]{1,0:T(8,128)(2,1)} %param.16) | copy-start | bytes 1572868
  108.0 6.4 %copy-start.8 = (s32[1,8]{1,0:T(1,128)S(1)}, s32[1,8]{1,0:T(1,128)}, u32[]{:S(2)}) copy-start(s32[1,8]{1,0:T(1,128)} %param.13) | copy-start | bytes 100
  108.0 6.6 %copy-start.4 = (s32[256]{0:T(256)S(1)}, s32[256]{0:T(256)}, u32[]{:S(2)}) copy-start(s32[256]{0:T(256)} %param.14) | copy-start | bytes 3076
  108.0 52.6 %all-to-all-start.1 = ((bf16[8,4,256,128]{3,2,1,0:T(8,128)(2,1)}), bf16[8,4,256,128]{3,2,1,0:T(8,128)(2,1)}, u32[]{:S(2)}, u32[]{:S(2)}) async-start(bf16[8,4,256,128]{3,2,1,0:T(8,128)(2,1)} %copy.28), calls=%async_computation.1 | async-start | bytes 4194304 | tf_op jit(solution)/shard_map/all_to_all | solution.py:85
  112.5 61.4 %reduce-scatter.2.cloned.1.call-start = ((), (), s32[]{:S(2)}) async-start(), calls=%async_computation.8 | async-start | bytes 147456 | tf_op jit(solution)/shard_map/reduce_scatter | solution.py:137
  160.6 6.6 %copy-start.3 = (f32[4096]{0:T(1024)S(1)}, f32[4096]{0:T(1024)}, u32[]{:S(2)}) copy-start(f32[4096]{0:T(1024)} %param.19) | copy-start | bytes 49156
  160.6 6.6 %copy-start.7 = (f32[1024]{0:T(1024)S(1)}, f32[1024]{0:T(1024)}, u32[]{:S(2)}) copy-start(f32[1024]{0:T(1024)} %param.21) | copy-start | bytes 12292
  175.1 0.7 copy-start.6
  175.1 7.8 %copy-start.5 = (f32[256]{0:T(256)}, f32[256]{0:T(256)S(1)}, u32[]{:S(2)}) copy-start(f32[256]{0:T(256)S(1)} %broadcast_multiply_fusion) | copy-start | bytes 3076
Sparse Core Ops, SparseCore 0:
  53.4 51.3 all-gather.1
  115.8 34.5 reduce-scatter.1

commit v4 on v3

--- a/solution.py
+++ b/solution.py
@@ -122,9 +122,8 @@
 
     piece = tower_weight.shape[1] // n_dp
     w_piece = lax.dynamic_slice_in_dim(tower_weight, d_idx * piece, piece, axis=1)
-    w_cols = gather_mp(w_piece, nz, nx).reshape(n_mp * w_piece.shape[0], piece)
-    w_all = lax.all_gather(w_cols, DP, axis=1, tiled=True)
-    w3 = w_all.reshape(n_mp, emb, width)
+    w_x = lax.all_gather(w_piece, "x", axis=0, tiled=True)
+    w_cols = lax.all_gather(w_x, "z", axis=0, tiled=True)
 
     held = user_codes.shape[0]
     home_local = lax.dynamic_slice_in_dim(request_home, d_idx * held, held)
@@ -134,14 +133,16 @@
     ).reshape(-1)
     pick = (home_local[None, :] == wanted[:, None]).astype(bf16)
     mine = jnp.dot(pick, user_codes, preferred_element_type=f32).astype(bf16)
-    user_seg = lax.psum_scatter(
-        mine.reshape(n_dp, seg_count, width), DP, scatter_dimension=0, tiled=False
-    )
+    sent = lax.all_to_all(mine.reshape(n_dp, seg_count, width), DP, 0, 0, tiled=True)
+    user_seg = jnp.sum(sent.astype(f32), axis=0).astype(bf16)
 
     count = ids.shape[0]
     flat_ids = jnp.transpose(ids[:, 0, :]).reshape(-1)
     pooled = pool_rows(table[0], flat_ids, count)
-    x0f = a2a_mp(pooled.reshape(n_mp, rows, emb), nz, nx)
+    w_cols, pooled = lax.optimization_barrier((w_cols, pooled))
+    w_all = lax.all_gather(w_cols, DP, axis=1, tiled=True)
+    w3 = w_all.reshape(n_mp, emb, width)
+    x0f = lax.all_to_all(pooled.reshape(n_mp, rows, emb), MP, 0, 0, tiled=True)
 
     member = members(counts[0], rows)
     cd3 = cross_down.reshape(n_mp, emb, rank)
@@ -166,7 +167,7 @@
         "cr,fdr->fcd", dz, cd3, preferred_element_type=f32
     )
     grads = dx0.astype(bf16)
-    returned = a2a_mp(grads, nz, nx)
+    returned = lax.all_to_all(grads, MP, 0, 0, tiled=True)
     return (score, returned.reshape(n_mp * rows, 1, emb))
 
 

time: 284 us -> 226 us (0.80)
  blocking collectives: 149 us -> 79.2 us
  waiting for transfers between devices: 45.8 us -> 59.2 us
  starting transfers between devices: 4.56 us -> 7.51 us
    all_to_all x5 -> x2, blocking collectives: 149 us -> 66.3 us  [the longest x1 56.1 us: local(): returned = lax.all_to_all(grads, MP, 0, 0, tiled=True)]
    all_gather x0 -> x1, waiting for transfers between devices: none -> 14.7 us  [local(): w_cols = lax.all_gather(w_x, 'z', axis=0, tiled=True)]
    all_gather x0 -> x1, blocking collectives: none -> 12.9 us  [local(): w_x = lax.all_gather(w_piece, 'x', axis=0, tiled=True)]
    all_to_all x1, starting transfers between devices: 4.49 us -> 7.43 us  [local(): x0f = lax.all_to_all(pooled.reshape(n_mp, rows, emb), MP, 0, 0, tiled=True)]
  transfers between devices with their start and end apart: 3 -> 3, of which waited for: 1 -> 2; matrix products, arithmetic and copies ran while one was open for 7% -> 6% of each run, Pallas kernels for 9% -> 11%
where the time goes in v4:
time: 226 us; the launch traced here: 225 us
  blocking collectives  79.2 us (35%)
  waiting for transfers between devices  59.2 us (26%)
  matrix products  31 us (14%)
  Pallas kernels  25 us (11%)
  between operations  14.1 us (6%)
  local copies, waits for them, and re-layouts  8.67 us (4%)
  starting transfers between devices  7.51 us (3%)
    all_to_all x1, blocking collectives, local(): returned = lax.all_to_all(grads, MP, 0, 0, tiled=True)  56.1 us
    all_to_all x1, waiting for transfers between devices, local(): x0f = lax.all_to_all(pooled.reshape(n_mp, rows, emb), MP, 0, 0, tiled=True)  44.5 us
    pallas_call x1, Pallas kernels, pool_rows(): pl.pallas_call(pool_kernel, grid_spec=spec, out_shape=jax.ShapeDtypeStruc...  25 us
    all_gather x1, waiting for transfers between devices, local(): w_cols = lax.all_gather(w_x, 'z', axis=0, tiled=True)  14.7 us
    all_gather x1, blocking collectives, local(): w_x = lax.all_gather(w_piece, 'x', axis=0, tiled=True)  12.9 us
    all_to_all x1, blocking collectives, local(): lax.all_to_all(mine.reshape(n_dp, seg_count, width), DP, 0, 0, tiled=True)  10.2 us
    dot_general x1, matrix products, local(): jnp.einsum('cr,fdr->fcd', dz, cd3, preferred_element_type=f32)  9.52 us
    all_to_all x1, starting transfers between devices, local(): x0f = lax.all_to_all(pooled.reshape(n_mp, rows, emb), MP, 0, 0, tiled=True)  7.43 us
  transfers between devices with their start and end apart: 3, of which 2 were waited for; matrix products, arithmetic and copies ran while one was open for 6% of the time, Pallas kernels for 11%

profile of v4, /device:TPU:2, one launch (start us, length us, event | category | flops | bytes accessed | tf_op | source)
XLA Modules:
  0.0 225.3 jit_solution(8551056310474003348)
XLA Ops:
  7.2 0.9 constant_dynamic-slice_fusion
  8.1 12.9 %all_gather.9 = bf16[512,128]{1,0:T(8,128)(2,1)} all-gather(bf16[128,128]{1,0:T(8,128)(2,1)S(1)} %constant_dynamic-slice_fusion), channel_id=1, replica_groups=mesh['y'=4,'c'=2,'z'=8,'x'=4] {'x'}, dimensions={0}, use_global_device_ids=true | all-gather | bytes 163840 | tf_op jit(solution)/shard_map/all_gather | solution.py:125
  21.1 1.5 copy.20
  22.6 25.0 %shard_map.122 = bf16[8192,128]{1,0:T(8,128)(2,1)} custom-call(s32[16384]{0:T(1024)} %bitcast.99, bf16[2048,128]{1,0:T(8,128)(2,1)} %bitcast.98), custom_call_target="tpu_custom_call" | custom-call | tf_op jit(solution)/shard_map/pallas_call | solution.py:44
  47.6 14.7 %all-gather.3.cloned.1.call-done = bf16[4096,128]{1,0:T(8,128)(2,1)} async-done(((bf16[512,128]{1,0:T(8,128)(2,1)}), bf16[4096,128]{1,0:T(8,128)(2,1)}) %all-gather.3.cloned.1.call-update) | async-done | bytes 1048592 | tf_op jit(solution)/shard_map/all_gather | solution.py:126
  62.3 0.1 iota_add_fusion
  62.4 0.1 add.106
  62.5 0.8 dynamic_slice.7
  63.3 0.2 fusion.30
  63.5 10.2 %all_to_all.15 = bf16[8,8,1024]{2,1,0:T(8,128)(2,1)S(1)} all-to-all(bf16[8,8,1024]{2,1,0:T(8,128)(2,1)S(1)} %fusion.30), channel_id=1, replica_groups=mesh['y'=4,'c'=2,'z'=8,'x'=4] {'y','c'}, dimensions={0} | all-to-all | bytes 262144 | tf_op jit(solution)/shard_map/all_to_all | solution.py:136
  73.7 7.4 %all-to-all-start = ((bf16[32,256,128]{2,1,0:T(8,128)(2,1)}), bf16[32,256,128]{2,1,0:T(8,128)(2,1)}, u32[]{:S(2)}, u32[]{:S(2)}) async-start(bf16[32,256,128]{2,1,0:T(8,128)(2,1)} %bitcast.96), calls=%async_computation | async-start | bytes 4194304 | tf_op jit(solution)/shard_map/all_to_all | solution.py:145
  81.1 0.2 reduce-window.4
  81.3 4.1 %copy.19 = bf16[256,4096]{0,1:T(8,128)(2,1)} copy(bf16[256,4096]{1,0:T(8,128)(2,1)} %param.18) | data formatting | bytes 4194304 | tf_op jit(solution)/shard_map/reshape | solution.py:149
  85.4 0.2 select_reduce_fusion.1
  85.6 0.1 select_reduce_fusion
  85.8 44.5 %all-to-all-done = bf16[32,256,128]{2,1,0:T(8,128)(2,1)} async-done(((bf16[32,256,128]{2,1,0:T(8,128)(2,1)}), bf16[32,256,128]{2,1,0:T(8,128)(2,1)}, u32[]{:S(2)}, u32[]{:S(2)}) %all-to-all-start) | async-done | bytes 2097184 | tf_op jit(solution)/shard_map/all_to_all | solution.py:145
  130.2 6.6 %fusion.35 = f32[256,32,128]{2,0,1:T(8,128)} fusion(bf16[256,32,128]{0,2,1:T(8,128)(2,1)} %bitcast.94, bf16[32,256,128]{2,1,0:T(8,128)(2,1)} %all-to-all-done, bf16[32,128,256]{2,1,0:T(8,128)(2,1)S(1)} %bitcast.92), kind=kOutput, calls=%fused_computation.31 | convolution fusion | flops 1073807360 | bytes 10485760 | tf_op jit(solution)/shard_map/cr,rfd->fcd/dot_general | solution.py:152
  136.8 6.7 %fusion.13 = f32[256,1024]{1,0:T(8,128)S(1)} fusion(bf16[32,128,1024]{2,1,0:T(8,128)(2,1)} %bitcast.108, bf16[32,256,128]{2,1,0:T(8,128)(2,1)} %all-to-all-done, f32[256,32,128]{2,0,1:T(8,128)} %fusion.35, f32[32,128]{1,0:T(8,128)S(1)} %bitcast.101, f32[1024]{0:T(1024)S(1)} %copy-done.5), kind=kOutput, calls=%fused_computation.15 | convolution fusion | flops 2152988672 | bytes 15749120 | tf_op jit(solution)/shard_map/fcd,fdh->ch/dot_general | solution.py:154
  143.5 0.4 fusion.34
  143.9 0.4 fusion.26
  144.4 7.1 %fusion.36 = f32[32,128,256]{1,2,0:T(8,128)} fusion(bf16[32,128,1024]{2,1,0:T(8,128)(2,1)} %bitcast.109, bf16[8,1024]{1,0:T(8,128)(2,1)S(1)} %reduce_sum.48, f32[256,1024]{1,0:T(8,128)S(1)} %fusion.13, f32[256]{0:T(256)S(1)} %maximum_divide_fusion, s32[8]{0:T(128)S(1)} %bitcast.107, s32[8]{0:T(128)S(1)} %fusion.50), kind=kOutput, calls=%fused_computation.34 | convolution fusion | flops 2154567680 | bytes 13648960 | tf_op jit(solution)/shard_map/ch,fdh->fcd/dot_general | solution.py:163
  151.5 9.5 %fusion.2 = bf16[32,256,128]{2,1,0:T(8,128)(2,1)} fusion(f32[32,128,256]{1,2,0:T(8,128)} %fusion.36, f32[256,32,128]{2,0,1:T(8,128)} %fusion.35, bf16[32,128,256]{2,1,0:T(8,128)(2,1)S(1)} %bitcast.93, f32[32,128]{1,0:T(8,128)S(1)} %bitcast.102, bf16[256,32,128]{0,2,1:T(8,128)(2,1)} %bitcast.95, bf16[32,256,128]{2,1,0:T(8,128)(2,1)} %all-to-all-done), kind=kOutput, calls=%fused_computation.5 | convolution fusion | flops 1082195968 | bytes 16793600 | tf_op jit(solution)/shard_map/cr,fdr->fcd/dot_general | solution.py:166
  161.0 56.1 %all_to_all.16 = bf16[32,256,128]{2,1,0:T(8,128)(2,1)S(1)} all-to-all(bf16[32,256,128]{2,1,0:T(8,128)(2,1)} %fusion.2), channel_id=1, replica_groups=mesh['y'=4,'c'=2,'z'=8,'x'=4] {'z','x'}, dimensions={0} | all-to-all | bytes 4194304 | tf_op jit(solution)/shard_map/all_to_all | solution.py:170
  217.1 1.3 copy.22
  (25 shorter events, 0.2 us)
Async XLA Ops:
  7.2 123.1 %copy-start = (bf16[4096,256]{1,0:T(8,128)(2,1)S(1)}, bf16[4096,256]{1,0:T(8,128)(2,1)}, u32[]{:S(2)}) copy-start(bf16[4096,256]{1,0:T(8,128)(2,1)} %param.17) | copy-start | bytes 6291460
  7.2 55.1 %all-gather.3.cloned.1.call-start = ((), (), s32[]{:S(2)}) async-start(), calls=%async_computation.3 | async-start | bytes 1179648 | tf_op jit(solution)/shard_map/all_gather | solution.py:126
  8.1 55.1 %copy-start.1 = (bf16[256,1024]{1,0:T(8,128)(2,1)S(1)}, bf16[256,1024]{1,0:T(8,128)(2,1)}, u32[]{:S(2)}) copy-start(bf16[256,1024]{1,0:T(8,128)(2,1)} %param.16) | copy-start | bytes 1572868
  21.1 115.7 %all-gather.5.cloned.1.call-start = ((), (), s32[]{:S(2)}) async-start(), calls=%async_computation.4 | async-start | bytes 9437184 | tf_op jit(solution)/shard_map/all_gather | solution.py:143
  73.7 7.4 %copy-start.6 = (s32[1,8]{1,0:T(1,128)S(1)}, s32[1,8]{1,0:T(1,128)}, u32[]{:S(2)}) copy-start(s32[1,8]{1,0:T(1,128)} %param.13) | copy-start | bytes 100
  73.7 56.5 %all-to-all-start = ((bf16[32,256,128]{2,1,0:T(8,128)(2,1)}), bf16[32,256,128]{2,1,0:T(8,128)(2,1)}, u32[]{:S(2)}, u32[]{:S(2)}) async-start(bf16[32,256,128]{2,1,0:T(8,128)(2,1)} %bitcast.96), calls=%async_computation | async-start | bytes 4194304 | tf_op jit(solution)/shard_map/all_to_all | solution.py:145
  81.3 4.1 %copy-start.3 = (s32[256]{0:T(256)S(1)}, s32[256]{0:T(256)}, u32[]{:S(2)}) copy-start(s32[256]{0:T(256)} %param.14) | copy-start | bytes 3076
  130.2 6.6 %copy-start.2 = (f32[4096]{0:T(1024)S(1)}, f32[4096]{0:T(1024)}, u32[]{:S(2)}) copy-start(f32[4096]{0:T(1024)} %param.19) | copy-start | bytes 49156
  130.2 6.6 %copy-start.5 = (f32[1024]{0:T(1024)S(1)}, f32[1024]{0:T(1024)}, u32[]{:S(2)}) copy-start(f32[1024]{0:T(1024)} %param.21) | copy-start | bytes 12292
  143.9 7.6 %copy-start.4 = (f32[256]{0:T(256)}, f32[256]{0:T(256)S(1)}, u32[]{:S(2)}) copy-start(f32[256]{0:T(256)S(1)} %broadcast_multiply_fusion) | copy-start | bytes 3076
Sparse Core Ops, SparseCore 0:
  21.2 41.0 all-gather.2
  64.1 54.3 all-gather.4

commit v5 on v4

--- a/solution.py
+++ b/solution.py
@@ -122,8 +122,9 @@
 
     piece = tower_weight.shape[1] // n_dp
     w_piece = lax.dynamic_slice_in_dim(tower_weight, d_idx * piece, piece, axis=1)
-    w_x = lax.all_gather(w_piece, "x", axis=0, tiled=True)
-    w_cols = lax.all_gather(w_x, "z", axis=0, tiled=True)
+    w_grid = lax.all_gather(w_piece, MP + DP, axis=0, tiled=False)
+    w_grid = w_grid.reshape((n_mp, n_dp) + w_piece.shape)
+    w3 = jnp.transpose(w_grid, (0, 2, 1, 3)).reshape(n_mp, emb, width)
 
     held = user_codes.shape[0]
     home_local = lax.dynamic_slice_in_dim(request_home, d_idx * held, held)
@@ -139,9 +140,6 @@
     count = ids.shape[0]
     flat_ids = jnp.transpose(ids[:, 0, :]).reshape(-1)
     pooled = pool_rows(table[0], flat_ids, count)
-    w_cols, pooled = lax.optimization_barrier((w_cols, pooled))
-    w_all = lax.all_gather(w_cols, DP, axis=1, tiled=True)
-    w3 = w_all.reshape(n_mp, emb, width)
     x0f = lax.all_to_all(pooled.reshape(n_mp, rows, emb), MP, 0, 0, tiled=True)
 
     member = members(counts[0], rows)

time: 226 us -> 268 us (1.19)
  local copies, waits for them, and re-layouts: 8.67 us -> 45.7 us
  blocking collectives: 79.2 us -> 57.8 us
  waiting for transfers between devices: 59.2 us -> 74.3 us
  starting transfers between devices: 7.51 us -> 16.3 us
    reshape x0 -> x2, local copies, waits for them, and re-layouts: none -> 36.5 us  [the longest x1 23.1 us: local(): w_grid = w_grid.reshape((n_mp, n_dp) + w_piece.shape)]
    all_gather x1 -> x0, blocking collectives: 12.9 us -> none  [local(): w_x = lax.all_gather(w_piece, 'x', axis=0, tiled=True)]
    all_gather x2 -> x1, waiting for transfers between devices: 14.7 us -> 25.6 us  [local(): w_grid = lax.all_gather(w_piece, MP + DP, axis=0, tiled=False)]
    all_to_all x1 -> x0, blocking collectives: 10.2 us -> none  [local(): lax.all_to_all(mine.reshape(n_dp, seg_count, width), DP, 0, 0, tiled=True)]
    all_to_all x0 -> x1, starting transfers between devices: none -> 4.47 us  [local(): lax.all_to_all(mine.reshape(n_dp, seg_count, width), DP, 0, 0, tiled=True)]
    all_to_all x1, starting transfers between devices: 7.43 us -> 11.8 us  [local(): x0f = lax.all_to_all(pooled.reshape(n_mp, rows, emb), MP, 0, 0, tiled=True)]
    all_to_all x1, waiting for transfers between devices: 44.5 us -> 48.6 us  [local(): x0f = lax.all_to_all(pooled.reshape(n_mp, rows, emb), MP, 0, 0, tiled=True)]
  transfers between devices with their start and end apart: 3 -> 3, of which waited for: 2 -> 2; matrix products, arithmetic and copies ran while one was open for 6% -> 6% of each run, Pallas kernels for 11% -> 9%
where the time goes in v5:
time: 268 us; the launch traced here: 267 us
  waiting for transfers between devices  74.3 us (28%)
  blocking collectives  57.8 us (22%)
  local copies, waits for them, and re-layouts  45.7 us (17%)
  matrix products  33.1 us (12%)
  Pallas kernels  25 us (9%)
  starting transfers between devices  16.3 us (6%)
  between operations  14.1 us (5%)
    all_to_all x1, blocking collectives, local(): returned = lax.all_to_all(grads, MP, 0, 0, tiled=True)  57.8 us
    all_to_all x1, waiting for transfers between devices, local(): x0f = lax.all_to_all(pooled.reshape(n_mp, rows, emb), MP, 0, 0, tiled=True)  48.6 us
    all_gather x1, waiting for transfers between devices, local(): w_grid = lax.all_gather(w_piece, MP + DP, axis=0, tiled=False)  25.6 us
    pallas_call x1, Pallas kernels, pool_rows(): pl.pallas_call(pool_kernel, grid_spec=spec, out_shape=jax.ShapeDtypeStruc...  25 us
    reshape x1, local copies, waits for them, and re-layouts, local(): w_grid = w_grid.reshape((n_mp, n_dp) + w_piece.shape)  23.1 us
    reshape x1, local copies, waits for them, and re-layouts, local(): w3 = jnp.transpose(w_grid, (0, 2, 1, 3)).reshape(n_mp, emb, width)  13.3 us
    all_to_all x1, starting transfers between devices, local(): x0f = lax.all_to_all(pooled.reshape(n_mp, rows, emb), MP, 0, 0, tiled=True)  11.8 us
    dot_general x1, matrix products, local(): jnp.einsum('cr,fdr->fcd', dz, cd3, preferred_element_type=f32)  9.52 us
  transfers between devices with their start and end apart: 3, of which 2 were waited for; matrix products, arithmetic and copies ran while one was open for 6% of the time, Pallas kernels for 9%

profile of v5, /device:TPU:2, one launch (start us, length us, event | category | flops | bytes accessed | tf_op | source)
XLA Modules:
  0.0 266.9 jit_solution(5501704676183630341)
XLA Ops:
  7.2 1.5 constant_dynamic-slice_fusion
  8.8 0.1 add.106
  8.9 0.8 dynamic_slice.7
  9.7 1.9 fusion.30
  11.6 4.5 %all-to-all-start.1 = ((bf16[8,8,1024]{2,1,0:T(8,128)(2,1)}), bf16[8,8,1024]{2,1,0:T(8,128)(2,1)S(1)}, u32[]{:S(2)}, u32[]{:S(2)}) async-start(bf16[8,8,1024]{2,1,0:T(8,128)(2,1)} %fusion.30), calls=%async_computation.1 | async-start | bytes 262144 | tf_op jit(solution)/shard_map/all_to_all | solution.py:137
  16.1 1.5 copy.22
  17.6 25.0 %shard_map.122 = bf16[8192,128]{1,0:T(8,128)(2,1)} custom-call(s32[16384]{0:T(1024)} %bitcast.106, bf16[2048,128]{1,0:T(8,128)(2,1)} %bitcast.105), custom_call_target="tpu_custom_call" | custom-call | tf_op jit(solution)/shard_map/pallas_call | solution.py:44
  42.5 11.8 %all-to-all-start = ((bf16[32,256,128]{2,1,0:T(8,128)(2,1)}), bf16[32,256,128]{2,1,0:T(8,128)(2,1)}, u32[]{:S(2)}, u32[]{:S(2)}) async-start(bf16[32,256,128]{2,1,0:T(8,128)(2,1)} %bitcast.103), calls=%async_computation | async-start | bytes 4194304 | tf_op jit(solution)/shard_map/all_to_all | solution.py:143
  54.4 0.2 reduce-window.4
  54.5 4.1 %copy.21 = bf16[256,4096]{0,1:T(8,128)(2,1)} copy(bf16[256,4096]{1,0:T(8,128)(2,1)} %param.18) | data formatting | bytes 4194304 | tf_op jit(solution)/shard_map/reshape | solution.py:147
  58.6 0.2 select_reduce_fusion.1
  58.8 0.1 select_reduce_fusion
  58.9 48.6 %all-to-all-done = bf16[32,256,128]{2,1,0:T(8,128)(2,1)} async-done(((bf16[32,256,128]{2,1,0:T(8,128)(2,1)}), bf16[32,256,128]{2,1,0:T(8,128)(2,1)}, u32[]{:S(2)}, u32[]{:S(2)}) %all-to-all-start) | async-done | bytes 2097184 | tf_op jit(solution)/shard_map/all_to_all | solution.py:143
  107.6 7.1 %fusion.35 = f32[256,32,128]{2,0,1:T(8,128)} fusion(bf16[256,32,128]{0,2,1:T(8,128)(2,1)} %bitcast.100, bf16[32,256,128]{2,1,0:T(8,128)(2,1)} %all-to-all-done, bf16[32,128,256]{2,1,0:T(8,128)(2,1)S(1)} %bitcast.97), kind=kOutput, calls=%fused_computation.32 | convolution fusion | flops 1073807360 | bytes 10485760 | tf_op jit(solution)/shard_map/cr,rfd->fcd/dot_general | solution.py:150
  114.7 25.6 %all-gather.3.cloned.1.call-done = bf16[32768,128]{1,0:T(8,128)(2,1)} async-done(((bf16[128,128]{1,0:T(8,128)(2,1)}), bf16[32768,128]{1,0:T(8,128)(2,1)}) %all-gather.3.cloned.1.call-update) | async-done | bytes 8388624 | tf_op jit(solution)/shard_map/all_gather | solution.py:125
  140.3 23.1 %copy.24 = bf16[32,8,128,128]{3,1,2,0:T(8,128)(2,1)} copy(bf16[32,8,128,128]{3,2,1,0:T(8,128)(2,1)} %bitcast.102) | data formatting | bytes 16777216 | tf_op jit(solution)/shard_map/reshape | solution.py:126
  163.4 13.3 %reshape.89 = bf16[32,128,1024]{2,1,0:T(8,128)(2,1)} reshape(bf16[32,128,8,128]{3,2,1,0:T(8,128)(2,1)} %bitcast.99) | data formatting | bytes 16777216 | tf_op jit(solution)/shard_map/reshape | solution.py:127
  176.7 6.7 %fusion.13 = f32[256,1024]{1,0:T(8,128)S(1)} fusion(bf16[32,128,1024]{2,1,0:T(8,128)(2,1)} %reshape.89, bf16[32,256,128]{2,1,0:T(8,128)(2,1)} %all-to-all-done, f32[256,32,128]{2,0,1:T(8,128)} %fusion.35, f32[32,128]{1,0:T(8,128)S(1)} %bitcast.108, f32[1024]{0:T(1024)S(1)} %copy-done.4), kind=kOutput, calls=%fused_computation.16 | convolution fusion | flops 2152988672 | bytes 15749120 | tf_op jit(solution)/shard_map/fcd,fdh->ch/dot_general | solution.py:152
  183.4 0.4 fusion.34
  183.9 0.4 fusion.26
  184.3 7.1 %fusion.36 = f32[32,128,256]{1,2,0:T(8,128)} fusion(bf16[32,128,1024]{2,1,0:T(8,128)(2,1)} %reshape.89, bf16[8,1024]{1,0:T(8,128)(2,1)S(1)} %reduce_sum.48, f32[256,1024]{1,0:T(8,128)S(1)} %fusion.13, f32[256]{0:T(256)S(1)} %maximum_divide_fusion, s32[8]{0:T(128)S(1)} %bitcast.114, s32[8]{0:T(128)S(1)} %fusion.50), kind=kOutput, calls=%fused_computation.35 | convolution fusion | flops 2154567680 | bytes 13648960 | tf_op jit(solution)/shard_map/ch,fdh->fcd/dot_general | solution.py:161
  191.4 9.5 %fusion.2 = bf16[32,256,128]{2,1,0:T(8,128)(2,1)} fusion(f32[32,128,256]{1,2,0:T(8,128)} %fusion.36, f32[256,32,128]{2,0,1:T(8,128)} %fusion.35, bf16[32,128,256]{2,1,0:T(8,128)(2,1)S(1)} %bitcast.98, f32[32,128]{1,0:T(8,128)S(1)} %bitcast.109, bf16[256,32,128]{0,2,1:T(8,128)(2,1)} %bitcast.101, bf16[32,256,128]{2,1,0:T(8,128)(2,1)} %all-to-all-done), kind=kOutput, calls=%fused_computation.6 | convolution fusion | flops 1082195968 | bytes 16793600 | tf_op jit(solution)/shard_map/cr,fdr->fcd/dot_general | solution.py:164
  200.9 57.8 %all_to_all.15 = bf16[32,256,128]{2,1,0:T(8,128)(2,1)S(1)} all-to-all(bf16[32,256,128]{2,1,0:T(8,128)(2,1)} %fusion.2), channel_id=1, replica_groups=mesh['y'=4,'c'=2,'z'=8,'x'=4] {'z','x'}, dimensions={0} | all-to-all | bytes 4194304 | tf_op jit(solution)/shard_map/all_to_all | solution.py:168
  258.7 1.3 copy.26
  (22 shorter events, 0.2 us)
Async XLA Ops:
  7.2 100.4 %copy-start = (bf16[4096,256]{1,0:T(8,128)(2,1)S(1)}, bf16[4096,256]{1,0:T(8,128)(2,1)}, u32[]{:S(2)}) copy-start(bf16[4096,256]{1,0:T(8,128)(2,1)} %param.17) | copy-start | bytes 6291460
  7.2 133.1 %all-gather.3.cloned.1.call-start = ((), (), s32[]{:S(2)}) async-start(), calls=%async_computation.3 | async-start | bytes 8421376 | tf_op jit(solution)/shard_map/all_gather | solution.py:125
  11.6 30.9 %all-to-all-start.1 = ((bf16[8,8,1024]{2,1,0:T(8,128)(2,1)}), bf16[8,8,1024]{2,1,0:T(8,128)(2,1)S(1)}, u32[]{:S(2)}, u32[]{:S(2)}) async-start(bf16[8,8,1024]{2,1,0:T(8,128)(2,1)} %fusion.30), calls=%async_computation.1 | async-start | bytes 262144 | tf_op jit(solution)/shard_map/all_to_all | solution.py:137
  42.5 11.8 %copy-start.5 = (s32[1,8]{1,0:T(1,128)S(1)}, s32[1,8]{1,0:T(1,128)}, u32[]{:S(2)}) copy-start(s32[1,8]{1,0:T(1,128)} %param.13) | copy-start | bytes 100
  42.5 65.1 %all-to-all-start = ((bf16[32,256,128]{2,1,0:T(8,128)(2,1)}), bf16[32,256,128]{2,1,0:T(8,128)(2,1)}, u32[]{:S(2)}, u32[]{:S(2)}) async-start(bf16[32,256,128]{2,1,0:T(8,128)(2,1)} %bitcast.103), calls=%async_computation | async-start | bytes 4194304 | tf_op jit(solution)/shard_map/all_to_all | solution.py:143
  54.5 4.1 %copy-start.2 = (s32[256]{0:T(256)S(1)}, s32[256]{0:T(256)}, u32[]{:S(2)}) copy-start(s32[256]{0:T(256)} %param.14) | copy-start | bytes 3076
  163.4 13.3 %copy-start.1 = (f32[4096]{0:T(1024)S(1)}, f32[4096]{0:T(1024)}, u32[]{:S(2)}) copy-start(f32[4096]{0:T(1024)} %param.19) | copy-start | bytes 49156
  163.4 13.3 %copy-start.4 = (f32[1024]{0:T(1024)S(1)}, f32[1024]{0:T(1024)}, u32[]{:S(2)}) copy-start(f32[1024]{0:T(1024)} %param.21) | copy-start | bytes 12292
  183.8 7.5 %copy-start.3 = (f32[256]{0:T(256)}, f32[256]{0:T(256)S(1)}, u32[]{:S(2)}) copy-start(f32[256]{0:T(256)S(1)} %broadcast_multiply_fusion) | copy-start | bytes 3076
Sparse Core Ops, SparseCore 0:
  11.7 128.5 all-gather.2

commit v6 on v4

--- a/solution.py
+++ b/solution.py
@@ -78,22 +78,6 @@
 MP = ("z", "x")
 
 
-def a2a_mp(v, nz, nx):
-    shape = v.shape
-    v = v.reshape((nz, nx) + shape[1:])
-    v = lax.all_to_all(v, "x", split_axis=1, concat_axis=1, tiled=True)
-    v = lax.all_to_all(v, "z", split_axis=0, concat_axis=0, tiled=True)
-    return v.reshape(shape)
-
-
-def gather_mp(v, nz, nx):
-    v = jnp.broadcast_to(v[None], (nx,) + v.shape)
-    v = lax.all_to_all(v, "x", split_axis=0, concat_axis=0, tiled=True)
-    v = jnp.broadcast_to(v[None], (nz,) + v.shape)
-    v = lax.all_to_all(v, "z", split_axis=0, concat_axis=0, tiled=True)
-    return v.reshape((nz * nx,) + v.shape[2:])
-
-
 def local(
     table,
     ids,
@@ -122,8 +106,9 @@
 
     piece = tower_weight.shape[1] // n_dp
     w_piece = lax.dynamic_slice_in_dim(tower_weight, d_idx * piece, piece, axis=1)
-    w_x = lax.all_gather(w_piece, "x", axis=0, tiled=True)
-    w_cols = lax.all_gather(w_x, "z", axis=0, tiled=True)
+    w_cols = lax.all_to_all(
+        jnp.broadcast_to(w_piece[None], (n_mp,) + w_piece.shape), MP, 0, 0, tiled=True
+    ).reshape(n_mp * w_piece.shape[0], piece)
 
     held = user_codes.shape[0]
     home_local = lax.dynamic_slice_in_dim(request_home, d_idx * held, held)
@@ -133,8 +118,9 @@
     ).reshape(-1)
     pick = (home_local[None, :] == wanted[:, None]).astype(bf16)
     mine = jnp.dot(pick, user_codes, preferred_element_type=f32).astype(bf16)
-    sent = lax.all_to_all(mine.reshape(n_dp, seg_count, width), DP, 0, 0, tiled=True)
-    user_seg = jnp.sum(sent.astype(f32), axis=0).astype(bf16)
+    user_seg = lax.psum_scatter(
+        mine.reshape(n_dp, seg_count, width), DP, scatter_dimension=0, tiled=False
+    )
 
     count = ids.shape[0]
     flat_ids = jnp.transpose(ids[:, 0, :]).reshape(-1)

time: 226 us -> 227 us (level)
  blocking collectives: 79.2 us -> 57.9 us
  starting transfers between devices: 7.51 us -> 19.3 us
  waiting for transfers between devices: 59.2 us -> 66.7 us
    reduce_scatter x0 -> x1, waiting for transfers between devices: none -> 22 us  [local(): lax.psum_scatter(mine.reshape(n_dp, seg_count, width), DP, scatter_dimens...]
    all_gather x1 -> x0, waiting for transfers between devices: 14.7 us -> none  [local(): w_cols = lax.all_gather(w_x, 'z', axis=0, tiled=True)]
    all_gather x1 -> x0, blocking collectives: 12.9 us -> none  [local(): w_x = lax.all_gather(w_piece, 'x', axis=0, tiled=True)]
    all_to_all x0 -> x1, starting transfers between devices: none -> 11.6 us  [local(): lax.all_to_all(jnp.broadcast_to(w_piece[None], (n_mp,) + w_piece.shape),...]
    all_to_all x1 -> x0, blocking collectives: 10.2 us -> none  [local(): lax.all_to_all(mine.reshape(n_dp, seg_count, width), DP, 0, 0, tiled=True)]
    all_to_all x0 -> x1, waiting for transfers between devices: none -> 2.42 us  [local(): lax.all_to_all(jnp.broadcast_to(w_piece[None], (n_mp,) + w_piece.shape),...]
  transfers between devices with their start and end apart: 3 -> 4, of which waited for: 2 -> 3; matrix products, arithmetic and copies ran while one was open for 6% -> 9% of each run, Pallas kernels for 11% -> 11%
where the time goes in v6:
time: 227 us; the launch traced here: 226 us
  waiting for transfers between devices  66.7 us (29%)
  blocking collectives  57.9 us (26%)
  matrix products  32.3 us (14%)
  Pallas kernels  25 us (11%)
  starting transfers between devices  19.3 us (9%)
  between operations  14.2 us (6%)
  local copies, waits for them, and re-layouts  10.5 us (5%)
    all_to_all x1, blocking collectives, local(): returned = lax.all_to_all(grads, MP, 0, 0, tiled=True)  57.9 us
    all_to_all x1, waiting for transfers between devices, local(): x0f = lax.all_to_all(pooled.reshape(n_mp, rows, emb), MP, 0, 0, tiled=True)  42.2 us
    pallas_call x1, Pallas kernels, pool_rows(): pl.pallas_call(pool_kernel, grid_spec=spec, out_shape=jax.ShapeDtypeStruc...  25 us
    reduce_scatter x1, waiting for transfers between devices, local(): lax.psum_scatter(mine.reshape(n_dp, seg_count, width), DP, scatter_dimens...  22 us
    all_to_all x1, starting transfers between devices, local(): lax.all_to_all(jnp.broadcast_to(w_piece[None], (n_mp,) + w_piece.shape),...  11.6 us
    dot_general x1, matrix products, local(): jnp.einsum('cr,fdr->fcd', dz, cd3, preferred_element_type=f32)  9.52 us
    all_to_all x1, starting transfers between devices, local(): x0f = lax.all_to_all(pooled.reshape(n_mp, rows, emb), MP, 0, 0, tiled=True)  7.56 us
    dot_general x1, matrix products, local(): dx1 = jnp.einsum('ch,fdh->fcd', dact, w3, preferred_element_type=f32)  7.12 us
  transfers between devices with their start and end apart: 4, of which 3 were waited for; matrix products, arithmetic and copies ran while one was open for 9% of the time, Pallas kernels for 11%

profile of v6, /device:TPU:2, one launch (start us, length us, event | category | flops | bytes accessed | tf_op | source)
XLA Modules:
  0.0 226.2 jit_solution(6189464982864186380)
XLA Ops:
  7.2 0.9 constant_dynamic-slice_fusion
  8.1 1.2 broadcast_in_dim.20
  9.3 11.6 %all-to-all-start = ((bf16[32,128,128]{2,1,0:T(8,128)(2,1)}), bf16[32,128,128]{2,1,0:T(8,128)(2,1)S(1)}, u32[]{:S(2)}, u32[]{:S(2)}) async-start(bf16[32,128,128]{2,1,0:T(8,128)(2,1)} %broadcast_in_dim.20), calls=%async_computation | async-start | bytes 2097152 | tf_op jit(solution)/shard_map/all_to_all | solution.py:109
  21.0 0.6 copy.20
  21.6 25.0 %shard_map.122 = bf16[8192,128]{1,0:T(8,128)(2,1)} custom-call(s32[16384]{0:T(1024)} %bitcast.105, bf16[2048,128]{1,0:T(8,128)(2,1)} %bitcast.104), custom_call_target="tpu_custom_call" | custom-call | tf_op jit(solution)/shard_map/pallas_call | solution.py:44
  46.6 2.4 %all-to-all-done = bf16[32,128,128]{2,1,0:T(8,128)(2,1)S(1)} async-done(((bf16[32,128,128]{2,1,0:T(8,128)(2,1)}), bf16[32,128,128]{2,1,0:T(8,128)(2,1)S(1)}, u32[]{:S(2)}, u32[]{:S(2)}) %all-to-all-start) | async-done | bytes 1048608 | tf_op jit(solution)/shard_map/all_to_all | solution.py:109
  49.0 1.0 copy-done.1
  50.1 7.6 %all-to-all-start.1 = ((bf16[32,256,128]{2,1,0:T(8,128)(2,1)}), bf16[32,256,128]{2,1,0:T(8,128)(2,1)}, u32[]{:S(2)}, u32[]{:S(2)}) async-start(bf16[32,256,128]{2,1,0:T(8,128)(2,1)} %bitcast.101), calls=%async_computation.1 | async-start | bytes 4194304 | tf_op jit(solution)/shard_map/all_to_all | solution.py:131
  57.9 0.8 dynamic_slice.7
  58.6 0.9 fusion.30
  59.6 0.2 reduce-window.4
  59.8 4.2 %copy.19 = bf16[256,4096]{0,1:T(8,128)(2,1)} copy(bf16[256,4096]{1,0:T(8,128)(2,1)} %param.18) | data formatting | bytes 4194304 | tf_op jit(solution)/shard_map/reshape | solution.py:135
  64.0 0.2 select_reduce_fusion.1
  64.3 42.2 %all-to-all-done.1 = bf16[32,256,128]{2,1,0:T(8,128)(2,1)} async-done(((bf16[32,256,128]{2,1,0:T(8,128)(2,1)}), bf16[32,256,128]{2,1,0:T(8,128)(2,1)}, u32[]{:S(2)}, u32[]{:S(2)}) %all-to-all-start.1) | async-done | bytes 2097184 | tf_op jit(solution)/shard_map/all_to_all | solution.py:131
  106.5 6.6 %fusion.35 = f32[256,32,128]{2,0,1:T(8,128)} fusion(bf16[256,32,128]{0,2,1:T(8,128)(2,1)} %bitcast.99, bf16[32,256,128]{2,1,0:T(8,128)(2,1)} %all-to-all-done.1, bf16[32,128,256]{2,1,0:T(8,128)(2,1)S(1)} %bitcast.97), kind=kOutput, calls=%fused_computation.31 | convolution fusion | flops 1073807360 | bytes 10485760 | tf_op jit(solution)/shard_map/cr,rfd->fcd/dot_general | solution.py:138
  113.1 6.7 %fusion.13 = f32[256,1024]{1,0:T(8,128)S(1)} fusion(bf16[32,128,1024]{2,1,0:T(8,128)(2,1)} %bitcast.114, bf16[32,256,128]{2,1,0:T(8,128)(2,1)} %all-to-all-done.1, f32[256,32,128]{2,0,1:T(8,128)} %fusion.35, f32[32,128]{1,0:T(8,128)S(1)} %bitcast.107, f32[1024]{0:T(1024)S(1)} %copy-done.8), kind=kOutput, calls=%fused_computation.15 | convolution fusion | flops 2152988672 | bytes 15749120 | tf_op jit(solution)/shard_map/fcd,fdh->ch/dot_general | solution.py:140
  119.7 22.0 %reduce-scatter.2.cloned.1.call-done = bf16[1,8,1024]{2,1,0:T(8,128)(2,1)} async-done(((bf16[8,8,1024]{2,1,0:T(8,128)(2,1)}), bf16[1,8,1024]{2,1,0:T(8,128)(2,1)}) %reduce-scatter.2.cloned.1.call-update) | async-done | bytes 16400 | tf_op jit(solution)/shard_map/reduce_scatter | solution.py:121
  141.7 1.1 fusion.34
  142.9 0.4 fusion.26
  143.3 0.2 copy-done.7
  143.6 7.1 %fusion.36 = f32[32,128,256]{1,2,0:T(8,128)} fusion(bf16[32,128,1024]{2,1,0:T(8,128)(2,1)} %bitcast.115, f32[256,1024]{1,0:T(8,128)S(1)} %fusion.13, f32[256]{0:T(256)S(1)} %maximum_divide_fusion, bf16[1,8,1024]{2,1,0:T(8,128)(2,1)S(1)} %copy-done.7, s32[8]{0:T(128)S(1)} %bitcast.113, s32[8]{0:T(128)S(1)} %fusion.53), kind=kOutput, calls=%fused_computation.34 | convolution fusion | flops 2154567680 | bytes 13648960 | tf_op jit(solution)/shard_map/ch,fdh->fcd/dot_general | solution.py:149
  150.7 9.5 %fusion.2 = bf16[32,256,128]{2,1,0:T(8,128)(2,1)} fusion(f32[32,128,256]{1,2,0:T(8,128)} %fusion.36, f32[256,32,128]{2,0,1:T(8,128)} %fusion.35, bf16[32,128,256]{2,1,0:T(8,128)(2,1)S(1)} %bitcast.98, f32[32,128]{1,0:T(8,128)S(1)} %bitcast.108, bf16[256,32,128]{0,2,1:T(8,128)(2,1)} %bitcast.100, bf16[32,256,128]{2,1,0:T(8,128)(2,1)} %all-to-all-done.1), kind=kOutput, calls=%fused_computation.5 | convolution fusion | flops 1082195968 | bytes 16793600 | tf_op jit(solution)/shard_map/cr,fdr->fcd/dot_general | solution.py:152
  160.2 57.9 %all_to_all.15 = bf16[32,256,128]{2,1,0:T(8,128)(2,1)S(1)} all-to-all(bf16[32,256,128]{2,1,0:T(8,128)(2,1)} %fusion.2), channel_id=1, replica_groups=mesh['y'=4,'c'=2,'z'=8,'x'=4] {'z','x'}, dimensions={0} | all-to-all | bytes 4194304 | tf_op jit(solution)/shard_map/all_to_all | solution.py:156
  218.1 1.3 copy.22
  (31 shorter events, 0.4 us)
Async XLA Ops:
  7.2 99.3 %copy-start = (bf16[4096,256]{1,0:T(8,128)(2,1)S(1)}, bf16[4096,256]{1,0:T(8,128)(2,1)}, u32[]{:S(2)}) copy-start(bf16[4096,256]{1,0:T(8,128)(2,1)} %param.17) | copy-start | bytes 6291460
  7.2 13.8 %copy-start.3 = (s32[8192,1,2]{0,2,1:T(2,128)S(1)}, s32[8192,1,2]{0,2,1:T(2,128)}, u32[]{:S(2)}) copy-start(s32[8192,1,2]{0,2,1:T(2,128)} %param.12) | copy-start | bytes 196612
  9.3 39.7 %all-to-all-start = ((bf16[32,128,128]{2,1,0:T(8,128)(2,1)}), bf16[32,128,128]{2,1,0:T(8,128)(2,1)S(1)}, u32[]{:S(2)}, u32[]{:S(2)}) async-start(bf16[32,128,128]{2,1,0:T(8,128)(2,1)} %broadcast_in_dim.20), calls=%async_computation | async-start | bytes 2097152 | tf_op jit(solution)/shard_map/all_to_all | solution.py:109
  20.9 92.1 %all-gather.2.cloned.1.call-start = ((), (), s32[]{:S(2)}) async-start(), calls=%async_computation.4 | async-start | bytes 9437184 | tf_op jit(solution)/shard_map/all_gather | solution.py:129
  49.0 1.0 copy-start.1
  50.1 8.6 %copy-start.2 = (bf16[256,1024]{1,0:T(8,128)(2,1)S(1)}, bf16[256,1024]{1,0:T(8,128)(2,1)}, u32[]{:S(2)}) copy-start(bf16[256,1024]{1,0:T(8,128)(2,1)} %param.16) | copy-start | bytes 1572868
  50.1 9.5 %copy-start.9 = (s32[1,8]{1,0:T(1,128)S(1)}, s32[1,8]{1,0:T(1,128)}, u32[]{:S(2)}) copy-start(s32[1,8]{1,0:T(1,128)} %param.13) | copy-start | bytes 100
  50.1 56.4 %all-to-all-start.1 = ((bf16[32,256,128]{2,1,0:T(8,128)(2,1)}), bf16[32,256,128]{2,1,0:T(8,128)(2,1)}, u32[]{:S(2)}, u32[]{:S(2)}) async-start(bf16[32,256,128]{2,1,0:T(8,128)(2,1)} %bitcast.101), calls=%async_computation.1 | async-start | bytes 4194304 | tf_op jit(solution)/shard_map/all_to_all | solution.py:131
  57.7 84.1 %reduce-scatter.2.cloned.1.call-start = ((), (), s32[]{:S(2)}) async-start(), calls=%async_computation.5 | async-start | bytes 147456 | tf_op jit(solution)/shard_map/reduce_scatter | solution.py:121
  59.8 4.2 %copy-start.5 = (s32[256]{0:T(256)S(1)}, s32[256]{0:T(256)}, u32[]{:S(2)}) copy-start(s32[256]{0:T(256)} %param.14) | copy-start | bytes 3076
  106.5 6.6 %copy-start.4 = (f32[4096]{0:T(1024)S(1)}, f32[4096]{0:T(1024)}, u32[]{:S(2)}) copy-start(f32[4096]{0:T(1024)} %param.19) | copy-start | bytes 49156
  106.5 6.6 %copy-start.8 = (f32[1024]{0:T(1024)S(1)}, f32[1024]{0:T(1024)}, u32[]{:S(2)}) copy-start(f32[1024]{0:T(1024)} %param.21) | copy-start | bytes 12292
  142.9 0.7 copy-start.7
  142.9 7.8 %copy-start.6 = (f32[256]{0:T(256)}, f32[256]{0:T(256)S(1)}, u32[]{:S(2)}) copy-start(f32[256]{0:T(256)S(1)} %broadcast_multiply_fusion) | copy-start | bytes 3076
Sparse Core Ops, SparseCore 0:
  50.2 54.6 all-gather.1
  107.4 34.3 reduce-scatter.1

commit v7 on v6

--- a/solution.py
+++ b/solution.py
@@ -118,16 +118,18 @@
     ).reshape(-1)
     pick = (home_local[None, :] == wanted[:, None]).astype(bf16)
     mine = jnp.dot(pick, user_codes, preferred_element_type=f32).astype(bf16)
-    user_seg = lax.psum_scatter(
-        mine.reshape(n_dp, seg_count, width), DP, scatter_dimension=0, tiled=False
-    )
 
     count = ids.shape[0]
     flat_ids = jnp.transpose(ids[:, 0, :]).reshape(-1)
     pooled = pool_rows(table[0], flat_ids, count)
     w_cols, pooled = lax.optimization_barrier((w_cols, pooled))
-    w_all = lax.all_gather(w_cols, DP, axis=1, tiled=True)
-    w3 = w_all.reshape(n_mp, emb, width)
+    payload = jnp.concatenate([w_cols, mine.reshape(-1, piece)], axis=0)
+    both = lax.all_gather(payload, DP, axis=1, tiled=True)
+    w3 = both[: w_cols.shape[0]].reshape(n_mp, emb, width)
+    ride = seg_count * width // piece
+    mine_all = lax.dynamic_slice_in_dim(both, w_cols.shape[0] + d_idx * ride, ride, axis=0)
+    mine_all = mine_all.reshape(seg_count, width // piece, n_dp, piece)
+    user_seg = jnp.sum(mine_all.astype(f32), axis=2).reshape(seg_count, width).astype(bf16)
     x0f = lax.all_to_all(pooled.reshape(n_mp, rows, emb), MP, 0, 0, tiled=True)
 
     member = members(counts[0], rows)

time: 227 us -> 214 us (0.943)
  waiting for transfers between devices: 66.7 us -> 44.3 us
  local copies, waits for them, and re-layouts: 10.5 us -> 17.6 us
    reduce_scatter x1 -> x0, waiting for transfers between devices: 22 us -> none  [local(): lax.psum_scatter(mine.reshape(n_dp, seg_count, width), DP, scatter_dimens...]
    slice x0 -> x1, local copies, waits for them, and re-layouts: none -> 7.86 us  [local(): w3 = both[:w_cols.shape[0]].reshape(n_mp, emb, width)]
    all_to_all x1, waiting for transfers between devices: 2.42 us -> 0.13 us  [local(): lax.all_to_all(jnp.broadcast_to(w_piece[None], (n_mp,) + w_piece.shape),...]
  transfers between devices with their start and end apart: 4 -> 3, of which waited for: 3 -> 2; matrix products, arithmetic and copies ran while one was open for 9% -> 7% of each run, Pallas kernels for 11% -> 12%
where the time goes in v7:
time: 214 us
  blocking collectives  57.2 us (27%)
  waiting for transfers between devices  44.3 us (21%)
  matrix products  31.4 us (15%)
  Pallas kernels  25 us (12%)
  starting transfers between devices  21.4 us (10%)
  local copies, waits for them, and re-layouts  17.6 us (8%)
  between operations  14.2 us (7%)
  other arithmetic  2.55 us (1%)
    all_to_all x1, blocking collectives, local(): returned = lax.all_to_all(grads, MP, 0, 0, tiled=True)  57.2 us
    all_to_all x1, waiting for transfers between devices, local(): x0f = lax.all_to_all(pooled.reshape(n_mp, rows, emb), MP, 0, 0, tiled=True)  44.2 us
    pallas_call x1, Pallas kernels, pool_rows(): pl.pallas_call(pool_kernel, grid_spec=spec, out_shape=jax.ShapeDtypeStruc...  25 us
    all_to_all x1, starting transfers between devices, local(): lax.all_to_all(jnp.broadcast_to(w_piece[None], (n_mp,) + w_piece.shape),...  11.6 us
    all_to_all x1, starting transfers between devices, local(): x0f = lax.all_to_all(pooled.reshape(n_mp, rows, emb), MP, 0, 0, tiled=True)  9.71 us
    dot_general x1, matrix products, local(): jnp.einsum('cr,fdr->fcd', dz, cd3, preferred_element_type=f32)  9.52 us
    slice x1, local copies, waits for them, and re-layouts, local(): w3 = both[:w_cols.shape[0]].reshape(n_mp, emb, width)  7.86 us
    dot_general x1, matrix products, local(): dx1 = jnp.einsum('ch,fdh->fcd', dact, w3, preferred_element_type=f32)  7.36 us
  transfers between devices with their start and end apart: 3, of which 2 were waited for; matrix products, arithmetic and copies ran while one was open for 7% of the time, Pallas kernels for 12%

profile of v7, /device:TPU:2, one launch (start us, length us, event | category | flops | bytes accessed | tf_op | source)
XLA Modules:
  0.0 213.7 jit_solution(2552130819753519532)
XLA Ops:
  7.2 0.9 constant_dynamic-slice_fusion
  8.1 1.2 broadcast_in_dim.20
  9.3 11.6 %all-to-all-start = ((bf16[32,128,128]{2,1,0:T(8,128)(2,1)}), bf16[32,128,128]{2,1,0:T(8,128)(2,1)S(1)}, u32[]{:S(2)}, u32[]{:S(2)}) async-start(bf16[32,128,128]{2,1,0:T(8,128)(2,1)} %broadcast_in_dim.20), calls=%async_computation | async-start | bytes 2097152 | tf_op jit(solution)/shard_map/all_to_all | solution.py:109
  21.2 0.6 copy.20
  21.8 0.8 dynamic_slice.10
  22.6 1.3 convolution_convert_fusion
  23.9 25.0 %shard_map.122 = bf16[8192,128]{1,0:T(8,128)(2,1)} custom-call(s32[16384]{0:T(1024)} %bitcast.108, bf16[2048,128]{1,0:T(8,128)(2,1)} %bitcast.107), custom_call_target="tpu_custom_call" | custom-call | tf_op jit(solution)/shard_map/pallas_call | solution.py:44
  49.0 1.1 pad_maximum_fusion
  50.1 9.7 %all-to-all-start.1 = ((bf16[32,256,128]{2,1,0:T(8,128)(2,1)}), bf16[32,256,128]{2,1,0:T(8,128)(2,1)}, u32[]{:S(2)}, u32[]{:S(2)}) async-start(bf16[32,256,128]{2,1,0:T(8,128)(2,1)} %bitcast.104), calls=%async_computation.1 | async-start | bytes 4194304 | tf_op jit(solution)/shard_map/all_to_all | solution.py:133
  59.9 0.2 reduce-window.4
  60.1 4.2 %copy.19 = bf16[256,4096]{0,1:T(8,128)(2,1)} copy(bf16[256,4096]{1,0:T(8,128)(2,1)} %param.18) | data formatting | bytes 4194304 | tf_op jit(solution)/shard_map/reshape | solution.py:137
  64.3 0.2 select_reduce_fusion.1
  64.5 44.2 %all-to-all-done.1 = bf16[32,256,128]{2,1,0:T(8,128)(2,1)} async-done(((bf16[32,256,128]{2,1,0:T(8,128)(2,1)}), bf16[32,256,128]{2,1,0:T(8,128)(2,1)}, u32[]{:S(2)}, u32[]{:S(2)}) %all-to-all-start.1) | async-done | bytes 2097184 | tf_op jit(solution)/shard_map/all_to_all | solution.py:133
  108.7 6.9 %fusion.34 = f32[256,32,128]{2,0,1:T(8,128)} fusion(bf16[256,32,128]{0,2,1:T(8,128)(2,1)} %bitcast.100, bf16[32,256,128]{2,1,0:T(8,128)(2,1)} %all-to-all-done.1, bf16[32,128,256]{2,1,0:T(8,128)(2,1)S(1)} %bitcast.98), kind=kOutput, calls=%fused_computation.31 | convolution fusion | flops 1073807360 | bytes 10485760 | tf_op jit(solution)/shard_map/cr,rfd->fcd/dot_general | solution.py:140
  115.6 7.9 %slice.4 = bf16[4096,1024]{1,0:T(8,128)(2,1)} slice(bf16[4608,1024]{1,0:T(8,128)(2,1)} %all-gather.2.cloned.1.call-done), slice={[0:4096], [0:1024]} | slice | bytes 16777216 | tf_op jit(solution)/shard_map/slice | solution.py:128
  123.5 0.9 bitcast_reduce_fusion
  124.4 5.5 %fusion.13 = f32[256,1024]{1,0:T(8,128)S(1)} fusion(bf16[32,128,1024]{2,1,0:T(8,128)(2,1)} %bitcast.102, bf16[32,256,128]{2,1,0:T(8,128)(2,1)} %all-to-all-done.1, f32[256,32,128]{2,0,1:T(8,128)S(1)} %copy-done.1, f32[32,128]{1,0:T(8,128)S(1)} %bitcast.110, f32[1024]{0:T(1024)S(1)} %copy-done.6), kind=kOutput, calls=%fused_computation.15 | convolution fusion | flops 2152988672 | bytes 15749120 | tf_op jit(solution)/shard_map/fcd,fdh->ch/dot_general | solution.py:142
  130.0 0.4 fusion.33
  130.4 0.5 copy-done.8
  130.9 0.4 fusion.26
  131.4 7.4 %fusion.35 = f32[32,128,256]{1,2,0:T(8,128)} fusion(bf16[32,128,1024]{2,1,0:T(8,128)(2,1)} %bitcast.103, f32[256,1024]{1,0:T(8,128)} %copy-done.8, f32[256]{0:T(256)S(1)} %maximum_divide_fusion, bf16[1,8,8,128]{3,2,1,0:T(8,128)(2,1)S(1)} %bitcast.113, s32[8]{0:T(128)S(1)} %bitcast.118, s32[8]{0:T(128)S(1)} %fusion.55), kind=kOutput, calls=%fused_computation.34 | convolution fusion | flops 2154567680 | bytes 13648960 | tf_op jit(solution)/shard_map/ch,fdh->fcd/dot_general | solution.py:151
  138.8 9.5 %fusion.2 = bf16[32,256,128]{2,1,0:T(8,128)(2,1)} fusion(f32[32,128,256]{1,2,0:T(8,128)} %fusion.35, f32[256,32,128]{2,0,1:T(8,128)} %fusion.34, bf16[32,128,256]{2,1,0:T(8,128)(2,1)S(1)} %bitcast.99, f32[32,128]{1,0:T(8,128)S(1)} %bitcast.111, bf16[256,32,128]{0,2,1:T(8,128)(2,1)} %bitcast.101, bf16[32,256,128]{2,1,0:T(8,128)(2,1)} %all-to-all-done.1), kind=kOutput, calls=%fused_computation.5 | convolution fusion | flops 1082195968 | bytes 16793600 | tf_op jit(solution)/shard_map/cr,fdr->fcd/dot_general | solution.py:154
  148.3 57.2 %all_to_all.15 = bf16[32,256,128]{2,1,0:T(8,128)(2,1)S(1)} all-to-all(bf16[32,256,128]{2,1,0:T(8,128)(2,1)} %fusion.2), channel_id=1, replica_groups=mesh['y'=4,'c'=2,'z'=8,'x'=4] {'z','x'}, dimensions={0} | all-to-all | bytes 4194304 | tf_op jit(solution)/shard_map/all_to_all | solution.py:158
  205.5 1.3 copy.32
  (30 shorter events, 0.6 us)
Async XLA Ops:
  7.2 101.5 %copy-start = (bf16[4096,256]{1,0:T(8,128)(2,1)S(1)}, bf16[4096,256]{1,0:T(8,128)(2,1)}, u32[]{:S(2)}) copy-start(bf16[4096,256]{1,0:T(8,128)(2,1)} %param.17) | copy-start | bytes 6291460
  7.2 14.0 %copy-start.2 = (s32[8192,1,2]{0,2,1:T(2,128)S(1)}, s32[8192,1,2]{0,2,1:T(2,128)}, u32[]{:S(2)}) copy-start(s32[8192,1,2]{0,2,1:T(2,128)} %param.12) | copy-start | bytes 196612
  9.3 39.7 %all-to-all-start = ((bf16[32,128,128]{2,1,0:T(8,128)(2,1)}), bf16[32,128,128]{2,1,0:T(8,128)(2,1)S(1)}, u32[]{:S(2)}, u32[]{:S(2)}) async-start(bf16[32,128,128]{2,1,0:T(8,128)(2,1)} %broadcast_in_dim.20), calls=%async_computation | async-start | bytes 2097152 | tf_op jit(solution)/shard_map/all_to_all | solution.py:109
  21.0 94.6 %all-gather.2.cloned.1.call-start = ((), (), s32[]{:S(2)}) async-start(), calls=%async_computation.3 | async-start | bytes 10616832 | tf_op jit(solution)/shard_map/all_gather | solution.py:127
  50.1 9.7 %copy-start.7 = (s32[1,8]{1,0:T(1,128)S(1)}, s32[1,8]{1,0:T(1,128)}, u32[]{:S(2)}) copy-start(s32[1,8]{1,0:T(1,128)} %param.13) | copy-start | bytes 100
  50.1 58.6 %all-to-all-start.1 = ((bf16[32,256,128]{2,1,0:T(8,128)(2,1)}), bf16[32,256,128]{2,1,0:T(8,128)(2,1)}, u32[]{:S(2)}, u32[]{:S(2)}) async-start(bf16[32,256,128]{2,1,0:T(8,128)(2,1)} %bitcast.104), calls=%async_computation.1 | async-start | bytes 4194304 | tf_op jit(solution)/shard_map/all_to_all | solution.py:133
  60.1 4.2 %copy-start.4 = (s32[256]{0:T(256)S(1)}, s32[256]{0:T(256)}, u32[]{:S(2)}) copy-start(s32[256]{0:T(256)} %param.14) | copy-start | bytes 3076
  115.6 8.8 %copy-start.3 = (f32[4096]{0:T(1024)S(1)}, f32[4096]{0:T(1024)}, u32[]{:S(2)}) copy-start(f32[4096]{0:T(1024)} %param.19) | copy-start | bytes 49156
  115.6 8.8 %copy-start.6 = (f32[1024]{0:T(1024)S(1)}, f32[1024]{0:T(1024)}, u32[]{:S(2)}) copy-start(f32[1024]{0:T(1024)} %param.21) | copy-start | bytes 12292
  115.6 8.8 %copy-start.1 = (f32[256,32,128]{2,0,1:T(8,128)S(1)}, f32[256,32,128]{2,0,1:T(8,128)}, u32[]{:S(2)}) copy-start(f32[256,32,128]{2,0,1:T(8,128)} %fusion.34) | copy-start | bytes 12582916
  130.0 1.0 copy-start.8
  130.9 7.8 %copy-start.5 = (f32[256]{0:T(256)}, f32[256]{0:T(256)S(1)}, u32[]{:S(2)}) copy-start(f32[256]{0:T(256)S(1)} %broadcast_multiply_fusion) | copy-start | bytes 3076
Sparse Core Ops, SparseCore 0:
  50.3 61.4 all-gather.1

commit v8 on v7

--- a/solution.py
+++ b/solution.py
@@ -125,7 +125,8 @@
     w_cols, pooled = lax.optimization_barrier((w_cols, pooled))
     payload = jnp.concatenate([w_cols, mine.reshape(-1, piece)], axis=0)
     both = lax.all_gather(payload, DP, axis=1, tiled=True)
-    w3 = both[: w_cols.shape[0]].reshape(n_mp, emb, width)
+    w3 = both.reshape(-1, emb, width)
+    extra = w3.shape[0] - n_mp
     ride = seg_count * width // piece
     mine_all = lax.dynamic_slice_in_dim(both, w_cols.shape[0] + d_idx * ride, ride, axis=0)
     mine_all = mine_all.reshape(seg_count, width // piece, n_dp, piece)
@@ -139,7 +140,8 @@
     z = jnp.einsum("fcd,fdr->cr", x0f, cd3, preferred_element_type=f32).astype(bf16)
     cross = jnp.einsum("cr,rfd->fcd", z, cu3, preferred_element_type=f32) + bias3
     x1 = (x0f * cross + x0f).astype(bf16)
-    act = jnp.einsum("fcd,fdh->ch", x1, w3, preferred_element_type=f32) + tower_bias
+    x1p = jnp.pad(x1, ((0, extra), (0, 0), (0, 0)))
+    act = jnp.einsum("fcd,fdh->ch", x1p, w3, preferred_element_type=f32) + tower_bias
     sig = jax.nn.sigmoid(act)
     hidden = (act * sig).astype(bf16)
     pair = dot_last(hidden, user_seg)
@@ -148,7 +150,7 @@
     code = jnp.dot(member.astype(bf16), user_seg, preferred_element_type=f32)
     slope = sig * (1.0 + act * (1.0 - sig))
     dact = (dscore[:, None] * code * scale * slope).astype(bf16)
-    dx1 = jnp.einsum("ch,fdh->fcd", dact, w3, preferred_element_type=f32)
+    dx1 = jnp.einsum("ch,fdh->fcd", dact, w3, preferred_element_type=f32)[:n_mp]
     dcross = (dx1 * x0f).astype(bf16)
     dz = jnp.einsum("fcd,rfd->cr", dcross, cu3, preferred_element_type=f32).astype(bf16)
     dx0 = dx1 * (1.0 + cross) + jnp.einsum(

time: 214 us -> 208 us (0.972)
  local copies, waits for them, and re-layouts: 17.6 us -> 9.15 us
    slice x1 -> x0, local copies, waits for them, and re-layouts: 7.86 us -> none  [local(): w3 = both[:w_cols.shape[0]].reshape(n_mp, emb, width)]
where the time goes in v8:
time: 208 us; the launch traced here: 207 us
  blocking collectives  57.3 us (28%)
  waiting for transfers between devices  44.4 us (21%)
  matrix products  33.4 us (16%)
  Pallas kernels  25 us (12%)
  starting transfers between devices  21.4 us (10%)
  between operations  14.2 us (7%)
  local copies, waits for them, and re-layouts  9.15 us (4%)
  other arithmetic  2.56 us (1%)
    all_to_all x1, blocking collectives, local(): returned = lax.all_to_all(grads, MP, 0, 0, tiled=True)  57.3 us
    all_to_all x1, waiting for transfers between devices, local(): x0f = lax.all_to_all(pooled.reshape(n_mp, rows, emb), MP, 0, 0, tiled=True)  44.2 us
    pallas_call x1, Pallas kernels, pool_rows(): pl.pallas_call(pool_kernel, grid_spec=spec, out_shape=jax.ShapeDtypeStruc...  25 us
    all_to_all x1, starting transfers between devices, local(): lax.all_to_all(jnp.broadcast_to(w_piece[None], (n_mp,) + w_piece.shape),...  11.6 us
    all_to_all x1, starting transfers between devices, local(): x0f = lax.all_to_all(pooled.reshape(n_mp, rows, emb), MP, 0, 0, tiled=True)  9.71 us
    dot_general x1, matrix products, local(): jnp.einsum('cr,fdr->fcd', dz, cd3, preferred_element_type=f32)  9.53 us
    dot_general x1, matrix products, local(): dx1 = jnp.einsum('ch,fdh->fcd', dact, w3, preferred_element_type=f32)[:n_mp]  7.79 us
    dot_general x1, matrix products, local(): jnp.einsum('fcd,fdh->ch', x1p, w3, preferred_element_type=f32) + tower_bias  7.1 us
  transfers between devices with their start and end apart: 3, of which 2 were waited for; matrix products, arithmetic and copies ran while one was open for 7% of the time, Pallas kernels for 12%

profile of v8, /device:TPU:2, one launch (start us, length us, event | category | flops | bytes accessed | tf_op | source)
XLA Modules:
  0.0 207.3 jit_solution(16127728594862227834)
XLA Ops:
  7.2 0.9 constant_dynamic-slice_fusion
  8.1 1.2 broadcast_in_dim.20
  9.3 11.6 %all-to-all-start = ((bf16[32,128,128]{2,1,0:T(8,128)(2,1)}), bf16[32,128,128]{2,1,0:T(8,128)(2,1)S(1)}, u32[]{:S(2)}, u32[]{:S(2)}) async-start(bf16[32,128,128]{2,1,0:T(8,128)(2,1)} %broadcast_in_dim.20), calls=%async_computation | async-start | bytes 2097152 | tf_op jit(solution)/shard_map/all_to_all | solution.py:109
  21.2 0.6 copy.20
  21.8 0.8 dynamic_slice.10
  22.6 1.3 convolution_convert_fusion
  23.9 25.0 %shard_map.122 = bf16[8192,128]{1,0:T(8,128)(2,1)} custom-call(s32[16384]{0:T(1024)} %bitcast.96, bf16[2048,128]{1,0:T(8,128)(2,1)} %bitcast.95), custom_call_target="tpu_custom_call" | custom-call | tf_op jit(solution)/shard_map/pallas_call | solution.py:44
  48.9 0.1 all-to-all-done
  49.0 1.1 pad_maximum_fusion
  50.1 9.7 %all-to-all-start.1 = ((bf16[32,256,128]{2,1,0:T(8,128)(2,1)}), bf16[32,256,128]{2,1,0:T(8,128)(2,1)}, u32[]{:S(2)}, u32[]{:S(2)}) async-start(bf16[32,256,128]{2,1,0:T(8,128)(2,1)} %bitcast.92), calls=%async_computation.1 | async-start | bytes 4194304 | tf_op jit(solution)/shard_map/all_to_all | solution.py:134
  59.9 0.2 reduce-window.4
  60.1 4.1 %copy.19 = bf16[256,4096]{0,1:T(8,128)(2,1)} copy(bf16[256,4096]{1,0:T(8,128)(2,1)} %param.18) | data formatting | bytes 4194304 | tf_op jit(solution)/shard_map/reshape | solution.py:138
  64.2 0.2 select_reduce_fusion.1
  64.4 0.1 select_reduce_fusion
  64.5 44.2 %all-to-all-done.1 = bf16[32,256,128]{2,1,0:T(8,128)(2,1)} async-done(((bf16[32,256,128]{2,1,0:T(8,128)(2,1)}), bf16[32,256,128]{2,1,0:T(8,128)(2,1)}, u32[]{:S(2)}, u32[]{:S(2)}) %all-to-all-start.1) | async-done | bytes 2097184 | tf_op jit(solution)/shard_map/all_to_all | solution.py:134
  108.7 6.9 %fusion.35 = f32[256,32,128]{2,0,1:T(8,128)} fusion(bf16[256,32,128]{0,2,1:T(8,128)(2,1)} %bitcast.90, bf16[32,256,128]{2,1,0:T(8,128)(2,1)} %all-to-all-done.1, bf16[32,128,256]{2,1,0:T(8,128)(2,1)S(1)} %bitcast.88), kind=kOutput, calls=%fused_computation.32 | convolution fusion | flops 1073807360 | bytes 10485760 | tf_op jit(solution)/shard_map/cr,rfd->fcd/dot_general | solution.py:141
  115.6 0.9 bitcast_reduce_fusion
  116.5 7.1 %fusion.14 = f32[256,1024]{1,0:T(8,128)S(1)} fusion(bf16[36,128,1024]{2,1,0:T(8,128)(2,1)} %bitcast.107, bf16[32,256,128]{2,1,0:T(8,128)(2,1)} %all-to-all-done.1, f32[256,32,128]{2,0,1:T(8,128)} %fusion.35, f32[32,128]{1,0:T(8,128)S(1)} %bitcast.98, f32[1024]{0:T(1024)S(1)} %copy-done.5), kind=kOutput, calls=%fused_computation.16 | convolution fusion | flops 2152988672 | bytes 16797696 | tf_op jit(solution)/shard_map/fcd,fdh->ch/dot_general | solution.py:144
  123.6 0.4 fusion.34
  124.1 0.4 fusion.27
  124.5 7.8 %convolution_bitcast_fusion = f32[36,256,128]{2,1,0:T(8,128)} fusion(bf16[36,128,1024]{2,1,0:T(8,128)(2,1)} %bitcast.108, f32[256,1024]{1,0:T(8,128)S(1)} %fusion.14, f32[256]{0:T(256)S(1)} %maximum_divide_fusion, bf16[1,8,8,128]{3,2,1,0:T(8,128)(2,1)S(1)} %bitcast.101, s32[8]{0:T(128)S(1)} %bitcast.106, s32[8]{0:T(128)S(1)} %fusion.55), kind=kOutput, calls=%fused_computation.8 | convolution fusion | flops 2423003136 | bytes 15221824 | tf_op jit(solution)/shard_map/ch,fdh->fcd/dot_general | solution.py:153
  132.3 9.5 %fusion.2 = bf16[32,256,128]{2,1,0:T(8,128)(2,1)} fusion(f32[36,256,128]{2,1,0:T(8,128)} %convolution_bitcast_fusion, f32[256,32,128]{2,0,1:T(8,128)} %fusion.35, bf16[32,128,256]{2,1,0:T(8,128)(2,1)S(1)} %bitcast.89, f32[32,128]{1,0:T(8,128)S(1)} %bitcast.99, bf16[256,32,128]{0,2,1:T(8,128)(2,1)} %bitcast.91, bf16[32,256,128]{2,1,0:T(8,128)(2,1)} %all-to-all-done.1), kind=kOutput, calls=%fused_computation.5 | convolution fusion | flops 1082195968 | bytes 20987904 | tf_op jit(solution)/shard_map/cr,fdr->fcd/dot_general | solution.py:156
  141.9 57.3 %all_to_all.15 = bf16[32,256,128]{2,1,0:T(8,128)(2,1)S(1)} all-to-all(bf16[32,256,128]{2,1,0:T(8,128)(2,1)} %fusion.2), channel_id=1, replica_groups=mesh['y'=4,'c'=2,'z'=8,'x'=4] {'z','x'}, dimensions={0} | all-to-all | bytes 4194304 | tf_op jit(solution)/shard_map/all_to_all | solution.py:160
  199.1 1.3 copy.32
  (25 shorter events, 0.3 us)
Async XLA Ops:
  7.2 101.5 %copy-start = (bf16[4096,256]{1,0:T(8,128)(2,1)S(1)}, bf16[4096,256]{1,0:T(8,128)(2,1)}, u32[]{:S(2)}) copy-start(bf16[4096,256]{1,0:T(8,128)(2,1)} %param.17) | copy-start | bytes 6291460
  7.2 14.0 %copy-start.1 = (s32[8192,1,2]{0,2,1:T(2,128)S(1)}, s32[8192,1,2]{0,2,1:T(2,128)}, u32[]{:S(2)}) copy-start(s32[8192,1,2]{0,2,1:T(2,128)} %param.12) | copy-start | bytes 196612
  9.3 39.7 %all-to-all-start = ((bf16[32,128,128]{2,1,0:T(8,128)(2,1)}), bf16[32,128,128]{2,1,0:T(8,128)(2,1)S(1)}, u32[]{:S(2)}, u32[]{:S(2)}) async-start(bf16[32,128,128]{2,1,0:T(8,128)(2,1)} %broadcast_in_dim.20), calls=%async_computation | async-start | bytes 2097152 | tf_op jit(solution)/shard_map/all_to_all | solution.py:109
  21.0 94.6 %all-gather.2.cloned.1.call-start = ((), (), s32[]{:S(2)}) async-start(), calls=%async_computation.3 | async-start | bytes 10616832 | tf_op jit(solution)/shard_map/all_gather | solution.py:127
  50.1 9.7 %copy-start.6 = (s32[1,8]{1,0:T(1,128)S(1)}, s32[1,8]{1,0:T(1,128)}, u32[]{:S(2)}) copy-start(s32[1,8]{1,0:T(1,128)} %param.13) | copy-start | bytes 100
  50.1 58.6 %all-to-all-start.1 = ((bf16[32,256,128]{2,1,0:T(8,128)(2,1)}), bf16[32,256,128]{2,1,0:T(8,128)(2,1)}, u32[]{:S(2)}, u32[]{:S(2)}) async-start(bf16[32,256,128]{2,1,0:T(8,128)(2,1)} %bitcast.92), calls=%async_computation.1 | async-start | bytes 4194304 | tf_op jit(solution)/shard_map/all_to_all | solution.py:134
  60.1 4.1 %copy-start.3 = (s32[256]{0:T(256)S(1)}, s32[256]{0:T(256)}, u32[]{:S(2)}) copy-start(s32[256]{0:T(256)} %param.14) | copy-start | bytes 3076
  108.7 7.8 %copy-start.2 = (f32[4096]{0:T(1024)S(1)}, f32[4096]{0:T(1024)}, u32[]{:S(2)}) copy-start(f32[4096]{0:T(1024)} %param.19) | copy-start | bytes 49156
  108.7 7.8 %copy-start.5 = (f32[1024]{0:T(1024)S(1)}, f32[1024]{0:T(1024)}, u32[]{:S(2)}) copy-start(f32[1024]{0:T(1024)} %param.21) | copy-start | bytes 12292
  124.1 8.3 %copy-start.4 = (f32[256]{0:T(256)}, f32[256]{0:T(256)S(1)}, u32[]{:S(2)}) copy-start(f32[256]{0:T(256)S(1)} %broadcast_multiply_fusion) | copy-start | bytes 3076
Sparse Core Ops, SparseCore 0:
  50.3 61.4 all-gather.1

commit v9 on v7

--- a/solution.py
+++ b/solution.py
@@ -123,11 +123,10 @@
     flat_ids = jnp.transpose(ids[:, 0, :]).reshape(-1)
     pooled = pool_rows(table[0], flat_ids, count)
     w_cols, pooled = lax.optimization_barrier((w_cols, pooled))
-    payload = jnp.concatenate([w_cols, mine.reshape(-1, piece)], axis=0)
-    both = lax.all_gather(payload, DP, axis=1, tiled=True)
-    w3 = both[: w_cols.shape[0]].reshape(n_mp, emb, width)
+    w_all, mine_all = lax.all_gather((w_cols, mine.reshape(-1, piece)), DP, axis=1, tiled=True)
+    w3 = w_all.reshape(n_mp, emb, width)
     ride = seg_count * width // piece
-    mine_all = lax.dynamic_slice_in_dim(both, w_cols.shape[0] + d_idx * ride, ride, axis=0)
+    mine_all = lax.dynamic_slice_in_dim(mine_all, d_idx * ride, ride, axis=0)
     mine_all = mine_all.reshape(seg_count, width // piece, n_dp, piece)
     user_seg = jnp.sum(mine_all.astype(f32), axis=2).reshape(seg_count, width).astype(bf16)
     x0f = lax.all_to_all(pooled.reshape(n_mp, rows, emb), MP, 0, 0, tiled=True)

time: 214 us -> 205 us (0.958)
  local copies, waits for them, and re-layouts: 17.6 us -> 10.8 us
    slice x1 -> x0, local copies, waits for them, and re-layouts: 7.86 us -> none  [local(): w3 = both[:w_cols.shape[0]].reshape(n_mp, emb, width)]
  transfers between devices with their start and end apart: 3 -> 4, of which waited for: 2 -> 1; matrix products, arithmetic and copies ran while one was open for 7% -> 8% of each run, Pallas kernels for 12% -> 12%
where the time goes in v9:
time: 205 us
  blocking collectives  56.2 us (27%)
  waiting for transfers between devices  43.3 us (21%)
  matrix products  32 us (16%)
  Pallas kernels  25 us (12%)
  starting transfers between devices  21.5 us (10%)
  between operations  14.2 us (7%)
  local copies, waits for them, and re-layouts  10.8 us (5%)
    all_to_all x1, blocking collectives, local(): returned = lax.all_to_all(grads, MP, 0, 0, tiled=True)  56.2 us
    all_to_all x1, waiting for transfers between devices, local(): x0f = lax.all_to_all(pooled.reshape(n_mp, rows, emb), MP, 0, 0, tiled=True)  43.3 us
    pallas_call x1, Pallas kernels, pool_rows(): pl.pallas_call(pool_kernel, grid_spec=spec, out_shape=jax.ShapeDtypeStruc...  25 us
    all_to_all x1, starting transfers between devices, local(): lax.all_to_all(jnp.broadcast_to(w_piece[None], (n_mp,) + w_piece.shape),...  11.6 us
    all_to_all x1, starting transfers between devices, local(): x0f = lax.all_to_all(pooled.reshape(n_mp, rows, emb), MP, 0, 0, tiled=True)  9.84 us
    dot_general x1, matrix products, local(): jnp.einsum('cr,fdr->fcd', dz, cd3, preferred_element_type=f32)  9.52 us
    dot_general x1, matrix products, local(): dx1 = jnp.einsum('ch,fdh->fcd', dact, w3, preferred_element_type=f32)  7.14 us
    dot_general x1, matrix products, local(): jnp.einsum('fcd,fdh->ch', x1, w3, preferred_element_type=f32) + tower_bias  6.68 us
  transfers between devices with their start and end apart: 4, of which 1 were waited for; matrix products, arithmetic and copies ran while one was open for 8% of the time, Pallas kernels for 12%

profile of v9, /device:TPU:2, one launch (start us, length us, event | category | flops | bytes accessed | tf_op | source)
XLA Modules:
  0.0 204.5 jit_solution(6850531242841016573)
XLA Ops:
  7.2 0.9 constant_dynamic-slice_fusion
  8.1 1.2 broadcast_in_dim.20
  9.3 11.6 %all-to-all-start = ((bf16[32,128,128]{2,1,0:T(8,128)(2,1)}), bf16[32,128,128]{2,1,0:T(8,128)(2,1)S(1)}, u32[]{:S(2)}, u32[]{:S(2)}) async-start(bf16[32,128,128]{2,1,0:T(8,128)(2,1)} %broadcast_in_dim.20), calls=%async_computation | async-start | bytes 2097152 | tf_op jit(solution)/shard_map/all_to_all | solution.py:109
  21.2 0.8 dynamic_slice.10
  21.9 1.3 convolution_convert_fusion
  23.2 0.7 reshape.96
  24.0 0.6 copy.20
  24.6 25.0 %shard_map.122 = bf16[8192,128]{1,0:T(8,128)(2,1)} custom-call(s32[16384]{0:T(1024)} %bitcast.106, bf16[2048,128]{1,0:T(8,128)(2,1)} %bitcast.105), custom_call_target="tpu_custom_call" | custom-call | tf_op jit(solution)/shard_map/pallas_call | solution.py:44
  49.6 1.0 copy-done.1
  50.7 9.8 %all-to-all-start.1 = ((bf16[32,256,128]{2,1,0:T(8,128)(2,1)}), bf16[32,256,128]{2,1,0:T(8,128)(2,1)}, u32[]{:S(2)}, u32[]{:S(2)}) async-start(bf16[32,256,128]{2,1,0:T(8,128)(2,1)} %bitcast.102), calls=%async_computation.1 | async-start | bytes 4194304 | tf_op jit(solution)/shard_map/all_to_all | solution.py:132
  60.5 0.2 reduce-window.4
  60.7 4.1 %copy.19 = bf16[256,4096]{0,1:T(8,128)(2,1)} copy(bf16[256,4096]{1,0:T(8,128)(2,1)} %param.18) | data formatting | bytes 4194304 | tf_op jit(solution)/shard_map/reshape | solution.py:136
  64.8 0.2 select_reduce_fusion.1
  65.0 0.1 select_reduce_fusion
  65.1 0.9 bitcast_reduce_fusion
  66.1 43.3 %all-to-all-done.1 = bf16[32,256,128]{2,1,0:T(8,128)(2,1)} async-done(((bf16[32,256,128]{2,1,0:T(8,128)(2,1)}), bf16[32,256,128]{2,1,0:T(8,128)(2,1)}, u32[]{:S(2)}, u32[]{:S(2)}) %all-to-all-start.1) | async-done | bytes 2097184 | tf_op jit(solution)/shard_map/all_to_all | solution.py:132
  109.4 6.6 %fusion.34 = f32[256,32,128]{2,0,1:T(8,128)} fusion(bf16[256,32,128]{0,2,1:T(8,128)(2,1)} %bitcast.100, bf16[32,256,128]{2,1,0:T(8,128)(2,1)} %all-to-all-done.1, bf16[32,128,256]{2,1,0:T(8,128)(2,1)S(1)} %bitcast.98), kind=kOutput, calls=%fused_computation.30 | convolution fusion | flops 1073807360 | bytes 10485760 | tf_op jit(solution)/shard_map/cr,rfd->fcd/dot_general | solution.py:139
  115.9 6.7 %fusion.13 = f32[256,1024]{1,0:T(8,128)S(1)} fusion(bf16[32,128,1024]{2,1,0:T(8,128)(2,1)} %bitcast.117, bf16[32,256,128]{2,1,0:T(8,128)(2,1)} %all-to-all-done.1, f32[256,32,128]{2,0,1:T(8,128)} %fusion.34, f32[32,128]{1,0:T(8,128)S(1)} %bitcast.108, f32[1024]{0:T(1024)S(1)} %copy-done.6), kind=kOutput, calls=%fused_computation.15 | convolution fusion | flops 2152988672 | bytes 15749120 | tf_op jit(solution)/shard_map/fcd,fdh->ch/dot_general | solution.py:141
  122.6 0.4 fusion.33
  123.1 0.4 fusion.26
  123.5 7.1 %fusion.35 = f32[32,128,256]{1,2,0:T(8,128)} fusion(bf16[32,128,1024]{2,1,0:T(8,128)(2,1)} %bitcast.118, f32[256,1024]{1,0:T(8,128)S(1)} %fusion.13, f32[256]{0:T(256)S(1)} %maximum_divide_fusion, bf16[1,8,8,128]{3,2,1,0:T(8,128)(2,1)S(1)} %bitcast.111, s32[8]{0:T(128)S(1)} %bitcast.116, s32[8]{0:T(128)S(1)} %fusion.55), kind=kOutput, calls=%fused_computation.33 | convolution fusion | flops 2154567680 | bytes 13648960 | tf_op jit(solution)/shard_map/ch,fdh->fcd/dot_general | solution.py:150
  130.7 9.5 %fusion.2 = bf16[32,256,128]{2,1,0:T(8,128)(2,1)} fusion(f32[32,128,256]{1,2,0:T(8,128)} %fusion.35, f32[256,32,128]{2,0,1:T(8,128)} %fusion.34, bf16[32,128,256]{2,1,0:T(8,128)(2,1)S(1)} %bitcast.99, f32[32,128]{1,0:T(8,128)S(1)} %bitcast.109, bf16[256,32,128]{0,2,1:T(8,128)(2,1)} %bitcast.101, bf16[32,256,128]{2,1,0:T(8,128)(2,1)} %all-to-all-done.1), kind=kOutput, calls=%fused_computation.5 | convolution fusion | flops 1082195968 | bytes 16793600 | tf_op jit(solution)/shard_map/cr,fdr->fcd/dot_general | solution.py:153
  140.2 56.2 %all_to_all.15 = bf16[32,256,128]{2,1,0:T(8,128)(2,1)S(1)} all-to-all(bf16[32,256,128]{2,1,0:T(8,128)(2,1)} %fusion.2), channel_id=1, replica_groups=mesh['y'=4,'c'=2,'z'=8,'x'=4] {'z','x'}, dimensions={0} | all-to-all | bytes 4194304 | tf_op jit(solution)/shard_map/all_to_all | solution.py:157
  196.3 1.3 copy.32
  (29 shorter events, 0.4 us)
Async XLA Ops:
  7.2 102.2 %copy-start = (bf16[4096,256]{1,0:T(8,128)(2,1)S(1)}, bf16[4096,256]{1,0:T(8,128)(2,1)}, u32[]{:S(2)}) copy-start(bf16[4096,256]{1,0:T(8,128)(2,1)} %param.17) | copy-start | bytes 6291460
  8.1 15.9 %copy-start.2 = (s32[8192,1,2]{0,2,1:T(2,128)S(1)}, s32[8192,1,2]{0,2,1:T(2,128)}, u32[]{:S(2)}) copy-start(s32[8192,1,2]{0,2,1:T(2,128)} %param.12) | copy-start | bytes 196612
  9.3 40.3 %all-to-all-start = ((bf16[32,128,128]{2,1,0:T(8,128)(2,1)}), bf16[32,128,128]{2,1,0:T(8,128)(2,1)S(1)}, u32[]{:S(2)}, u32[]{:S(2)}) async-start(bf16[32,128,128]{2,1,0:T(8,128)(2,1)} %broadcast_in_dim.20), calls=%async_computation | async-start | bytes 2097152 | tf_op jit(solution)/shard_map/all_to_all | solution.py:109
  20.9 44.2 %all-gather.5.cloned.1.call-start = ((), (), s32[]{:S(2)}) async-start(), calls=%async_computation.4 | async-start | bytes 1179648 | tf_op jit(solution)/shard_map/all_gather | solution.py:126
  23.9 92.0 %all-gather.3.cloned.1.call-start = ((), (), s32[]{:S(2)}) async-start(), calls=%async_computation.3 | async-start | bytes 9437184 | tf_op jit(solution)/shard_map/all_gather | solution.py:126
  49.6 1.0 copy-start.1
  50.7 9.9 %copy-start.7 = (s32[1,8]{1,0:T(1,128)S(1)}, s32[1,8]{1,0:T(1,128)}, u32[]{:S(2)}) copy-start(s32[1,8]{1,0:T(1,128)} %param.13) | copy-start | bytes 100
  50.7 58.7 %all-to-all-start.1 = ((bf16[32,256,128]{2,1,0:T(8,128)(2,1)}), bf16[32,256,128]{2,1,0:T(8,128)(2,1)}, u32[]{:S(2)}, u32[]{:S(2)}) async-start(bf16[32,256,128]{2,1,0:T(8,128)(2,1)} %bitcast.102), calls=%async_computation.1 | async-start | bytes 4194304 | tf_op jit(solution)/shard_map/all_to_all | solution.py:132
  60.7 4.1 %copy-start.4 = (s32[256]{0:T(256)S(1)}, s32[256]{0:T(256)}, u32[]{:S(2)}) copy-start(s32[256]{0:T(256)} %param.14) | copy-start | bytes 3076
  109.4 6.6 %copy-start.3 = (f32[4096]{0:T(1024)S(1)}, f32[4096]{0:T(1024)}, u32[]{:S(2)}) copy-start(f32[4096]{0:T(1024)} %param.19) | copy-start | bytes 49156
  109.4 6.6 %copy-start.6 = (f32[1024]{0:T(1024)S(1)}, f32[1024]{0:T(1024)}, u32[]{:S(2)}) copy-start(f32[1024]{0:T(1024)} %param.21) | copy-start | bytes 12292
  123.1 7.6 %copy-start.5 = (f32[256]{0:T(256)}, f32[256]{0:T(256)S(1)}, u32[]{:S(2)}) copy-start(f32[256]{0:T(256)S(1)} %broadcast_multiply_fusion) | copy-start | bytes 3076
Sparse Core Ops, SparseCore 0:
  24.1 26.9 all-gather.4
  52.9 56.9 all-gather.2

commit v10 on v9

--- a/solution.py
+++ b/solution.py
@@ -46,6 +46,45 @@
         grid_spec=spec,
         out_shape=jax.ShapeDtypeStruct((count, emb), slab.dtype),
     )(flat_ids, slab)
+
+
+def back_kernel(dx1_ref, x0_ref, cross_ref, up_ref, down_ref, out_ref):
+    feats, _, emb = dx1_ref.shape
+    contract = (((1,), (1,)), ((), ()))
+
+    def down_pass(f, acc):
+        cols = pl.ds(pl.multiple_of(f * emb, emb), emb)
+        dcross = (dx1_ref[f] * x0_ref[f].astype(jnp.float32)).astype(jnp.bfloat16)
+        return acc + lax.dot_general(
+            dcross, up_ref[:, cols], contract, preferred_element_type=jnp.float32
+        )
+
+    acc = jnp.zeros((dx1_ref.shape[1], up_ref.shape[0]), jnp.float32)
+    dz = lax.fori_loop(0, feats, down_pass, acc).astype(jnp.bfloat16)
+
+    def up_pass(f, carry):
+        rows = pl.ds(pl.multiple_of(f * emb, emb), emb)
+        back = lax.dot_general(
+            dz, down_ref[rows, :], contract, preferred_element_type=jnp.float32
+        )
+        out_ref[f] = (dx1_ref[f] * (1.0 + cross_ref[f]) + back).astype(out_ref.dtype)
+        return carry
+
+    lax.fori_loop(0, feats, up_pass, 0)
+
+
+def back_rows(dx1, x0f, cross, cross_up, cross_down, blk=128):
+    feats, rows, emb = dx1.shape
+    part = pl.BlockSpec((feats, blk, emb), lambda i: (0, i, 0))
+    whole_up = pl.BlockSpec(cross_up.shape, lambda i: (0, 0))
+    whole_down = pl.BlockSpec(cross_down.shape, lambda i: (0, 0))
+    return pl.pallas_call(
+        back_kernel,
+        grid=(rows // blk,),
+        in_specs=[part, part, part, whole_up, whole_down],
+        out_specs=part,
+        out_shape=jax.ShapeDtypeStruct(dx1.shape, jnp.bfloat16),
+    )(dx1, x0f, cross, cross_up, cross_down)
 
 
 def members(counts_row, rows):
@@ -148,12 +187,7 @@
     slope = sig * (1.0 + act * (1.0 - sig))
     dact = (dscore[:, None] * code * scale * slope).astype(bf16)
     dx1 = jnp.einsum("ch,fdh->fcd", dact, w3, preferred_element_type=f32)
-    dcross = (dx1 * x0f).astype(bf16)
-    dz = jnp.einsum("fcd,rfd->cr", dcross, cu3, preferred_element_type=f32).astype(bf16)
-    dx0 = dx1 * (1.0 + cross) + jnp.einsum(
-        "cr,fdr->fcd", dz, cd3, preferred_element_type=f32
-    )
-    grads = dx0.astype(bf16)
+    grads = back_rows(dx1, x0f, cross, cross_up, cross_down)
     returned = lax.all_to_all(grads, MP, 0, 0, tiled=True)
     return (score, returned.reshape(n_mp * rows, 1, emb))
 

time: 205 us -> 223 us (1.088)
  Pallas kernels: 25 us -> 51.8 us
  matrix products: 32 us -> 21.6 us
  waiting for transfers between devices: 43.3 us -> 47.8 us
  local copies, waits for them, and re-layouts: 10.8 us -> 7.98 us
    pallas_call x0 -> x1, Pallas kernels: none -> 26.8 us  [back_rows(): pl.pallas_call(back_kernel, grid=(rows // blk,), in_specs=[part, part, pa...]
    dot_general x1 -> x0, matrix products: 9.52 us -> none  [local(): jnp.einsum('cr,fdr->fcd', dz, cd3, preferred_element_type=f32)]
    reshape x1 -> x0, local copies, waits for them, and re-layouts: 4.08 us -> none  [local(): cu3 = cross_up.reshape(rank, n_mp, emb)]
    all_to_all x1, waiting for transfers between devices: 43.3 us -> 47.4 us  [local(): x0f = lax.all_to_all(pooled.reshape(n_mp, rows, emb), MP, 0, 0, tiled=True)]
  transfers between devices with their start and end apart: 4 -> 4, of which waited for: 1 -> 2; matrix products, arithmetic and copies ran while one was open for 8% -> 5% of each run, Pallas kernels for 12% -> 11%
where the time goes in v10:
time: 223 us; the launch traced here: 222 us
  blocking collectives  56 us (25%)
  Pallas kernels  51.8 us (23%)
  waiting for transfers between devices  47.8 us (21%)
  matrix products  21.6 us (10%)
  starting transfers between devices  21.2 us (10%)
  between operations  14.2 us (6%)
  local copies, waits for them, and re-layouts  7.98 us (4%)
    all_to_all x1, blocking collectives, local(): returned = lax.all_to_all(grads, MP, 0, 0, tiled=True)  56 us
    all_to_all x1, waiting for transfers between devices, local(): x0f = lax.all_to_all(pooled.reshape(n_mp, rows, emb), MP, 0, 0, tiled=True)  47.4 us
    pallas_call x1, Pallas kernels, back_rows(): pl.pallas_call(back_kernel, grid=(rows // blk,), in_specs=[part, part, pa...  26.8 us
    pallas_call x1, Pallas kernels, pool_rows(): pl.pallas_call(pool_kernel, grid_spec=spec, out_shape=jax.ShapeDtypeStruc...  25 us
    all_to_all x1, starting transfers between devices, local(): lax.all_to_all(jnp.broadcast_to(w_piece[None], (n_mp,) + w_piece.shape),...  11.6 us
    all_to_all x1, starting transfers between devices, local(): x0f = lax.all_to_all(pooled.reshape(n_mp, rows, emb), MP, 0, 0, tiled=True)  9.48 us
    dot_general x1, matrix products, local(): jnp.einsum('cr,rfd->fcd', z, cu3, preferred_element_type=f32) + bias3  7.31 us
    dot_general x1, matrix products, local(): dx1 = jnp.einsum('ch,fdh->fcd', dact, w3, preferred_element_type=f32)  7.12 us
  transfers between devices with their start and end apart: 4, of which 2 were waited for; matrix products, arithmetic and copies ran while one was open for 5% of the time, Pallas kernels for 11%

profile of v10, /device:TPU:2, one launch (start us, length us, event | category | flops | bytes accessed | tf_op | source)
XLA Modules:
  0.0 222.0 jit_solution(15905622523039597873)
XLA Ops:
  7.2 0.8 constant_dynamic-slice_fusion
  8.0 1.2 broadcast_in_dim.20
  9.2 11.6 %all-to-all-start = ((bf16[32,128,128]{2,1,0:T(8,128)(2,1)}), bf16[32,128,128]{2,1,0:T(8,128)(2,1)S(1)}, u32[]{:S(2)}, u32[]{:S(2)}) async-start(bf16[32,128,128]{2,1,0:T(8,128)(2,1)} %broadcast_in_dim.20), calls=%async_computation | async-start | bytes 2097152 | tf_op jit(solution)/shard_map/all_to_all | solution.py:148
  21.1 0.8 dynamic_slice.10
  21.8 0.2 convolution_convert_fusion
  22.1 0.7 reshape.96
  22.9 0.6 copy.19
  23.5 25.0 %shard_map.122 = bf16[8192,128]{1,0:T(8,128)(2,1)} custom-call(s32[16384]{0:T(1024)} %bitcast.70, bf16[2048,128]{1,0:T(8,128)(2,1)} %bitcast.69), custom_call_target="tpu_custom_call" | custom-call | tf_op jit(solution)/shard_map/pallas_call | solution.py:44
  48.5 0.4 all-to-all-done
  48.9 1.0 copy-done.2
  50.0 9.5 %all-to-all-start.1 = ((bf16[32,256,128]{2,1,0:T(8,128)(2,1)}), bf16[32,256,128]{2,1,0:T(8,128)(2,1)S(1)}, u32[]{:S(2)}, u32[]{:S(2)}) async-start(bf16[32,256,128]{2,1,0:T(8,128)(2,1)} %bitcast.65), calls=%async_computation.1 | async-start | bytes 4194304 | tf_op jit(solution)/shard_map/all_to_all | solution.py:171
  59.7 0.2 select_reduce_fusion.1
  60.0 0.9 bitcast_reduce_fusion
  60.9 47.4 %all-to-all-done.1.x0_ref = bf16[32,256,128]{2,1,0:T(8,128)(2,1)S(1)} async-done(((bf16[32,256,128]{2,1,0:T(8,128)(2,1)}), bf16[32,256,128]{2,1,0:T(8,128)(2,1)S(1)}, u32[]{:S(2)}, u32[]{:S(2)}) %all-to-all-start.1) | async-done | bytes 2097184 | tf_op jit(solution)/shard_map/all_to_all | solution.py:171
  108.3 7.3 %add_bitcast_fusion.cross_ref = f32[32,256,128]{2,1,0:T(8,128)} fusion(f32[32,128]{1,0:T(8,128)S(1)} %bitcast.72, bf16[32,256,128]{2,1,0:T(8,128)(2,1)S(1)} %all-to-all-done.1.x0_ref, bf16[32,128,256]{2,1,0:T(8,128)(2,1)} %bitcast.67, bf16[256,4096]{1,0:T(8,128)(2,1)} %up_ref.1), kind=kOutput, calls=%fused_computation.2 | convolution fusion | flops 1074855936 | bytes 10502144 | tf_op jit(solution)/shard_map/cr,rfd->fcd/dot_general | solution.py:178
  115.6 6.1 %fusion.10 = f32[256,1024]{1,0:T(8,128)S(1)} fusion(bf16[32,128,1024]{2,1,0:T(8,128)(2,1)} %bitcast.80, f32[32,256,128]{2,1,0:T(8,128)} %add_bitcast_fusion.cross_ref, bf16[32,256,128]{2,1,0:T(8,128)(2,1)S(1)} %all-to-all-done.1.x0_ref, f32[1024]{0:T(1024)S(1)} %copy-done.7), kind=kOutput, calls=%fused_computation.11 | convolution fusion | flops 2151940096 | bytes 15732736 | tf_op jit(solution)/shard_map/fcd,fdh->ch/dot_general | solution.py:180
  121.7 0.4 fusion.19
  122.1 0.6 copy-done.9
  122.7 0.4 fusion.17
  123.1 0.8 copy-done.10
  123.9 7.1 %convolution_bitcast_fusion.dx1_ref = f32[32,256,128]{2,1,0:T(8,128)} fusion(bf16[32,128,1024]{2,1,0:T(8,128)(2,1)} %bitcast.81, f32[256,1024]{1,0:T(8,128)S(1)} %copy-done.10, f32[256]{0:T(256)S(1)} %maximum_divide_fusion, bf16[1,8,8,128]{3,2,1,0:T(8,128)(2,1)S(1)} %bitcast.74, s32[8]{0:T(128)S(1)} %bitcast.79, s32[8]{0:T(128)S(1)} %fusion.39), kind=kOutput, calls=%fused_computation.3 | convolution fusion | flops 2154567680 | bytes 13648960 | tf_op jit(solution)/shard_map/ch,fdh->fcd/dot_general | solution.py:189
  131.0 26.8 %shard_map.123 = bf16[32,256,128]{2,1,0:T(8,128)(2,1)} custom-call(f32[32,256,128]{2,1,0:T(8,128)} %convolution_bitcast_fusion.dx1_ref, bf16[32,256,128]{2,1,0:T(8,128)(2,1)} %copy-done.1, f32[32,256,128]{2,1,0:T(8,128)} %add_bitcast_fusion.cross_ref, bf16[256,4096]{1,0:T(8,128)(2,1)} %up_ref.1, bf16[4096,256]{1,0:T(8,128)(2,1)} %down_ref.1), custom_call_target="tpu_custom_call" | custom-call | tf_op jit(solution)/shard_map/pallas_call | solution.py:81
  157.9 56.0 %all_to_all.15 = bf16[32,256,128]{2,1,0:T(8,128)(2,1)S(1)} all-to-all(bf16[32,256,128]{2,1,0:T(8,128)(2,1)} %shard_map.123), channel_id=1, replica_groups=mesh['y'=4,'c'=2,'z'=8,'x'=4] {'z','x'}, dimensions={0} | all-to-all | bytes 4194304 | tf_op jit(solution)/shard_map/all_to_all | solution.py:191
  213.9 1.3 copy.35
  (34 shorter events, 0.6 us)
Async XLA Ops:
  7.2 14.7 %copy-start = (bf16[256,1024]{1,0:T(8,128)(2,1)S(1)}, bf16[256,1024]{1,0:T(8,128)(2,1)}, u32[]{:S(2)}) copy-start(bf16[256,1024]{1,0:T(8,128)(2,1)} %param.16) | copy-start | bytes 1572868
  8.0 14.8 %copy-start.3 = (s32[8192,1,2]{0,2,1:T(2,128)S(1)}, s32[8192,1,2]{0,2,1:T(2,128)}, u32[]{:S(2)}) copy-start(s32[8192,1,2]{0,2,1:T(2,128)} %param.12) | copy-start | bytes 196612
  9.2 39.7 %all-to-all-start = ((bf16[32,128,128]{2,1,0:T(8,128)(2,1)}), bf16[32,128,128]{2,1,0:T(8,128)(2,1)S(1)}, u32[]{:S(2)}, u32[]{:S(2)}) async-start(bf16[32,128,128]{2,1,0:T(8,128)(2,1)} %broadcast_in_dim.20), calls=%async_computation | async-start | bytes 2097152 | tf_op jit(solution)/shard_map/all_to_all | solution.py:148
  20.8 39.1 %all-gather.5.cloned.1.call-start = ((), (), s32[]{:S(2)}) async-start(), calls=%async_computation.4 | async-start | bytes 1179648 | tf_op jit(solution)/shard_map/all_gather | solution.py:165
  22.8 92.8 %all-gather.3.cloned.1.call-start = ((), (), s32[]{:S(2)}) async-start(), calls=%async_computation.3 | async-start | bytes 9437184 | tf_op jit(solution)/shard_map/all_gather | solution.py:165
  48.9 1.0 copy-start.2
  50.0 9.5 %copy-start.8 = (s32[1,8]{1,0:T(1,128)S(1)}, s32[1,8]{1,0:T(1,128)}, u32[]{:S(2)}) copy-start(s32[1,8]{1,0:T(1,128)} %param.13) | copy-start | bytes 100
  50.0 9.7 %copy-start.5 = (s32[256]{0:T(256)S(1)}, s32[256]{0:T(256)}, u32[]{:S(2)}) copy-start(s32[256]{0:T(256)} %param.14) | copy-start | bytes 3076
  50.0 58.3 %copy-start.4 = (f32[4096]{0:T(1024)S(1)}, f32[4096]{0:T(1024)}, u32[]{:S(2)}) copy-start(f32[4096]{0:T(1024)} %param.19) | copy-start | bytes 49156
  50.0 58.3 %all-to-all-start.1 = ((bf16[32,256,128]{2,1,0:T(8,128)(2,1)}), bf16[32,256,128]{2,1,0:T(8,128)(2,1)S(1)}, u32[]{:S(2)}, u32[]{:S(2)}) async-start(bf16[32,256,128]{2,1,0:T(8,128)(2,1)} %bitcast.65), calls=%async_computation.1 | async-start | bytes 4194304 | tf_op jit(solution)/shard_map/all_to_all | solution.py:171
  108.3 7.3 %copy-start.1 = (bf16[32,256,128]{2,1,0:T(8,128)(2,1)}, bf16[32,256,128]{2,1,0:T(8,128)(2,1)S(1)}, u32[]{:S(2)}) copy-start(bf16[32,256,128]{2,1,0:T(8,128)(2,1)S(1)} %all-to-all-done.1.x0_ref) | copy-start | bytes 6291460
  108.3 7.3 %copy-start.7 = (f32[1024]{0:T(1024)S(1)}, f32[1024]{0:T(1024)}, u32[]{:S(2)}) copy-start(f32[1024]{0:T(1024)} %param.21) | copy-start | bytes 12292
  121.7 1.0 copy-start.9
  122.7 8.4 %copy-start.6 = (f32[256]{0:T(256)}, f32[256]{0:T(256)S(1)}, u32[]{:S(2)}) copy-start(f32[256]{0:T(256)S(1)} %broadcast_multiply_fusion) | copy-start | bytes 3076
  122.7 1.2 copy-start.10
Sparse Core Ops, SparseCore 0:
  23.5 26.9 all-gather.4
  52.3 56.9 all-gather.2

commit v11 on v10

--- a/solution.py
+++ b/solution.py
@@ -50,23 +50,18 @@
 
 def back_kernel(dx1_ref, x0_ref, cross_ref, up_ref, down_ref, out_ref):
     feats, _, emb = dx1_ref.shape
-    contract = (((1,), (1,)), ((), ()))
 
     def down_pass(f, acc):
+        rows = pl.ds(pl.multiple_of(f * emb, emb), emb)
+        dcross = (dx1_ref[f] * x0_ref[f].astype(jnp.float32)).astype(jnp.bfloat16)
+        return acc + jnp.dot(dcross, up_ref[rows, :], preferred_element_type=jnp.float32)
+
+    acc = jnp.zeros((dx1_ref.shape[1], up_ref.shape[1]), jnp.float32)
+    dz = lax.fori_loop(0, feats, down_pass, acc).astype(jnp.bfloat16)
+
+    def up_pass(f, carry):
         cols = pl.ds(pl.multiple_of(f * emb, emb), emb)
-        dcross = (dx1_ref[f] * x0_ref[f].astype(jnp.float32)).astype(jnp.bfloat16)
-        return acc + lax.dot_general(
-            dcross, up_ref[:, cols], contract, preferred_element_type=jnp.float32
-        )
-
-    acc = jnp.zeros((dx1_ref.shape[1], up_ref.shape[0]), jnp.float32)
-    dz = lax.fori_loop(0, feats, down_pass, acc).astype(jnp.bfloat16)
-
-    def up_pass(f, carry):
-        rows = pl.ds(pl.multiple_of(f * emb, emb), emb)
-        back = lax.dot_general(
-            dz, down_ref[rows, :], contract, preferred_element_type=jnp.float32
-        )
+        back = jnp.dot(dz, down_ref[:, cols], preferred_element_type=jnp.float32)
         out_ref[f] = (dx1_ref[f] * (1.0 + cross_ref[f]) + back).astype(out_ref.dtype)
         return carry
 
@@ -187,7 +182,7 @@
     slope = sig * (1.0 + act * (1.0 - sig))
     dact = (dscore[:, None] * code * scale * slope).astype(bf16)
     dx1 = jnp.einsum("ch,fdh->fcd", dact, w3, preferred_element_type=f32)
-    grads = back_rows(dx1, x0f, cross, cross_up, cross_down)
+    grads = back_rows(dx1, x0f, cross, cross_up.T, cross_down.T)
     returned = lax.all_to_all(grads, MP, 0, 0, tiled=True)
     return (score, returned.reshape(n_mp * rows, 1, emb))
 

time: 223 us -> 221 us (level)
  local copies, waits for them, and re-layouts: 7.98 us -> 16.4 us
  waiting for transfers between devices: 47.8 us -> 39.5 us
    all_to_all x1, waiting for transfers between devices: 47.4 us -> 39 us  [local(): x0f = lax.all_to_all(pooled.reshape(n_mp, rows, emb), MP, 0, 0, tiled=True)]
    unnamed x24 -> x26, local copies, waits for them, and re-layouts: 4.4 us -> 12.8 us
  transfers between devices with their start and end apart: 4 -> 4, of which waited for: 2 -> 2; matrix products, arithmetic and copies ran while one was open for 5% -> 9% of each run, Pallas kernels for 11% -> 11%
where the time goes in v11:
time: 221 us; the launch traced here: 220 us
  blocking collectives  56.1 us (25%)
  Pallas kernels  49.7 us (22%)
  waiting for transfers between devices  39.5 us (18%)
  matrix products  21.6 us (10%)
  starting transfers between devices  21 us (10%)
  local copies, waits for them, and re-layouts  16.4 us (7%)
  between operations  14.2 us (6%)
    all_to_all x1, blocking collectives, local(): returned = lax.all_to_all(grads, MP, 0, 0, tiled=True)  56.1 us
    all_to_all x1, waiting for transfers between devices, local(): x0f = lax.all_to_all(pooled.reshape(n_mp, rows, emb), MP, 0, 0, tiled=True)  39 us
    pallas_call x1, Pallas kernels, pool_rows(): pl.pallas_call(pool_kernel, grid_spec=spec, out_shape=jax.ShapeDtypeStruc...  25 us
    pallas_call x1, Pallas kernels, back_rows(): pl.pallas_call(back_kernel, grid=(rows // blk,), in_specs=[part, part, pa...  24.8 us
    unnamed x26, local copies, waits for them, and re-layouts  12.8 us
    all_to_all x1, starting transfers between devices, local(): lax.all_to_all(jnp.broadcast_to(w_piece[None], (n_mp,) + w_piece.shape),...  11.6 us
    all_to_all x1, starting transfers between devices, local(): x0f = lax.all_to_all(pooled.reshape(n_mp, rows, emb), MP, 0, 0, tiled=True)  9.35 us
    dot_general x1, matrix products, local(): jnp.einsum('cr,rfd->fcd', z, cu3, preferred_element_type=f32) + bias3  7.31 us
  transfers between devices with their start and end apart: 4, of which 2 were waited for; matrix products, arithmetic and copies ran while one was open for 9% of the time, Pallas kernels for 11%

profile of v11, /device:TPU:2, one launch (start us, length us, event | category | flops | bytes accessed | tf_op | source)
XLA Modules:
  0.0 219.9 jit_solution(9054724180118858724)
XLA Ops:
  7.2 0.8 constant_dynamic-slice_fusion
  8.0 1.2 broadcast_in_dim.20
  9.2 11.6 %all-to-all-start = ((bf16[32,128,128]{2,1,0:T(8,128)(2,1)}), bf16[32,128,128]{2,1,0:T(8,128)(2,1)S(1)}, u32[]{:S(2)}, u32[]{:S(2)}) async-start(bf16[32,128,128]{2,1,0:T(8,128)(2,1)} %broadcast_in_dim.20), calls=%async_computation | async-start | bytes 2097152 | tf_op jit(solution)/shard_map/all_to_all | solution.py:143
  21.1 0.8 dynamic_slice.10
  22.1 0.7 reshape.96
  22.9 0.6 copy.23
  23.5 25.0 %shard_map.122 = bf16[8192,128]{1,0:T(8,128)(2,1)} custom-call(s32[16384]{0:T(1024)} %bitcast.74, bf16[2048,128]{1,0:T(8,128)(2,1)} %bitcast.73), custom_call_target="tpu_custom_call" | custom-call | tf_op jit(solution)/shard_map/pallas_call | solution.py:44
  48.5 0.4 all-to-all-done
  48.9 1.0 copy-done.2
  50.0 9.3 %all-to-all-start.1 = ((bf16[32,256,128]{2,1,0:T(8,128)(2,1)}), bf16[32,256,128]{2,1,0:T(8,128)(2,1)S(1)}, u32[]{:S(2)}, u32[]{:S(2)}) async-start(bf16[32,256,128]{2,1,0:T(8,128)(2,1)} %bitcast.68), calls=%async_computation.1 | async-start | bytes 4194304 | tf_op jit(solution)/shard_map/all_to_all | solution.py:166
  59.5 4.1 %copy.19 = bf16[256,4096]{0,1:T(8,128)(2,1)} copy(bf16[256,4096]{1,0:T(8,128)(2,1)} %param.18) | data formatting | bytes 4194304 | tf_op args[7]
  63.6 4.3 %copy.20 = bf16[4096,256]{0,1:T(8,128)(2,1)} copy(bf16[4096,256]{1,0:T(8,128)(2,1)} %param.17) | data formatting | bytes 4194304 | tf_op args[6]
  68.2 0.9 bitcast_reduce_fusion
  69.1 39.0 %all-to-all-done.1.x0_ref = bf16[32,256,128]{2,1,0:T(8,128)(2,1)S(1)} async-done(((bf16[32,256,128]{2,1,0:T(8,128)(2,1)}), bf16[32,256,128]{2,1,0:T(8,128)(2,1)S(1)}, u32[]{:S(2)}, u32[]{:S(2)}) %all-to-all-start.1) | async-done | bytes 2097184 | tf_op jit(solution)/shard_map/all_to_all | solution.py:166
  108.1 7.3 %add_bitcast_fusion.cross_ref = f32[32,256,128]{2,1,0:T(8,128)} fusion(f32[32,128]{1,0:T(8,128)S(1)} %bitcast.76, bf16[32,256,128]{2,1,0:T(8,128)(2,1)S(1)} %all-to-all-done.1.x0_ref, bf16[32,128,256]{2,1,0:T(8,128)(2,1)} %bitcast.67, bf16[256,4096]{1,0:T(8,128)(2,1)} %param.18), kind=kOutput, calls=%fused_computation.2 | convolution fusion | flops 1074855936 | bytes 10502144 | tf_op jit(solution)/shard_map/cr,rfd->fcd/dot_general | solution.py:173
  115.4 6.1 %fusion.10 = f32[256,1024]{1,0:T(8,128)S(1)} fusion(bf16[32,128,1024]{2,1,0:T(8,128)(2,1)} %bitcast.84, f32[32,256,128]{2,1,0:T(8,128)} %add_bitcast_fusion.cross_ref, bf16[32,256,128]{2,1,0:T(8,128)(2,1)S(1)} %all-to-all-done.1.x0_ref, f32[1024]{0:T(1024)S(1)} %copy-done.7), kind=kOutput, calls=%fused_computation.11 | convolution fusion | flops 2151940096 | bytes 15732736 | tf_op jit(solution)/shard_map/fcd,fdh->ch/dot_general | solution.py:175
  121.5 0.4 fusion.19
  121.9 0.6 copy-done.9
  122.5 0.4 fusion.17
  123.0 0.8 copy-done.10
  123.8 7.1 %convolution_bitcast_fusion.dx1_ref = f32[32,256,128]{2,1,0:T(8,128)} fusion(bf16[32,128,1024]{2,1,0:T(8,128)(2,1)} %bitcast.85, f32[256,1024]{1,0:T(8,128)S(1)} %copy-done.10, f32[256]{0:T(256)S(1)} %maximum_divide_fusion, bf16[1,8,8,128]{3,2,1,0:T(8,128)(2,1)S(1)} %bitcast.78, s32[8]{0:T(128)S(1)} %bitcast.83, s32[8]{0:T(128)S(1)} %fusion.39), kind=kOutput, calls=%fused_computation.3 | convolution fusion | flops 2154567680 | bytes 13648960 | tf_op jit(solution)/shard_map/ch,fdh->fcd/dot_general | solution.py:184
  130.9 24.8 %shard_map.123 = bf16[32,256,128]{2,1,0:T(8,128)(2,1)} custom-call(f32[32,256,128]{2,1,0:T(8,128)} %convolution_bitcast_fusion.dx1_ref, bf16[32,256,128]{2,1,0:T(8,128)(2,1)} %copy-done.1, f32[32,256,128]{2,1,0:T(8,128)} %add_bitcast_fusion.cross_ref, bf16[4096,256]{1,0:T(8,128)(2,1)} %bitcast.70, bf16[256,4096]{1,0:T(8,128)(2,1)} %bitcast.71), custom_call_target="tpu_custom_call" | custom-call | tf_op jit(solution)/shard_map/pallas_call | solution.py:76
  155.7 56.1 %all_to_all.15 = bf16[32,256,128]{2,1,0:T(8,128)(2,1)S(1)} all-to-all(bf16[32,256,128]{2,1,0:T(8,128)(2,1)} %shard_map.123), channel_id=1, replica_groups=mesh['y'=4,'c'=2,'z'=8,'x'=4] {'z','x'}, dimensions={0} | all-to-all | bytes 4194304 | tf_op jit(solution)/shard_map/all_to_all | solution.py:186
  211.7 1.3 copy.39
  (36 shorter events, 1.0 us)
Async XLA Ops:
  7.2 14.7 %copy-start = (bf16[256,1024]{1,0:T(8,128)(2,1)S(1)}, bf16[256,1024]{1,0:T(8,128)(2,1)}, u32[]{:S(2)}) copy-start(bf16[256,1024]{1,0:T(8,128)(2,1)} %param.16) | copy-start | bytes 1572868
  8.0 14.8 %copy-start.3 = (s32[8192,1,2]{0,2,1:T(2,128)S(1)}, s32[8192,1,2]{0,2,1:T(2,128)}, u32[]{:S(2)}) copy-start(s32[8192,1,2]{0,2,1:T(2,128)} %param.12) | copy-start | bytes 196612
  9.2 39.7 %all-to-all-start = ((bf16[32,128,128]{2,1,0:T(8,128)(2,1)}), bf16[32,128,128]{2,1,0:T(8,128)(2,1)S(1)}, u32[]{:S(2)}, u32[]{:S(2)}) async-start(bf16[32,128,128]{2,1,0:T(8,128)(2,1)} %broadcast_in_dim.20), calls=%async_computation | async-start | bytes 2097152 | tf_op jit(solution)/shard_map/all_to_all | solution.py:143
  20.8 47.4 %all-gather.5.cloned.1.call-start = ((), (), s32[]{:S(2)}) async-start(), calls=%async_computation.4 | async-start | bytes 1179648 | tf_op jit(solution)/shard_map/all_gather | solution.py:160
  22.8 92.6 %all-gather.3.cloned.1.call-start = ((), (), s32[]{:S(2)}) async-start(), calls=%async_computation.3 | async-start | bytes 9437184 | tf_op jit(solution)/shard_map/all_gather | solution.py:160
  48.9 1.0 copy-start.2
  50.0 9.4 %copy-start.8 = (s32[1,8]{1,0:T(1,128)S(1)}, s32[1,8]{1,0:T(1,128)}, u32[]{:S(2)}) copy-start(s32[1,8]{1,0:T(1,128)} %param.13) | copy-start | bytes 100
  50.0 58.1 %all-to-all-start.1 = ((bf16[32,256,128]{2,1,0:T(8,128)(2,1)}), bf16[32,256,128]{2,1,0:T(8,128)(2,1)S(1)}, u32[]{:S(2)}, u32[]{:S(2)}) async-start(bf16[32,256,128]{2,1,0:T(8,128)(2,1)} %bitcast.68), calls=%async_computation.1 | async-start | bytes 4194304 | tf_op jit(solution)/shard_map/all_to_all | solution.py:166
  63.6 4.3 %copy-start.5 = (s32[256]{0:T(256)S(1)}, s32[256]{0:T(256)}, u32[]{:S(2)}) copy-start(s32[256]{0:T(256)} %param.14) | copy-start | bytes 3076
  63.6 44.5 %copy-start.4 = (f32[4096]{0:T(1024)S(1)}, f32[4096]{0:T(1024)}, u32[]{:S(2)}) copy-start(f32[4096]{0:T(1024)} %param.19) | copy-start | bytes 49156
  108.1 7.3 %copy-start.1 = (bf16[32,256,128]{2,1,0:T(8,128)(2,1)}, bf16[32,256,128]{2,1,0:T(8,128)(2,1)S(1)}, u32[]{:S(2)}) copy-start(bf16[32,256,128]{2,1,0:T(8,128)(2,1)S(1)} %all-to-all-done.1.x0_ref) | copy-start | bytes 6291460
  108.1 7.3 %copy-start.7 = (f32[1024]{0:T(1024)S(1)}, f32[1024]{0:T(1024)}, u32[]{:S(2)}) copy-start(f32[1024]{0:T(1024)} %param.21) | copy-start | bytes 12292
  121.5 1.0 copy-start.9
  122.5 8.4 %copy-start.6 = (f32[256]{0:T(256)}, f32[256]{0:T(256)S(1)}, u32[]{:S(2)}) copy-start(f32[256]{0:T(256)S(1)} %broadcast_multiply_fusion) | copy-start | bytes 3076
  122.5 1.2 copy-start.10
Sparse Core Ops, SparseCore 0:
  23.5 26.9 all-gather.4
  52.3 56.9 all-gather.2

commit v12 on v9

--- a/solution.py
+++ b/solution.py
@@ -136,8 +136,9 @@
     cu3 = cross_up.reshape(rank, n_mp, emb)
     bias3 = cross_bias.reshape(n_mp, 1, emb)
     z = jnp.einsum("fcd,fdr->cr", x0f, cd3, preferred_element_type=f32).astype(bf16)
-    cross = jnp.einsum("cr,rfd->fcd", z, cu3, preferred_element_type=f32) + bias3
-    x1 = (x0f * cross + x0f).astype(bf16)
+    cross = (jnp.einsum("cr,rfd->fcd", z, cu3, preferred_element_type=f32) + bias3).astype(bf16)
+    x0w = x0f.astype(f32)
+    x1 = (x0w * cross.astype(f32) + x0w).astype(bf16)
     act = jnp.einsum("fcd,fdh->ch", x1, w3, preferred_element_type=f32) + tower_bias
     sig = jax.nn.sigmoid(act)
     hidden = (act * sig).astype(bf16)
@@ -147,10 +148,11 @@
     code = jnp.dot(member.astype(bf16), user_seg, preferred_element_type=f32)
     slope = sig * (1.0 + act * (1.0 - sig))
     dact = (dscore[:, None] * code * scale * slope).astype(bf16)
-    dx1 = jnp.einsum("ch,fdh->fcd", dact, w3, preferred_element_type=f32)
-    dcross = (dx1 * x0f).astype(bf16)
+    dx1 = jnp.einsum("ch,fdh->fcd", dact, w3, preferred_element_type=f32).astype(bf16)
+    dx1 = dx1.astype(f32)
+    dcross = (dx1 * x0w).astype(bf16)
     dz = jnp.einsum("fcd,rfd->cr", dcross, cu3, preferred_element_type=f32).astype(bf16)
-    dx0 = dx1 * (1.0 + cross) + jnp.einsum(
+    dx0 = dx1 * (1.0 + cross.astype(f32)) + jnp.einsum(
         "cr,fdr->fcd", dz, cd3, preferred_element_type=f32
     )
     grads = dx0.astype(bf16)

time: 205 us -> 202 us (0.985)
  matrix products: 32 us -> 28.6 us
  transfers between devices with their start and end apart: 4 -> 4, of which waited for: 1 -> 1; matrix products, arithmetic and copies ran while one was open for 8% -> 7% of each run, Pallas kernels for 12% -> 12%
where the time goes in v12:
time: 202 us; the launch traced here: 201 us
  blocking collectives  56.2 us (28%)
  waiting for transfers between devices  43.3 us (21%)
  matrix products  28.6 us (14%)
  Pallas kernels  25 us (12%)
  starting transfers between devices  21.5 us (11%)
  between operations  14.2 us (7%)
  local copies, waits for them, and re-layouts  10.7 us (5%)
    all_to_all x1, blocking collectives, local(): returned = lax.all_to_all(grads, MP, 0, 0, tiled=True)  56.2 us
    all_to_all x1, waiting for transfers between devices, local(): x0f = lax.all_to_all(pooled.reshape(n_mp, rows, emb), MP, 0, 0, tiled=True)  43.3 us
    pallas_call x1, Pallas kernels, pool_rows(): pl.pallas_call(pool_kernel, grid_spec=spec, out_shape=jax.ShapeDtypeStruc...  25 us
    all_to_all x1, starting transfers between devices, local(): lax.all_to_all(jnp.broadcast_to(w_piece[None], (n_mp,) + w_piece.shape),...  11.6 us
    all_to_all x1, starting transfers between devices, local(): x0f = lax.all_to_all(pooled.reshape(n_mp, rows, emb), MP, 0, 0, tiled=True)  9.84 us
    dot_general x1, matrix products, local(): jnp.einsum('cr,fdr->fcd', dz, cd3, preferred_element_type=f32)  7.74 us
    dot_general x1, matrix products, local(): jnp.einsum('ch,fdh->fcd', dact, w3, preferred_element_type=f32).astype(bf16)  6.79 us
    dot_general x1, matrix products, local(): jnp.einsum('fcd,fdh->ch', x1, w3, preferred_element_type=f32) + tower_bias  6.04 us
  transfers between devices with their start and end apart: 4, of which 1 were waited for; matrix products, arithmetic and copies ran while one was open for 7% of the time, Pallas kernels for 12%

profile of v12, /device:TPU:2, one launch (start us, length us, event | category | flops | bytes accessed | tf_op | source)
XLA Modules:
  0.0 201.0 jit_solution(1923765959502489707)
XLA Ops:
  7.2 0.9 constant_dynamic-slice_fusion
  8.1 1.2 broadcast_in_dim.20
  9.3 11.6 %all-to-all-start = ((bf16[32,128,128]{2,1,0:T(8,128)(2,1)}), bf16[32,128,128]{2,1,0:T(8,128)(2,1)S(1)}, u32[]{:S(2)}, u32[]{:S(2)}) async-start(bf16[32,128,128]{2,1,0:T(8,128)(2,1)} %broadcast_in_dim.20), calls=%async_computation | async-start | bytes 2097152 | tf_op jit(solution)/shard_map/all_to_all | solution.py:109
  21.2 0.8 dynamic_slice.10
  21.9 1.3 convolution_convert_fusion.1
  23.2 0.7 reshape.96
  24.0 0.6 copy.20
  24.6 25.0 %shard_map.122 = bf16[8192,128]{1,0:T(8,128)(2,1)} custom-call(s32[16384]{0:T(1024)} %bitcast.106, bf16[2048,128]{1,0:T(8,128)(2,1)} %bitcast.105), custom_call_target="tpu_custom_call" | custom-call | tf_op jit(solution)/shard_map/pallas_call | solution.py:44
  49.6 1.0 copy-done.1
  50.6 9.8 %all-to-all-start.1 = ((bf16[32,256,128]{2,1,0:T(8,128)(2,1)}), bf16[32,256,128]{2,1,0:T(8,128)(2,1)}, u32[]{:S(2)}, u32[]{:S(2)}) async-start(bf16[32,256,128]{2,1,0:T(8,128)(2,1)} %bitcast.100), calls=%async_computation.1 | async-start | bytes 4194304 | tf_op jit(solution)/shard_map/all_to_all | solution.py:132
  60.5 0.2 reduce-window.4
  60.6 4.1 %copy.19 = bf16[256,4096]{0,1:T(8,128)(2,1)} copy(bf16[256,4096]{1,0:T(8,128)(2,1)} %param.18) | data formatting | bytes 4194304 | tf_op jit(solution)/shard_map/reshape | solution.py:136
  64.7 0.2 select_reduce_fusion.1
  64.9 0.1 select_reduce_fusion
  65.0 0.9 bitcast_reduce_fusion
  66.0 43.3 %all-to-all-done.1 = bf16[32,256,128]{2,1,0:T(8,128)(2,1)} async-done(((bf16[32,256,128]{2,1,0:T(8,128)(2,1)}), bf16[32,256,128]{2,1,0:T(8,128)(2,1)}, u32[]{:S(2)}, u32[]{:S(2)}) %all-to-all-start.1) | async-done | bytes 2097184 | tf_op jit(solution)/shard_map/all_to_all | solution.py:132
  109.3 5.9 %add_convert_fusion = bf16[256,32,128]{2,0,1:T(8,128)(2,1)} fusion(bf16[256,32,128]{0,2,1:T(8,128)(2,1)} %bitcast.102, f32[32,128]{1,0:T(8,128)S(1)} %bitcast.108, bf16[32,256,128]{2,1,0:T(8,128)(2,1)} %all-to-all-done.1, bf16[32,128,256]{2,1,0:T(8,128)(2,1)S(1)} %bitcast.98), kind=kOutput, calls=%fused_computation.8 | convolution fusion | flops 1075904512 | bytes 8404992 | tf_op jit(solution)/shard_map/cr,rfd->fcd/dot_general | solution.py:139
  115.2 6.0 %fusion.12 = f32[256,1024]{1,0:T(8,128)S(1)} fusion(bf16[32,128,1024]{2,1,0:T(8,128)(2,1)} %bitcast.116, bf16[32,256,128]{2,1,0:T(8,128)(2,1)} %all-to-all-done.1, bf16[256,32,128]{2,0,1:T(8,128)(2,1)} %add_convert_fusion, f32[1024]{0:T(1024)S(1)} %copy-done.6), kind=kOutput, calls=%fused_computation.16 | convolution fusion | flops 2152988672 | bytes 13635584 | tf_op jit(solution)/shard_map/fcd,fdh->ch/dot_general | solution.py:142
  121.3 0.4 fusion.30
  121.7 0.4 fusion.25
  122.2 6.8 %convolution_convert_fusion = bf16[32,128,256]{1,2,0:T(8,128)(2,1)} fusion(bf16[32,128,1024]{2,1,0:T(8,128)(2,1)} %bitcast.117, f32[256,1024]{1,0:T(8,128)S(1)} %fusion.12, f32[256]{0:T(256)S(1)} %maximum_divide_fusion, bf16[1,8,8,128]{3,2,1,0:T(8,128)(2,1)S(1)} %bitcast.110, s32[8]{0:T(128)S(1)} %bitcast.115, s32[8]{0:T(128)S(1)} %fusion.52), kind=kOutput, calls=%fused_computation.11 | convolution fusion | flops 2155616256 | bytes 11551808 | tf_op jit(solution)/shard_map/ch,fdh->fcd/dot_general | solution.py:151
  128.9 7.7 %fusion.2 = bf16[32,256,128]{2,1,0:T(8,128)(2,1)} fusion(bf16[32,128,256]{1,2,0:T(8,128)(2,1)} %convolution_convert_fusion, bf16[256,32,128]{2,0,1:T(8,128)(2,1)} %add_convert_fusion, bf16[32,128,256]{2,1,0:T(8,128)(2,1)S(1)} %bitcast.99, bf16[256,32,128]{0,2,1:T(8,128)(2,1)} %bitcast.103, bf16[32,256,128]{2,1,0:T(8,128)(2,1)} %all-to-all-done.1), kind=kOutput, calls=%fused_computation.5 | convolution fusion | flops 1084293120 | bytes 12582912 | tf_op jit(solution)/shard_map/cr,fdr->fcd/dot_general | solution.py:155
  136.7 56.2 %all_to_all.15 = bf16[32,256,128]{2,1,0:T(8,128)(2,1)S(1)} all-to-all(bf16[32,256,128]{2,1,0:T(8,128)(2,1)} %fusion.2), channel_id=1, replica_groups=mesh['y'=4,'c'=2,'z'=8,'x'=4] {'z','x'}, dimensions={0} | all-to-all | bytes 4194304 | tf_op jit(solution)/shard_map/all_to_all | solution.py:159
  192.9 1.3 copy.32
  (29 shorter events, 0.4 us)
Async XLA Ops:
  7.2 102.1 %copy-start = (bf16[4096,256]{1,0:T(8,128)(2,1)S(1)}, bf16[4096,256]{1,0:T(8,128)(2,1)}, u32[]{:S(2)}) copy-start(bf16[4096,256]{1,0:T(8,128)(2,1)} %param.17) | copy-start | bytes 6291460
  8.1 15.9 %copy-start.2 = (s32[8192,1,2]{0,2,1:T(2,128)S(1)}, s32[8192,1,2]{0,2,1:T(2,128)}, u32[]{:S(2)}) copy-start(s32[8192,1,2]{0,2,1:T(2,128)} %param.12) | copy-start | bytes 196612
  9.3 40.3 %all-to-all-start = ((bf16[32,128,128]{2,1,0:T(8,128)(2,1)}), bf16[32,128,128]{2,1,0:T(8,128)(2,1)S(1)}, u32[]{:S(2)}, u32[]{:S(2)}) async-start(bf16[32,128,128]{2,1,0:T(8,128)(2,1)} %broadcast_in_dim.20), calls=%async_computation | async-start | bytes 2097152 | tf_op jit(solution)/shard_map/all_to_all | solution.py:109
  20.9 44.1 %all-gather.5.cloned.1.call-start = ((), (), s32[]{:S(2)}) async-start(), calls=%async_computation.4 | async-start | bytes 1179648 | tf_op jit(solution)/shard_map/all_gather | solution.py:126
  23.9 91.3 %all-gather.3.cloned.1.call-start = ((), (), s32[]{:S(2)}) async-start(), calls=%async_computation.3 | async-start | bytes 9437184 | tf_op jit(solution)/shard_map/all_gather | solution.py:126
  49.6 1.0 copy-start.1
  50.6 9.9 %copy-start.7 = (s32[1,8]{1,0:T(1,128)S(1)}, s32[1,8]{1,0:T(1,128)}, u32[]{:S(2)}) copy-start(s32[1,8]{1,0:T(1,128)} %param.13) | copy-start | bytes 100
  50.6 58.7 %all-to-all-start.1 = ((bf16[32,256,128]{2,1,0:T(8,128)(2,1)}), bf16[32,256,128]{2,1,0:T(8,128)(2,1)}, u32[]{:S(2)}, u32[]{:S(2)}) async-start(bf16[32,256,128]{2,1,0:T(8,128)(2,1)} %bitcast.100), calls=%async_computation.1 | async-start | bytes 4194304 | tf_op jit(solution)/shard_map/all_to_all | solution.py:132
  60.6 4.1 %copy-start.4 = (s32[256]{0:T(256)S(1)}, s32[256]{0:T(256)}, u32[]{:S(2)}) copy-start(s32[256]{0:T(256)} %param.14) | copy-start | bytes 3076
  60.6 48.6 %copy-start.3 = (f32[4096]{0:T(1024)S(1)}, f32[4096]{0:T(1024)}, u32[]{:S(2)}) copy-start(f32[4096]{0:T(1024)} %param.19) | copy-start | bytes 49156
  109.3 5.9 %copy-start.6 = (f32[1024]{0:T(1024)S(1)}, f32[1024]{0:T(1024)}, u32[]{:S(2)}) copy-start(f32[1024]{0:T(1024)} %param.21) | copy-start | bytes 12292
  121.7 7.3 %copy-start.5 = (f32[256]{0:T(256)}, f32[256]{0:T(256)S(1)}, u32[]{:S(2)}) copy-start(f32[256]{0:T(256)S(1)} %broadcast_multiply_fusion) | copy-start | bytes 3076
Sparse Core Ops, SparseCore 0:
  24.1 26.9 all-gather.4
  52.9 56.9 all-gather.2

commit v13 on v9

--- a/solution.py
+++ b/solution.py
@@ -147,7 +147,8 @@
     code = jnp.dot(member.astype(bf16), user_seg, preferred_element_type=f32)
     slope = sig * (1.0 + act * (1.0 - sig))
     dact = (dscore[:, None] * code * scale * slope).astype(bf16)
-    dx1 = jnp.einsum("ch,fdh->fcd", dact, w3, preferred_element_type=f32)
+    dx1 = jnp.einsum("ch,fdh->fcd", dact, w3, preferred_element_type=f32).astype(bf16)
+    dx1 = dx1.astype(f32)
     dcross = (dx1 * x0f).astype(bf16)
     dz = jnp.einsum("fcd,rfd->cr", dcross, cu3, preferred_element_type=f32).astype(bf16)
     dx0 = dx1 * (1.0 + cross) + jnp.einsum(

time: 205 us -> 204 us (level)
  no operation moved by 1% of the time
where the time goes in v13:
time: 204 us; the launch traced here: 203 us
  blocking collectives  56.2 us (28%)
  waiting for transfers between devices  43.3 us (21%)
  matrix products  30.5 us (15%)
  Pallas kernels  25 us (12%)
  starting transfers between devices  21.5 us (11%)
  between operations  14.2 us (7%)
  local copies, waits for them, and re-layouts  10.7 us (5%)
    all_to_all x1, blocking collectives, local(): returned = lax.all_to_all(grads, MP, 0, 0, tiled=True)  56.2 us
    all_to_all x1, waiting for transfers between devices, local(): x0f = lax.all_to_all(pooled.reshape(n_mp, rows, emb), MP, 0, 0, tiled=True)  43.3 us
    pallas_call x1, Pallas kernels, pool_rows(): pl.pallas_call(pool_kernel, grid_spec=spec, out_shape=jax.ShapeDtypeStruc...  25 us
    all_to_all x1, starting transfers between devices, local(): lax.all_to_all(jnp.broadcast_to(w_piece[None], (n_mp,) + w_piece.shape),...  11.6 us
    all_to_all x1, starting transfers between devices, local(): x0f = lax.all_to_all(pooled.reshape(n_mp, rows, emb), MP, 0, 0, tiled=True)  9.84 us
    dot_general x1, matrix products, local(): jnp.einsum('cr,fdr->fcd', dz, cd3, preferred_element_type=f32)  8.36 us
    dot_general x1, matrix products, local(): jnp.einsum('ch,fdh->fcd', dact, w3, preferred_element_type=f32).astype(bf16)  6.79 us
    dot_general x1, matrix products, local(): jnp.einsum('fcd,fdh->ch', x1, w3, preferred_element_type=f32) + tower_bias  6.66 us
  transfers between devices with their start and end apart: 4, of which 1 were waited for; matrix products, arithmetic and copies ran while one was open for 8% of the time, Pallas kernels for 12%

profile of v13, /device:TPU:2, one launch (start us, length us, event | category | flops | bytes accessed | tf_op | source)
XLA Modules:
  0.0 202.9 jit_solution(891965679830925361)
XLA Ops:
  7.2 0.9 constant_dynamic-slice_fusion
  8.1 1.2 broadcast_in_dim.20
  9.3 11.6 %all-to-all-start = ((bf16[32,128,128]{2,1,0:T(8,128)(2,1)}), bf16[32,128,128]{2,1,0:T(8,128)(2,1)S(1)}, u32[]{:S(2)}, u32[]{:S(2)}) async-start(bf16[32,128,128]{2,1,0:T(8,128)(2,1)} %broadcast_in_dim.20), calls=%async_computation | async-start | bytes 2097152 | tf_op jit(solution)/shard_map/all_to_all | solution.py:109
  21.2 0.8 dynamic_slice.10
  21.9 1.3 convolution_convert_fusion.1
  23.2 0.7 reshape.96
  24.0 0.6 copy.20
  24.6 25.0 %shard_map.122 = bf16[8192,128]{1,0:T(8,128)(2,1)} custom-call(s32[16384]{0:T(1024)} %bitcast.106, bf16[2048,128]{1,0:T(8,128)(2,1)} %bitcast.105), custom_call_target="tpu_custom_call" | custom-call | tf_op jit(solution)/shard_map/pallas_call | solution.py:44
  49.6 1.0 copy-done.1
  50.6 9.8 %all-to-all-start.1 = ((bf16[32,256,128]{2,1,0:T(8,128)(2,1)}), bf16[32,256,128]{2,1,0:T(8,128)(2,1)}, u32[]{:S(2)}, u32[]{:S(2)}) async-start(bf16[32,256,128]{2,1,0:T(8,128)(2,1)} %bitcast.102), calls=%async_computation.1 | async-start | bytes 4194304 | tf_op jit(solution)/shard_map/all_to_all | solution.py:132
  60.5 0.2 reduce-window.4
  60.7 4.1 %copy.19 = bf16[256,4096]{0,1:T(8,128)(2,1)} copy(bf16[256,4096]{1,0:T(8,128)(2,1)} %param.18) | data formatting | bytes 4194304 | tf_op jit(solution)/shard_map/reshape | solution.py:136
  64.8 0.2 select_reduce_fusion.1
  65.0 0.1 select_reduce_fusion
  65.1 1.0 bitcast_reduce_fusion
  66.0 43.3 %all-to-all-done.1 = bf16[32,256,128]{2,1,0:T(8,128)(2,1)} async-done(((bf16[32,256,128]{2,1,0:T(8,128)(2,1)}), bf16[32,256,128]{2,1,0:T(8,128)(2,1)}, u32[]{:S(2)}, u32[]{:S(2)}) %all-to-all-start.1) | async-done | bytes 2097184 | tf_op jit(solution)/shard_map/all_to_all | solution.py:132
  109.3 6.6 %fusion.32 = f32[256,32,128]{2,0,1:T(8,128)} fusion(bf16[256,32,128]{0,2,1:T(8,128)(2,1)} %bitcast.100, bf16[32,256,128]{2,1,0:T(8,128)(2,1)} %all-to-all-done.1, bf16[32,128,256]{2,1,0:T(8,128)(2,1)S(1)} %bitcast.98), kind=kOutput, calls=%fused_computation.31 | convolution fusion | flops 1073807360 | bytes 10485760 | tf_op jit(solution)/shard_map/cr,rfd->fcd/dot_general | solution.py:139
  115.9 6.7 %fusion.13 = f32[256,1024]{1,0:T(8,128)S(1)} fusion(bf16[32,128,1024]{2,1,0:T(8,128)(2,1)} %bitcast.117, bf16[32,256,128]{2,1,0:T(8,128)(2,1)} %all-to-all-done.1, f32[256,32,128]{2,0,1:T(8,128)} %fusion.32, f32[32,128]{1,0:T(8,128)S(1)} %bitcast.110, f32[1024]{0:T(1024)S(1)} %copy-done.6), kind=kOutput, calls=%fused_computation.16 | convolution fusion | flops 2152988672 | bytes 15749120 | tf_op jit(solution)/shard_map/fcd,fdh->ch/dot_general | solution.py:141
  122.6 0.4 fusion.31
  123.0 0.4 fusion.26
  123.5 6.8 %convolution_convert_fusion = bf16[32,128,256]{1,2,0:T(8,128)(2,1)} fusion(bf16[32,128,1024]{2,1,0:T(8,128)(2,1)} %bitcast.118, f32[256,1024]{1,0:T(8,128)S(1)} %fusion.13, f32[256]{0:T(256)S(1)} %maximum_divide_fusion, bf16[1,8,8,128]{3,2,1,0:T(8,128)(2,1)S(1)} %bitcast.109, s32[8]{0:T(128)S(1)} %bitcast.116, s32[8]{0:T(128)S(1)} %fusion.54), kind=kOutput, calls=%fused_computation.11 | convolution fusion | flops 2155616256 | bytes 11551808 | tf_op jit(solution)/shard_map/ch,fdh->fcd/dot_general | solution.py:150
  130.2 8.4 %fusion.2 = bf16[32,256,128]{2,1,0:T(8,128)(2,1)} fusion(bf16[32,128,256]{1,2,0:T(8,128)(2,1)} %convolution_convert_fusion, f32[256,32,128]{2,0,1:T(8,128)} %fusion.32, bf16[32,128,256]{2,1,0:T(8,128)(2,1)S(1)} %bitcast.99, f32[32,128]{1,0:T(8,128)S(1)} %bitcast.111, bf16[256,32,128]{0,2,1:T(8,128)(2,1)} %bitcast.101, bf16[32,256,128]{2,1,0:T(8,128)(2,1)} %all-to-all-done.1), kind=kOutput, calls=%fused_computation.5 | convolution fusion | flops 1084293120 | bytes 14696448 | tf_op jit(solution)/shard_map/cr,fdr->fcd/dot_general | solution.py:154
  138.6 56.2 %all_to_all.15 = bf16[32,256,128]{2,1,0:T(8,128)(2,1)S(1)} all-to-all(bf16[32,256,128]{2,1,0:T(8,128)(2,1)} %fusion.2), channel_id=1, replica_groups=mesh['y'=4,'c'=2,'z'=8,'x'=4] {'z','x'}, dimensions={0} | all-to-all | bytes 4194304 | tf_op jit(solution)/shard_map/all_to_all | solution.py:158
  194.8 1.3 copy.32
  (29 shorter events, 0.4 us)
Async XLA Ops:
  7.2 102.1 %copy-start = (bf16[4096,256]{1,0:T(8,128)(2,1)S(1)}, bf16[4096,256]{1,0:T(8,128)(2,1)}, u32[]{:S(2)}) copy-start(bf16[4096,256]{1,0:T(8,128)(2,1)} %param.17) | copy-start | bytes 6291460
  8.1 15.9 %copy-start.2 = (s32[8192,1,2]{0,2,1:T(2,128)S(1)}, s32[8192,1,2]{0,2,1:T(2,128)}, u32[]{:S(2)}) copy-start(s32[8192,1,2]{0,2,1:T(2,128)} %param.12) | copy-start | bytes 196612
  9.3 40.3 %all-to-all-start = ((bf16[32,128,128]{2,1,0:T(8,128)(2,1)}), bf16[32,128,128]{2,1,0:T(8,128)(2,1)S(1)}, u32[]{:S(2)}, u32[]{:S(2)}) async-start(bf16[32,128,128]{2,1,0:T(8,128)(2,1)} %broadcast_in_dim.20), calls=%async_computation | async-start | bytes 2097152 | tf_op jit(solution)/shard_map/all_to_all | solution.py:109
  20.9 44.1 %all-gather.5.cloned.1.call-start = ((), (), s32[]{:S(2)}) async-start(), calls=%async_computation.4 | async-start | bytes 1179648 | tf_op jit(solution)/shard_map/all_gather | solution.py:126
  23.9 91.9 %all-gather.3.cloned.1.call-start = ((), (), s32[]{:S(2)}) async-start(), calls=%async_computation.3 | async-start | bytes 9437184 | tf_op jit(solution)/shard_map/all_gather | solution.py:126
  49.6 1.0 copy-start.1
  50.6 9.9 %copy-start.7 = (s32[1,8]{1,0:T(1,128)S(1)}, s32[1,8]{1,0:T(1,128)}, u32[]{:S(2)}) copy-start(s32[1,8]{1,0:T(1,128)} %param.13) | copy-start | bytes 100
  50.6 58.7 %all-to-all-start.1 = ((bf16[32,256,128]{2,1,0:T(8,128)(2,1)}), bf16[32,256,128]{2,1,0:T(8,128)(2,1)}, u32[]{:S(2)}, u32[]{:S(2)}) async-start(bf16[32,256,128]{2,1,0:T(8,128)(2,1)} %bitcast.102), calls=%async_computation.1 | async-start | bytes 4194304 | tf_op jit(solution)/shard_map/all_to_all | solution.py:132
  60.7 4.1 %copy-start.4 = (s32[256]{0:T(256)S(1)}, s32[256]{0:T(256)}, u32[]{:S(2)}) copy-start(s32[256]{0:T(256)} %param.14) | copy-start | bytes 3076
  109.3 6.6 %copy-start.3 = (f32[4096]{0:T(1024)S(1)}, f32[4096]{0:T(1024)}, u32[]{:S(2)}) copy-start(f32[4096]{0:T(1024)} %param.19) | copy-start | bytes 49156
  109.3 6.6 %copy-start.6 = (f32[1024]{0:T(1024)S(1)}, f32[1024]{0:T(1024)}, u32[]{:S(2)}) copy-start(f32[1024]{0:T(1024)} %param.21) | copy-start | bytes 12292
  123.0 7.3 %copy-start.5 = (f32[256]{0:T(256)}, f32[256]{0:T(256)S(1)}, u32[]{:S(2)}) copy-start(f32[256]{0:T(256)S(1)} %broadcast_multiply_fusion) | copy-start | bytes 3076
Sparse Core Ops, SparseCore 0:
  24.1 26.9 all-gather.4
  52.9 56.9 all-gather.2

commit v14 on v13

--- a/solution.py
+++ b/solution.py
@@ -137,7 +137,7 @@
     bias3 = cross_bias.reshape(n_mp, 1, emb)
     z = jnp.einsum("fcd,fdr->cr", x0f, cd3, preferred_element_type=f32).astype(bf16)
     cross = jnp.einsum("cr,rfd->fcd", z, cu3, preferred_element_type=f32) + bias3
-    x1 = (x0f * cross + x0f).astype(bf16)
+    x1 = lax.optimization_barrier((x0f * cross + x0f).astype(bf16))
     act = jnp.einsum("fcd,fdh->ch", x1, w3, preferred_element_type=f32) + tower_bias
     sig = jax.nn.sigmoid(act)
     hidden = (act * sig).astype(bf16)

time: 204 us -> 204 us (level)
  no operation moved by 1% of the time
where the time goes in v14:
time: 204 us
  blocking collectives  56.2 us (28%)
  waiting for transfers between devices  43.6 us (21%)
  matrix products  30.6 us (15%)
  Pallas kernels  25 us (12%)
  starting transfers between devices  21.5 us (11%)
  between operations  14.2 us (7%)
  local copies, waits for them, and re-layouts  11 us (5%)
    all_to_all x1, blocking collectives, local(): returned = lax.all_to_all(grads, MP, 0, 0, tiled=True)  56.2 us
    all_to_all x1, waiting for transfers between devices, local(): x0f = lax.all_to_all(pooled.reshape(n_mp, rows, emb), MP, 0, 0, tiled=True)  43.6 us
    pallas_call x1, Pallas kernels, pool_rows(): pl.pallas_call(pool_kernel, grid_spec=spec, out_shape=jax.ShapeDtypeStruc...  25 us
    all_to_all x1, starting transfers between devices, local(): lax.all_to_all(jnp.broadcast_to(w_piece[None], (n_mp,) + w_piece.shape),...  11.6 us
    all_to_all x1, starting transfers between devices, local(): x0f = lax.all_to_all(pooled.reshape(n_mp, rows, emb), MP, 0, 0, tiled=True)  9.84 us
    dot_general x1, matrix products, local(): jnp.einsum('cr,fdr->fcd', dz, cd3, preferred_element_type=f32)  8.35 us
    dot_general x1, matrix products, local(): jnp.einsum('cr,rfd->fcd', z, cu3, preferred_element_type=f32) + bias3  7.94 us
    dot_general x1, matrix products, local(): jnp.einsum('ch,fdh->fcd', dact, w3, preferred_element_type=f32).astype(bf16)  6.74 us
  transfers between devices with their start and end apart: 4, of which 1 were waited for; matrix products, arithmetic and copies ran while one was open for 8% of the time, Pallas kernels for 12%

profile of v14, /device:TPU:2, one launch (start us, length us, event | category | flops | bytes accessed | tf_op | source)
XLA Modules:
  0.0 203.5 jit_solution(5926843920754802580)
XLA Ops:
  7.2 0.9 constant_dynamic-slice_fusion
  8.1 1.2 broadcast_in_dim.20
  9.3 11.6 %all-to-all-start = ((bf16[32,128,128]{2,1,0:T(8,128)(2,1)}), bf16[32,128,128]{2,1,0:T(8,128)(2,1)S(1)}, u32[]{:S(2)}, u32[]{:S(2)}) async-start(bf16[32,128,128]{2,1,0:T(8,128)(2,1)} %broadcast_in_dim.20), calls=%async_computation | async-start | bytes 2097152 | tf_op jit(solution)/shard_map/all_to_all | solution.py:109
  21.2 0.8 dynamic_slice.10
  21.9 1.3 convolution_convert_fusion.1
  23.2 0.7 reshape.96
  24.0 0.6 copy.20
  24.6 25.0 %shard_map.122 = bf16[8192,128]{1,0:T(8,128)(2,1)} custom-call(s32[16384]{0:T(1024)} %bitcast.106, bf16[2048,128]{1,0:T(8,128)(2,1)} %bitcast.105), custom_call_target="tpu_custom_call" | custom-call | tf_op jit(solution)/shard_map/pallas_call | solution.py:44
  49.6 1.0 copy-done.1
  50.6 9.8 %all-to-all-start.1 = ((bf16[32,256,128]{2,1,0:T(8,128)(2,1)}), bf16[32,256,128]{2,1,0:T(8,128)(2,1)}, u32[]{:S(2)}, u32[]{:S(2)}) async-start(bf16[32,256,128]{2,1,0:T(8,128)(2,1)} %bitcast.102), calls=%async_computation.1 | async-start | bytes 4194304 | tf_op jit(solution)/shard_map/all_to_all | solution.py:132
  60.5 0.2 reduce-window.4
  60.7 4.1 %copy.19 = bf16[256,4096]{0,1:T(8,128)(2,1)} copy(bf16[256,4096]{1,0:T(8,128)(2,1)} %param.18) | data formatting | bytes 4194304 | tf_op jit(solution)/shard_map/reshape | solution.py:136
  64.8 0.9 bitcast_reduce_fusion
  65.7 43.6 %all-to-all-done.1 = bf16[32,256,128]{2,1,0:T(8,128)(2,1)} async-done(((bf16[32,256,128]{2,1,0:T(8,128)(2,1)}), bf16[32,256,128]{2,1,0:T(8,128)(2,1)}, u32[]{:S(2)}, u32[]{:S(2)}) %all-to-all-start.1) | async-done | bytes 2097184 | tf_op jit(solution)/shard_map/all_to_all | solution.py:132
  109.3 7.9 %fusion.1 = (bf16[32,256,128]{2,1,0:T(8,128)(2,1)}, f32[256,32,128]{2,0,1:T(8,128)}) fusion(bf16[32,256,128]{2,1,0:T(8,128)(2,1)} %all-to-all-done.1, f32[32,128]{1,0:T(8,128)S(1)} %bitcast.108, bf16[256,32,128]{0,2,1:T(8,128)(2,1)} %bitcast.100, bf16[32,128,256]{2,1,0:T(8,128)(2,1)S(1)} %bitcast.98), kind=kOutput, calls=%fused_computation.3 | convolution fusion | flops 1079050240 | bytes 12599296 | tf_op jit(solution)/shard_map/cr,rfd->fcd/dot_general | solution.py:139
  117.3 5.4 %fusion.7 = f32[256,1024]{1,0:T(8,128)S(1)} fusion(bf16[32,256,128]{2,1,0:T(8,128)(2,1)} %get-tuple-element.8, bf16[32,128,1024]{2,1,0:T(8,128)(2,1)} %bitcast.117, f32[1024]{0:T(1024)S(1)} %copy-done.6), kind=kOutput, calls=%fused_computation.14 | convolution fusion | flops 2147745792 | bytes 11538432 | tf_op jit(solution)/shard_map/fcd,fdh->ch/dot_general | solution.py:141
  122.7 0.4 fusion.23
  123.1 0.3 copy-done.4
  123.4 0.2 select_reduce_fusion.1
  123.6 0.4 fusion.18
  124.1 6.7 %convolution_convert_fusion = bf16[32,128,256]{1,2,0:T(8,128)(2,1)} fusion(bf16[32,128,1024]{2,1,0:T(8,128)(2,1)} %bitcast.118, f32[256,1024]{1,0:T(8,128)S(1)} %fusion.7, f32[256]{0:T(256)S(1)} %maximum_divide_fusion, bf16[1,8,8,128]{3,2,1,0:T(8,128)(2,1)S(1)} %bitcast.111, s32[8]{0:T(128)S(1)} %bitcast.116, s32[8]{0:T(128)S(1)} %fusion.46), kind=kOutput, calls=%fused_computation.9 | convolution fusion | flops 2155616256 | bytes 11551808 | tf_op jit(solution)/shard_map/ch,fdh->fcd/dot_general | solution.py:150
  130.8 8.4 %fusion.2 = bf16[32,256,128]{2,1,0:T(8,128)(2,1)} fusion(bf16[32,128,256]{1,2,0:T(8,128)(2,1)} %convolution_convert_fusion, f32[256,32,128]{2,0,1:T(8,128)} %get-tuple-element.9, bf16[32,128,256]{2,1,0:T(8,128)(2,1)S(1)} %bitcast.99, f32[32,128]{1,0:T(8,128)S(1)} %bitcast.109, bf16[256,32,128]{0,2,1:T(8,128)(2,1)} %bitcast.101, ...), kind=kOutput, calls=%fused_computation.5 | convolution fusion | flops 1084293120 | bytes 14696448 | tf_op jit(solution)/shard_map/cr,fdr->fcd/dot_general | solution.py:154
  139.2 56.2 %all_to_all.15 = bf16[32,256,128]{2,1,0:T(8,128)(2,1)S(1)} all-to-all(bf16[32,256,128]{2,1,0:T(8,128)(2,1)} %fusion.2), channel_id=1, replica_groups=mesh['y'=4,'c'=2,'z'=8,'x'=4] {'z','x'}, dimensions={0} | all-to-all | bytes 4194304 | tf_op jit(solution)/shard_map/all_to_all | solution.py:158
  195.4 1.3 copy.32
  (28 shorter events, 0.4 us)
Async XLA Ops:
  7.2 102.2 %copy-start = (bf16[4096,256]{1,0:T(8,128)(2,1)S(1)}, bf16[4096,256]{1,0:T(8,128)(2,1)}, u32[]{:S(2)}) copy-start(bf16[4096,256]{1,0:T(8,128)(2,1)} %param.17) | copy-start | bytes 6291460
  8.1 15.9 %copy-start.2 = (s32[8192,1,2]{0,2,1:T(2,128)S(1)}, s32[8192,1,2]{0,2,1:T(2,128)}, u32[]{:S(2)}) copy-start(s32[8192,1,2]{0,2,1:T(2,128)} %param.12) | copy-start | bytes 196612
  9.3 40.3 %all-to-all-start = ((bf16[32,128,128]{2,1,0:T(8,128)(2,1)}), bf16[32,128,128]{2,1,0:T(8,128)(2,1)S(1)}, u32[]{:S(2)}, u32[]{:S(2)}) async-start(bf16[32,128,128]{2,1,0:T(8,128)(2,1)} %broadcast_in_dim.20), calls=%async_computation | async-start | bytes 2097152 | tf_op jit(solution)/shard_map/all_to_all | solution.py:109
  20.9 43.8 %all-gather.5.cloned.1.call-start = ((), (), s32[]{:S(2)}) async-start(), calls=%async_computation.4 | async-start | bytes 1179648 | tf_op jit(solution)/shard_map/all_gather | solution.py:126
  24.0 93.3 %all-gather.3.cloned.1.call-start = ((), (), s32[]{:S(2)}) async-start(), calls=%async_computation.3 | async-start | bytes 9437184 | tf_op jit(solution)/shard_map/all_gather | solution.py:126
  49.6 1.0 copy-start.1
  50.6 9.9 %copy-start.7 = (s32[1,8]{1,0:T(1,128)S(1)}, s32[1,8]{1,0:T(1,128)}, u32[]{:S(2)}) copy-start(s32[1,8]{1,0:T(1,128)} %param.13) | copy-start | bytes 100
  50.6 58.7 %all-to-all-start.1 = ((bf16[32,256,128]{2,1,0:T(8,128)(2,1)}), bf16[32,256,128]{2,1,0:T(8,128)(2,1)}, u32[]{:S(2)}, u32[]{:S(2)}) async-start(bf16[32,256,128]{2,1,0:T(8,128)(2,1)} %bitcast.102), calls=%async_computation.1 | async-start | bytes 4194304 | tf_op jit(solution)/shard_map/all_to_all | solution.py:132
  60.7 48.7 %copy-start.3 = (f32[4096]{0:T(1024)S(1)}, f32[4096]{0:T(1024)}, u32[]{:S(2)}) copy-start(f32[4096]{0:T(1024)} %param.19) | copy-start | bytes 49156
  109.3 7.9 %copy-start.6 = (f32[1024]{0:T(1024)S(1)}, f32[1024]{0:T(1024)}, u32[]{:S(2)}) copy-start(f32[1024]{0:T(1024)} %param.21) | copy-start | bytes 12292
  122.7 0.7 copy-start.4
  123.4 7.5 %copy-start.5 = (f32[256]{0:T(256)}, f32[256]{0:T(256)S(1)}, u32[]{:S(2)}) copy-start(f32[256]{0:T(256)S(1)} %get-tuple-element.13) | copy-start | bytes 3076
Sparse Core Ops, SparseCore 0:
  24.1 26.9 all-gather.4
  52.9 56.9 all-gather.2
